TPU v7x, 128 devices: a whole 4x4x4 slice. The times are simulated.
128 devices in a mesh: group: 8 (over y_lo, x), head: 16 (over y_hi, z, core).
Axes of the slice: x: 4, y: 4 (y_hi: 2, y_lo: 2; y = y_hi * 2 + y_lo), z: 4, core: 2. Of those that a mesh axis runs over, the one named last changes fastest.
Arguments:
- symbol_lookup_table: bfloat16 [65536, 2048], P(None, 'head'), may hold values from -6 to 6
- joined_linear_maps: float32 [5, 2048, 2048], P(None, 'group', 'head'), may hold values from -0.125 to 0.125
- feedforward_lookup_map: float32 [2048, 7168], P('group', 'head'), may hold values from -0.125 to 0.125
- timeblend_result_map: float32 [2048, 2048], P('head', 'group'), may hold values from -0.125 to 0.125
- feedforward_content_map: float32 [7168, 2048], P('head', 'group'), may hold values from -0.0625 to 0.0625
- lag_blend_coefs: float32 [8, 2048], replicated, may hold values from 0 to 1
- blend_narrowing_map: bfloat16 [2048, 160], replicated, may hold values from -0.125 to 0.125
- blend_widening_maps: bfloat16 [5, 32, 2048], replicated, may hold values from -0.59765625 to 0.59765625
- fading_narrowing_map: bfloat16 [2048, 64], replicated, may hold values from -0.125 to 0.125
- fading_widening_map: bfloat16 [64, 2048], P(None, 'head'), as said below
- initial_fading_power: float32 [2048], P('head'), may hold values from -12 to -2.9
- present_symbol_extra: float32 [2048], P('head'), may hold values from -3 to 3
- attender_scaling_coefs: float32 [2048], P('head'), may hold values from 0.5 to 2
- active_cluster_sheets: int32 [8], replicated, may hold values from 2 to 4, as said below
- sheets_for_inquiry: int32 [7], replicated, may hold values from 2 to 7, as said below
- sheet_symbol_indices: int32 [24, 256], replicated, may hold values from 0 to 65535
Outputs:
- hidden_states: bfloat16 [8192, 2048], P('group', 'head')
- page_states: float32 [32, 32, 4096], P('group', 'head')
- shift_edges: float32 [32, 2, 2048], P('group', None, 'head')
Inputs may be any that keep to these rules, and one draw needn't show every extreme that they name: `active_cluster_sheets`: they sum to 24; the two groups at one end of the axis, the first two or the last two, hold 4 pages each. `sheets_for_inquiry`: they sum to 24; the first page of every group but group 0 continues a request; the first or the last request holds 7 pages. `fading_widening_map`: each entry lies within 2.5 / sqrt(64) of zero.
All inputs are finite; a program needn't handle non-finite values.
Results may differ from a plain program's by a relative error of at most 0.017.
Values may be sent and summed in bfloat16 or wider, within the bound.
No kernel may reach another device: no remote copies, remote signals or barrier semaphores. Data moves between devices by JAX's collectives and lax.ppermute only.
A program may use at most 192 MiB of HBM per device.

v0:
```python
import jax
import jax.numpy as jnp
from jax import lax
from jax.sharding import PartitionSpec as P

ATTENTION_DEPTH = 64
PAGE = 256
SLOTS = 4
BLOCK = 128


EXACT_ARITHMETIC = lax.Precision.HIGHEST
LAYER_EPS = 1e-05
GROUP_EPS = 0.00064


def passed_along(value, axis, steps):
    count = lax.axis_size(axis)
    initial, last = (max(0, -steps), min(count, count - steps))
    return lax.ppermute(value, axis, [(source, source + steps) for source in range(initial, last)])


def layer_norm(value_rows):
    value_rows = value_rows.astype(jnp.float32)
    centered = value_rows - jnp.mean(value_rows, axis=-1, keepdims=True)
    return centered * lax.rsqrt(jnp.mean(centered * centered, axis=-1, keepdims=True) + LAYER_EPS)


def mixed_inputs(current, previous, lag_blend_coefs, blend_narrowing_map, blend_widening_maps):
    delta_rows = previous - current
    seeded = (current + delta_rows * lag_blend_coefs[0]).astype(jnp.bfloat16)
    low_rank = jnp.tanh(
        jnp.dot(seeded, blend_narrowing_map, preferred_element_type=jnp.float32)
    ).astype(jnp.bfloat16)
    rank_width = blend_widening_maps.shape[1]
    result_lines = []
    for number in range(5):
        column_part = low_rank[:, number * rank_width : (number + 1) * rank_width]
        offset = jnp.dot(
            column_part, blend_widening_maps[number], preferred_element_type=jnp.float32
        )
        result_lines.append(
            (current + delta_rows * (lag_blend_coefs[number + 1] + offset)).astype(jnp.bfloat16)
        )
    return result_lines


def log_decay(mixed_decay, fading_narrowing_map, fading_widening_map, initial_fading_power):
    hidden_low = jnp.tanh(
        jnp.dot(mixed_decay, fading_narrowing_map, preferred_element_type=jnp.float32)
    ).astype(jnp.bfloat16)
    return -jnp.exp(
        initial_fading_power
        + jnp.dot(hidden_low, fading_widening_map, preferred_element_type=jnp.float32)
    )


def group_norm(value_rows):
    shaped = value_rows.reshape(value_rows.shape[0], -1, ATTENTION_DEPTH)
    centered = shaped - jnp.mean(shaped, axis=-1, keepdims=True)
    normed = centered * lax.rsqrt(jnp.mean(centered * centered, axis=-1, keepdims=True) + GROUP_EPS)
    return normed.reshape(value_rows.shape)


def per_device(
    symbol_lookup_table,
    joined_linear_maps,
    feedforward_lookup_map,
    timeblend_result_map,
    feedforward_content_map,
    lag_blend_coefs,
    blend_narrowing_map,
    blend_widening_maps,
    fading_narrowing_map,
    fading_widening_map,
    initial_fading_power,
    present_symbol_extra,
    attender_scaling_coefs,
    active_cluster_sheets,
    sheets_for_inquiry,
    sheet_symbol_indices,
):
    group_count = lax.axis_size("group")
    group_here = lax.axis_index("group")
    head_here = lax.axis_index("head")
    features_on_shard = present_symbol_extra.shape[0]
    attenders_on_shard = features_on_shard // ATTENTION_DEPTH
    slot_rows = SLOTS * PAGE
    full_width = lag_blend_coefs.shape[1]
    group_number = jnp.arange(group_count, dtype=jnp.int32)
    pick_group = group_number == group_here
    live_count = jnp.sum(jnp.where(pick_group, active_cluster_sheets, 0))
    group_first = jnp.cumsum(active_cluster_sheets) - active_cluster_sheets
    first_page = jnp.sum(jnp.where(pick_group, group_first, 0))
    slot_number = jnp.arange(SLOTS, dtype=jnp.int32)
    slot_live = slot_number < live_count
    request_first = jnp.cumsum(sheets_for_inquiry) - sheets_for_inquiry
    page_here = first_page + slot_number
    begins = jnp.any(page_here[:, None] == request_first[None, :], axis=1)
    continues = jnp.where(slot_live & jnp.logical_not(begins), 1.0, 0.0).astype(jnp.float32)
    safe_page = jnp.where(slot_live, page_here, 0)
    tokens_here = jnp.take(sheet_symbol_indices, safe_page, axis=0)
    before_token = jnp.take(sheet_symbol_indices[:, -1], jnp.maximum(safe_page - 1, 0))
    own_rows = jnp.take(symbol_lookup_table, tokens_here.reshape(-1), axis=0)
    own_edges = jnp.take(symbol_lookup_table, before_token, axis=0)
    embedded, edge_rows = (
        lax.all_gather(own_rows, "head", axis=1, tiled=True),
        lax.all_gather(own_edges, "head", axis=1, tiled=True),
    )
    stack_half = joined_linear_maps.astype(jnp.bfloat16)
    key_half = feedforward_lookup_map.astype(jnp.bfloat16)
    output_half = timeblend_result_map.astype(jnp.bfloat16)
    value_half = feedforward_content_map.astype(jnp.bfloat16)
    projections, key_weight, output_weight, value_weight = (
        lax.all_gather(stack_half, "group", axis=1, tiled=True),
        lax.all_gather(key_half, "group", axis=0, tiled=True),
        lax.all_gather(output_half, "group", axis=1, tiled=True),
        lax.all_gather(value_half, "group", axis=1, tiled=True),
    )
    current = layer_norm(embedded)
    edge_first = layer_norm(edge_rows) * continues[:, None]
    current_pages = current.reshape(SLOTS, PAGE, full_width)
    previous = jnp.concatenate([edge_first[:, None, :], current_pages[:, :-1, :]], axis=1).reshape(
        slot_rows, full_width
    )
    mixed_decay, mixed_key, mixed_value, mixed_query, mixed_gate = mixed_inputs(
        current, previous, lag_blend_coefs, blend_narrowing_map, blend_widening_maps
    )
    fading_multipliers = log_decay(
        mixed_decay, fading_narrowing_map, fading_widening_map, initial_fading_power
    )
    acceptance_lines = jnp.dot(mixed_query, projections[0], preferred_element_type=jnp.float32)
    present_lookups = jnp.dot(mixed_key, projections[1], preferred_element_type=jnp.float32)
    present_contents = jnp.dot(mixed_value, projections[2], preferred_element_type=jnp.float32)
    gate_raw = jnp.dot(mixed_gate, projections[3], preferred_element_type=jnp.float32)
    gating = jax.nn.silu(gate_raw)
    blocks = slot_rows // BLOCK
    per_page = PAGE // BLOCK

    def to_blocks(value_rows):
        return value_rows.reshape(blocks, BLOCK, attenders_on_shard, ATTENTION_DEPTH).transpose(
            0, 2, 1, 3
        )

    block_index = jnp.arange(blocks, dtype=jnp.int32)
    block_start = block_index % per_page == 0
    block_slot = block_index // per_page
    slot_keep = continues * (slot_number > 0)
    keep_state = jnp.where(block_start, jnp.take(slot_keep, block_slot), 1.0)
    keep_factor = jnp.where(block_start, jnp.take(continues, block_slot), 1.0)
    attender_extra = present_symbol_extra.reshape(attenders_on_shard, ATTENTION_DEPTH)
    strictly_lower = jnp.arange(BLOCK)[:, None] > jnp.arange(BLOCK)[None, :]

    def decay_block(retained_memory, inputs):
        sequential_sweep, factor = retained_memory
        segment_askers, segment_lookups, value_block, decay_rows, keep_one, keep_two = inputs
        sequential_sweep = sequential_sweep * keep_one
        factor = factor * keep_two
        inclusive = jnp.cumsum(decay_rows, axis=1)
        exclusive = inclusive - decay_rows
        query_scaled = segment_askers * jnp.exp(exclusive)
        key_scaled = segment_lookups * jnp.exp(-inclusive)
        scores = jnp.einsum("hts,hus->htu", query_scaled, key_scaled, precision=EXACT_ARITHMETIC)
        scores = jnp.where(strictly_lower, scores, 0.0)
        selfpair_contribution = jnp.sum(
            segment_askers * attender_extra[:, None, :] * segment_lookups, axis=2
        )
        sublevel_result = (
            jnp.einsum("htu,huj->htj", scores, value_block, precision=EXACT_ARITHMETIC)
            + selfpair_contribution[:, :, None] * value_block
            + jnp.einsum("hts,hsj->htj", query_scaled, sequential_sweep, precision=EXACT_ARITHMETIC)
        )
        block_total = inclusive[:, -1, :]
        key_end = segment_lookups * jnp.exp(block_total[:, None, :] - inclusive)
        sequential_sweep = jnp.exp(block_total)[:, :, None] * sequential_sweep + jnp.einsum(
            "hts,htj->hsj", key_end, value_block, precision=EXACT_ARITHMETIC
        )
        carry_rows = query_scaled * factor[:, None, :]
        factor = factor * jnp.exp(block_total)
        return ((sequential_sweep, factor), (sublevel_result, carry_rows, sequential_sweep, factor))

    start_state = jnp.zeros((attenders_on_shard, ATTENTION_DEPTH, ATTENTION_DEPTH), jnp.float32)
    start_factor = jnp.ones((attenders_on_shard, ATTENTION_DEPTH), jnp.float32)
    final_carry, (block_out, carry_rows, block_states, block_factors) = lax.scan(
        decay_block,
        (start_state, start_factor),
        (
            to_blocks(acceptance_lines),
            to_blocks(present_lookups),
            to_blocks(present_contents),
            to_blocks(fading_multipliers),
            keep_state,
            keep_factor,
        ),
    )
    page_end = block_states[per_page - 1 :: per_page]
    page_factor = block_factors[per_page - 1 :: per_page]
    last_pick = (slot_number == live_count - 1).astype(jnp.float32)
    leaving_state = jnp.einsum("s,shij->hij", last_pick, page_end, precision=EXACT_ARITHMETIC)
    leaving_factor = jnp.einsum("s,shi->hi", last_pick, page_factor, precision=EXACT_ARITHMETIC)

    def relay_step(turn_number, incoming):
        return passed_along(
            (leaving_factor[:, :, None] * incoming + leaving_state).astype(jnp.bfloat16), "group", 1
        ).astype(jnp.float32)

    incoming = lax.fori_loop(0, group_count - 1, relay_step, jnp.zeros_like(leaving_state))
    block_out = block_out + jnp.einsum(
        "bhts,hsj->bhtj", carry_rows, incoming, precision=EXACT_ARITHMETIC
    )
    page_end = page_end + page_factor[:, :, :, None] * incoming[None]
    attended = block_out.transpose(0, 2, 1, 3).reshape(slot_rows, features_on_shard)
    normed = (group_norm(attended) * attender_scaling_coefs * gating).astype(jnp.bfloat16)
    mixer_total = lax.psum(
        jnp.dot(normed, output_weight, preferred_element_type=jnp.float32).astype(jnp.bfloat16),
        "head",
    ).astype(jnp.float32)
    residual = (embedded.astype(jnp.float32) + mixer_total).astype(jnp.bfloat16)
    last_residual = lax.dynamic_slice_in_dim(residual, live_count * PAGE - 1, 1, 0)
    arriving = passed_along(last_residual, "group", 1)
    channel_in = layer_norm(residual)
    channel_pages = channel_in.reshape(SLOTS, PAGE, full_width)
    edge_two = (
        jnp.concatenate([layer_norm(arriving), channel_pages[:-1, -1, :]], axis=0)
        * continues[:, None]
    )
    channel_prev = jnp.concatenate(
        [edge_two[:, None, :], channel_pages[:, :-1, :]], axis=1
    ).reshape(slot_rows, full_width)
    channel_delta = channel_prev - channel_in
    key_input = (channel_in + channel_delta * lag_blend_coefs[6]).astype(jnp.bfloat16)
    gate_input = (channel_in + channel_delta * lag_blend_coefs[7]).astype(jnp.bfloat16)
    gate_raw_two = jnp.dot(gate_input, projections[4], preferred_element_type=jnp.float32)
    key_raw = jnp.dot(key_input, key_weight, preferred_element_type=jnp.float32)
    squared = jnp.square(jax.nn.relu(key_raw)).astype(jnp.bfloat16)
    channel = lax.psum_scatter(
        jnp.dot(squared, value_weight, preferred_element_type=jnp.float32).astype(jnp.bfloat16),
        "head",
        scatter_dimension=1,
        tiled=True,
    ).astype(jnp.float32)
    gate_two = jax.nn.sigmoid(gate_raw_two)
    residual_local = lax.dynamic_slice_in_dim(
        residual, head_here * features_on_shard, features_on_shard, 1
    )
    hidden = (residual_local.astype(jnp.float32) + gate_two * channel).astype(jnp.bfloat16)
    row_live = jnp.repeat(slot_live, PAGE)
    hidden_out = jnp.where(row_live[:, None], hidden, jnp.zeros_like(hidden))
    state_out = page_end.reshape(SLOTS, attenders_on_shard, ATTENTION_DEPTH * ATTENTION_DEPTH)
    state_out = jnp.where(slot_live[:, None, None], state_out, jnp.zeros_like(state_out))
    first_edge = lax.dynamic_slice_in_dim(
        current_pages[:, -1, :], head_here * features_on_shard, features_on_shard, 1
    )
    second_edge = lax.dynamic_slice_in_dim(
        channel_pages[:, -1, :], head_here * features_on_shard, features_on_shard, 1
    )
    edge_out = jnp.stack([first_edge, second_edge], axis=1)
    edge_out = jnp.where(slot_live[:, None, None], edge_out, jnp.zeros_like(edge_out))
    return (hidden_out, state_out, edge_out)


def solution(mesh):
    in_specs = (
        P(None, "head"),
        P(None, "group", "head"),
        P("group", "head"),
        P("head", "group"),
        P("head", "group"),
        P(),
        P(),
        P(),
        P(),
        P(None, "head"),
        P("head"),
        P("head"),
        P("head"),
        P(),
        P(),
        P(),
    )
    out_specs = (P("group", "head"), P("group", "head", None), P("group", None, "head"))
    return jax.shard_map(
        per_device, mesh=mesh, in_specs=in_specs, out_specs=out_specs, check_vma=False
    )
```

profile of v0, /device:TPU:2, one launch (start us, length us, event | category | flops | bytes accessed | tf_op | source)
XLA Modules:
  0.0 668.1 jit_solution(10876387743382121126)
XLA Ops:
  7.2 1.9 convert_element_type.97
  15.4 10.9 %gather_fusion.1 = bf16[1024,128]{1,0:T(8,128)(2,1)S(1)} fusion(bf16[65536,128]{1,0:T(8,128)(2,1)} %param.22, s32[1024]{0:T(1024)S(1)} %broadcast_clamp_fusion), kind=kCustom, calls=%fused_computation.3 | custom fusion | bytes 528384 | tf_op jit(solution)/shard_map/jit(_take)/gather | solution.py:104
  36.5 8.6 %gather_fusion.3 = bf16[4,128]{1,0:T(4,128)(2,1)S(1)} fusion(bf16[65536,128]{1,0:T(8,128)(2,1)} %param.22, s32[1024]{0:T(1024)S(1)} %pad_clamp_fusion.1), kind=kCustom, calls=%fused_computation.5 | custom fusion | bytes 2064 | tf_op jit(solution)/shard_map/jit(_take)/gather | solution.py:105
  46.4 25.7 %all_gather.19 = bf16[4,2048]{1,0:T(4,128)(2,1)S(1)} all-gather(bf16[4,128]{1,0:T(4,128)(2,1)S(1)} %broadcast_select_fusion.2), channel_id=1, replica_groups=mesh['group'=8,'head'=16] {'head'}, dimensions={1}, use_global_device_ids=true | all-gather | bytes 17408 | tf_op jit(solution)/shard_map/all_gather | solution.py:108
  73.6 28.4 %all_gather.21 = bf16[128,2048]{1,0:T(8,128)(2,1)S(1)} all-gather(bf16[128,256]{1,0:T(8,128)(2,1)S(1)} %convert_element_type.102), channel_id=1, replica_groups=mesh['group'=8,'head'=16] {'group'}, dimensions={1}, use_global_device_ids=true | all-gather | bytes 589824 | tf_op jit(solution)/shard_map/all_gather | solution.py:117
  103.3 2.3 slice_bitcast_fusion.4
  107.2 5.7 all-gather.5.cloned.1.call-done
  112.9 3.0 convert_reduce_fusion
  115.9 3.4 fusion.32
  120.2 4.7 pad_maximum_fusion
  125.9 4.7 bitcast_subtract_fusion.2
  130.6 2.7 fusion.49
  133.8 8.0 %fusion.56 = bf16[1024,64]{0,1:T(8,128)(2,1)S(1)} fusion(bf16[2048,64]{0,1:T(8,128)(2,1)} %param.30, f32[1024,2048]{1,0:T(8,128)} %copy-done.4, bf16[1024,2048]{1,0:T(8,128)(2,1)} %all-gather.5.cloned.1.call-done, f32[2048]{0:T(1024)S(1)} %bitcast.323, f32[1024]{0:T(1024)S(1)} %add_rsqrt_fusion.1, f32[1024]{0:T(1024)S(1)} %broadcast_multiply_fusion.2, ...), kind=kOutput, calls=%fused_computation.107 | convolution fusion | flops 417398784 | bytes 13189120 | tf_op jit(solution)/shard_map/dot_general | solution.py:50
  143.2 1.9 copy.138
  145.1 6.0 add_convert_fusion.3
  151.1 2.4 convolution_bitcast_fusion.1
  153.5 3.6 add_convert_fusion.4
  158.7 3.6 add_convert_fusion.5
  163.8 74.7 %while.32 = (s32[]{:T(128)}, f32[2,64,64]{2,1,0:T(8,128)S(1)}, f32[2,64]{1,0:T(2,128)S(1)}, f32[8,2,128,64]{2,3,0,1:T(8,128)}, f32[8,2,128,64]{3,2,0,1:T(8,128)}...) while((s32[]{:T(128)}, f32[2,64,64]{2,1,0:T(8,128)S(1)}, ...), condition=%wide.region_12.14_spmd.clone, body=%wide.region_9.13_spmd.clone.sunk | while | flops 77955200 | bytes 2999012 | solution.py:184
  197.2 1.7 fusion.134
  226.8 1.7 bitcast_dynamic-update-slice_fusion.4
  240.1 47.3 %while.33 = (s32[]{:T(128)}, f32[2,64,64]{2,1,0:T(8,128)S(1)}, f32[2,64]{1,0:T(2,128)S(1)}, f32[2,64,64]{2,1,0:T(8,128)S(1)}, s32[]{:T(128)}, /*index=5*/s32[]{:T(128)}) while((s32[]{:T(128)}, f32[2,64,64]{2,1,0:T(8,128)S(1)}, f32[2,64]{1,0:T(2,128)S(1)}, f32[2,64,64]{2,1,0:T(8,128)S(1)}, s32[]{:T(128)}, ...), condition=%wide.region_14.16_spmd.clone, body=%wide.region_13.15_spmd.clone.sunk | while | flops 40963 | bytes 197239 | solution.py:207
  240.2 3.4 collective-permute-start
  243.6 2.4 collective-permute-done
  246.1 3.5 collective-permute-start
  249.6 2.3 collective-permute-done
  252.0 3.5 collective-permute-start
  255.5 2.3 collective-permute-done
  257.9 3.9 collective-permute-start
  261.8 1.9 collective-permute-done
  263.8 6.0 collective-permute-start
  271.5 6.3 collective-permute-start
  279.5 6.3 collective-permute-start
  287.4 2.6 fusion.109
  292.7 7.7 %multiply_convert_fusion.1 = bf16[1024,128]{1,0:T(8,128)(2,1)S(1)} fusion(bf16[5,2048,128]{2,1,0:T(8,128)(2,1)} %all-gather.7.cloned.1.call-done, f32[1024,2048]{1,0:T(8,128)} %copy-done.4, bf16[1024,2048]{1,0:T(8,128)(2,1)} %all-gather.5.cloned.1.call-done, f32[2048]{0:T(1024)S(1)} %bitcast.322, f32[1024]{0:T(1024)S(1)} %add_rsqrt_fusion.1, ...), kind=kOutput, calls=%fused_computation.114 | convolution fusion | flops 686948352 | bytes 15155712 | tf_op jit(solution)/shard_map/dot_general | solution.py:135
  300.4 3.2 convolution_convert_fusion.1
  305.9 153.8 %all-reduce.2.cloned.1.call-done = bf16[1024,2048]{1,0:T(8,128)(2,1)} async-done(((bf16[1024,2048]{1,0:T(8,128)(2,1)}), bf16[1024,2048]{1,0:T(8,128)(2,1)}) %all-reduce.2.cloned.1.call-update) | async-done | bytes 4194320 | tf_op jit(solution)/shard_map/psum | solution.py:214
  459.8 4.8 convert_reduce_fusion.1
  465.8 3.6 collective-permute-start.1
  470.4 3.2 copy-done.7
  476.3 4.6 pad_maximum_fusion.1
  480.9 4.5 bitcast_subtract_fusion.1
  485.4 19.0 %all-gather.9.cloned.1.call-done = bf16[2048,448]{0,1:T(8,128)(2,1)} async-done(((bf16[256,448]{0,1:T(8,128)(2,1)}), bf16[2048,448]{0,1:T(8,128)(2,1)}) %all-gather.9.cloned.1.call-update) | async-done | bytes 1835024 | tf_op jit(solution)/shard_map/all_gather | solution.py:116
  504.4 46.5 %all-gather.11.cloned.1.call-done = bf16[448,2048]{1,0:T(8,128)(2,1)} async-done(((bf16[448,256]{1,0:T(8,128)(2,1)}), bf16[448,2048]{1,0:T(8,128)(2,1)}) %all-gather.11.cloned.1.call-update) | async-done | bytes 1835024 | tf_op jit(solution)/shard_map/all_gather | solution.py:118
  550.9 12.2 %convolution_convert_fusion = bf16[1024,2048]{1,0:T(8,128)(2,1)} fusion(bf16[448,2048]{1,0:T(8,128)(2,1)} %all-gather.11.cloned.1.call-done, bf16[2048,448]{0,1:T(8,128)(2,1)} %all-gather.9.cloned.1.call-done, f32[1024,2048]{1,0:T(8,128)} %bitcast_subtract_fusion.1, f32[2048]{0:T(1024)S(1)} %bitcast.321, bf16[1024,2048]{1,0:T(8,128)(2,1)} %copy-done.5, ...), kind=kOutput, calls=%fused_computation.83 | convolution fusion | flops 3774152704 | bytes 20463616 | tf_op jit(solution)/shard_map/dot_general | solution.py:237
  563.1 6.5 copy.116
  574.1 78.5 %reduce-scatter.4.cloned.1.call-done = bf16[128,1024]{1,0:T(8,128)(2,1)} async-done(((bf16[2048,1024]{1,0:T(8,128)(2,1)}), bf16[128,1024]{1,0:T(8,128)(2,1)}) %reduce-scatter.4.cloned.1.call-update) | async-done | bytes 262160
  653.8 7.3 %fusion.57 = bf16[1024,128]{1,0:T(8,128)(2,1)} fusion(f32[1024,2048]{1,0:T(8,128)} %bitcast_subtract_fusion.1, f32[2048]{0:T(1024)S(1)} %bitcast.320, bf16[5,2048,128]{2,1,0:T(8,128)(2,1)} %all-gather.7.cloned.1.call-done, bf16[1024,128]{1,0:T(8,128)(2,1)S(1)} %copy.117, bf16[1024,2048]{1,0:T(8,128)(2,1)} %copy-done.5, s32[]{:T(128)S(6)} %select_n.209, ...), kind=kOutput, calls=%fused_computation.108 | convolution fusion | flops 550633472 | bytes 13911044 | tf_op jit(solution)/shard_map/dot_general | solution.py:233
  (314 shorter events, 119.4 us)
Async XLA Ops:
  7.2 123.4 %copy-start = (bf16[2048,160]{0,1:T(8,128)(2,1)S(1)}, bf16[2048,160]{0,1:T(8,128)(2,1)}, u32[]{:S(2)}) copy-start(bf16[2048,160]{0,1:T(8,128)(2,1)} %param.28) | copy-start | bytes 1966084
  7.2 96.1 %all-gather.7.cloned.1.call-start = ((), (), s32[]{:S(2)}) async-start(), calls=%async_computation.2 | async-start | bytes 2949120 | tf_op jit(solution)/shard_map/all_gather | solution.py:115
  9.2 103.7 %all-gather.5.cloned.1.call-start = ((), (), s32[]{:S(2)}) async-start(), calls=%async_computation.1 | async-start | bytes 4456448 | tf_op jit(solution)/shard_map/all_gather | solution.py:107
  27.2 432.6 %all-reduce.2.cloned.1.call-start = ((), (), s32[]{:S(2)}) async-start(), calls=%async_computation.3 | async-start | bytes 8388608 | tf_op jit(solution)/shard_map/psum | solution.py:214
  112.9 6.4 copy-start.2
  120.2 5.7 copy-start.8
  130.6 3.2 copy-start.4
  133.8 24.8 %copy-start.12 = (bf16[1024,160]{0,1:T(8,128)(2,1)}, bf16[1024,160]{0,1:T(8,128)(2,1)S(1)}, u32[]{:S(2)}) copy-start(bf16[1024,160]{0,1:T(8,128)(2,1)S(1)} %fusion.49) | copy-start | bytes 983044
  133.8 8.0 %copy-start.13 = (bf16[64,128]{1,0:T(8,128)(2,1)S(1)}, bf16[64,128]{1,0:T(8,128)(2,1)}, u32[]{:S(2)}) copy-start(bf16[64,128]{1,0:T(8,128)(2,1)} %param.31) | copy-start | bytes 49156
  133.8 8.0 %copy-start.14 = (f32[128]{0:T(128)S(1)}, f32[128]{0:T(128)}, u32[]{:S(2)}) copy-start(f32[128]{0:T(128)} %param.32) | copy-start | bytes 1540
  145.1 8.4 %slice-start = ((s8[8388608]{0:T(1024)(128)(4,1)}), s8[4194304]{0:T(1024)(128)(4,1)S(1)}, s32[]{:S(2)}) async-start(s8[8388608]{0:T(1024)(128)(4,1)} %bitcast.287), calls=%async_computation.7 | async-start | bytes 8388608
  145.1 8.4 %copy-start.3 = (bf16[1024,2048]{1,0:T(8,128)(2,1)S(1)}, bf16[1024,2048]{1,0:T(8,128)(2,1)}, u32[]{:S(2)}) copy-start(bf16[1024,2048]{1,0:T(8,128)(2,1)} %all-gather.5.cloned.1.call-done) | copy-start | bytes 12582916
  145.1 8.4 %slice-start.1 = ((s8[8388608]{0:T(1024)(128)(4,1)}), s8[4194304]{0:T(1024)(128)(4,1)S(1)}, s32[]{:S(2)}) async-start(s8[8388608]{0:T(1024)(128)(4,1)} %bitcast.287), calls=%async_computation.8 | async-start | bytes 8388608
  158.6 5.1 copy-start.15
  238.5 54.2 %copy-start.16 = (f32[128]{0:T(128)S(1)}, f32[128]{0:T(128)}, u32[]{:S(2)}) copy-start(f32[128]{0:T(128)} %param.34) | copy-start | bytes 1540
  240.2 5.8 collective-permute-start
  246.1 5.8 collective-permute-start
  252.0 5.8 collective-permute-start
  257.9 5.8 collective-permute-start
  263.8 7.5 %collective-permute-start = (bf16[2,64,64]{2,1,0:T(8,128)(2,1)S(1)}, bf16[2,64,64]{2,1,0:T(8,128)(2,1)S(1)}, u32[]{:S(2)}, u32[]{:S(2)}) collective-permute-start(bf16[2,64,64]{2,1,0:T(8,128)(2,1)S(1)} %fusion.135), channel_id=1, source_target_pairs={{0,16},{16,32},{32,48},{48,64},{64,80},{80,96},{96,112},{1,17},{17... | collective-permute-start | bytes 49160 | tf_op jit(solution)/shard_map/while/body/eval_jaxpr/ppermute | solution.py:20
  271.5 7.9 %collective-permute-start = (bf16[2,64,64]{2,1,0:T(8,128)(2,1)S(1)}, bf16[2,64,64]{2,1,0:T(8,128)(2,1)S(1)}, u32[]{:S(2)}, u32[]{:S(2)}) collective-permute-start(bf16[2,64,64]{2,1,0:T(8,128)(2,1)S(1)} %fusion.135), channel_id=1, source_target_pairs={{0,16},{16,32},{32,48},{48,64},{64,80},{80,96},{96,112},{1,17},{17... | collective-permute-start | bytes 49160 | tf_op jit(solution)/shard_map/while/body/eval_jaxpr/ppermute | solution.py:20
  279.5 7.9 %collective-permute-start = (bf16[2,64,64]{2,1,0:T(8,128)(2,1)S(1)}, bf16[2,64,64]{2,1,0:T(8,128)(2,1)S(1)}, u32[]{:S(2)}, u32[]{:S(2)}) collective-permute-start(bf16[2,64,64]{2,1,0:T(8,128)(2,1)S(1)} %fusion.135), channel_id=1, source_target_pairs={{0,16},{16,32},{32,48},{48,64},{64,80},{80,96},{96,112},{1,17},{17... | collective-permute-start | bytes 49160 | tf_op jit(solution)/shard_map/while/body/eval_jaxpr/ppermute | solution.py:20
  300.4 3.3 copy-start.10
  300.4 4.1 copy-start.11
  303.6 200.8 %all-gather.9.cloned.1.call-start = ((), (), s32[]{:S(2)}) async-start(), calls=%async_computation.4 | async-start | bytes 2064384 | tf_op jit(solution)/shard_map/all_gather | solution.py:116
  304.4 246.5 %all-gather.11.cloned.1.call-start = ((), (), s32[]{:S(2)}) async-start(), calls=%async_computation.5 | async-start | bytes 2064384 | tf_op jit(solution)/shard_map/all_gather | solution.py:118
  305.2 347.4 %reduce-scatter.4.cloned.1.call-start = ((), (), s32[]{:S(2)}) async-start(), calls=%async_computation.6 | async-start | bytes 4456448
  464.5 5.8 copy-start.5
  465.8 7.8 %collective-permute-start.1 = (bf16[1,2048]{1,0:T(2,128)(2,1)S(1)}, bf16[1,2048]{1,0:T(2,128)(2,1)S(1)}, u32[]{:S(2)}, u32[]{:S(2)}) collective-permute-start(bf16[1,2048]{1,0:T(2,128)(2,1)S(1)} %constant_dynamic-slice_fusion.5), channel_id=1, source_target_pairs={{0,16},{16,32},{32,48},{48,64},{64,80},{80,96},{96,112},{1,17},{17... | collective-permute-start | bytes 12296 | tf_op jit(solution)/shard_map/ppermute | solution.py:20
  470.4 3.2 copy-start.7
  476.3 4.6 copy-start.6
  563.1 8.2 %copy-start.9 = (f32[8,2,64,64]{3,2,1,0:T(8,128)S(1)}, f32[8,2,64,64]{3,2,1,0:T(8,128)}, u32[]{:S(2)}) copy-start(f32[8,2,64,64]{3,2,1,0:T(8,128)} %get-tuple-element.108) | copy-start | bytes 786436
  652.6 8.5 %copy-start.1 = (bf16[2048,160]{0,1:T(8,128)(2,1)S(1)}, bf16[2048,160]{0,1:T(8,128)(2,1)}, u32[]{:S(2)}) copy-start(bf16[2048,160]{0,1:T(8,128)(2,1)} %param.28) | copy-start | bytes 1966084
Sparse Core Ops, SparseCore 0:
  9.6 42.8 all-gather.6
  55.4 57.4 all-gather.4
  303.7 155.9 all-reduce.1
  461.2 43.1 all-gather.8
  506.4 44.4 all-gather.10
  569.7 82.7 reduce-scatter.3
where the time goes:
time: 678 us; the launch traced here: 668 us
  waiting for transfers between devices  317 us (47%)
  matrix products  96 us (14%)
  local copies, waits for them, and re-layouts  78 us (12%)
  other arithmetic  67.7 us (10%)
  blocking collectives  54.1 us (8%)
  starting transfers between devices  36.6 us (5%)
  between operations  17.7 us (3%)
    psum x1, waiting for transfers between devices, per_device(): lax.psum(jnp.dot(normed, output_weight, preferred_element_type=jnp.float3...  154 us
    unnamed x7, waiting for transfers between devices  78.6 us
    all_gather x1, waiting for transfers between devices, per_device(): lax.all_gather(value_half, 'group', axis=1, tiled=True)  46.5 us
    ppermute x8, starting transfers between devices, passed_along(): lax.ppermute(value, axis, [(source, source + steps) for source in range(i...  36.4 us
    all_gather x1, blocking collectives, per_device(): lax.all_gather(output_half, 'group', axis=1, tiled=True)  28.4 us
    dynamic_slice x56, local copies, waits for them, and re-layouts, per_device(): lax.scan(decay_block, (start_state, start_factor), (to_blocks(acceptance_...  27.3 us
    all_gather x1, blocking collectives, per_device(): lax.all_gather(own_edges, 'head', axis=1, tiled=True)  25.7 us
    all_gather x1, waiting for transfers between devices, per_device(): lax.all_gather(key_half, 'group', axis=0, tiled=True)  19 us
  transfers between devices with their start and end apart: 14, of which 12 were waited for; matrix products, arithmetic and copies ran while one was open for 10% of the time, Pallas kernels for 0%

commit v1 on v0

--- a/solution.py
+++ b/solution.py
@@ -101,22 +101,25 @@
     safe_page = jnp.where(slot_live, page_here, 0)
     tokens_here = jnp.take(sheet_symbol_indices, safe_page, axis=0)
     before_token = jnp.take(sheet_symbol_indices[:, -1], jnp.maximum(safe_page - 1, 0))
-    own_rows = jnp.take(symbol_lookup_table, tokens_here.reshape(-1), axis=0)
-    own_edges = jnp.take(symbol_lookup_table, before_token, axis=0)
-    embedded, edge_rows = (
-        lax.all_gather(own_rows, "head", axis=1, tiled=True),
-        lax.all_gather(own_edges, "head", axis=1, tiled=True),
-    )
-    stack_half = joined_linear_maps.astype(jnp.bfloat16)
-    key_half = feedforward_lookup_map.astype(jnp.bfloat16)
-    output_half = timeblend_result_map.astype(jnp.bfloat16)
-    value_half = feedforward_content_map.astype(jnp.bfloat16)
-    projections, key_weight, output_weight, value_weight = (
-        lax.all_gather(stack_half, "group", axis=1, tiled=True),
-        lax.all_gather(key_half, "group", axis=0, tiled=True),
-        lax.all_gather(output_half, "group", axis=1, tiled=True),
-        lax.all_gather(value_half, "group", axis=1, tiled=True),
-    )
+    edge_pad = jnp.concatenate([before_token, jnp.zeros((8 - SLOTS,), before_token.dtype)])
+    all_tokens = jnp.concatenate([tokens_here.reshape(-1), edge_pad])
+    own_rows = jnp.take(symbol_lookup_table, all_tokens, axis=0)
+    gathered_rows = lax.all_gather(own_rows, "head", axis=1, tiled=True)
+    embedded = gathered_rows[:slot_rows]
+    edge_rows = gathered_rows[slot_rows : slot_rows + SLOTS]
+    map_count = joined_linear_maps.shape[0]
+    first_pack = jnp.concatenate(
+        [joined_linear_maps, timeblend_result_map.T[None]], axis=0
+    ).astype(jnp.bfloat16)
+    second_pack = jnp.stack(
+        [feedforward_lookup_map, feedforward_content_map.T], axis=0
+    ).astype(jnp.bfloat16)
+    first_full = lax.all_gather(first_pack, "group", axis=1, tiled=True)
+    second_full = lax.all_gather(second_pack, "group", axis=1, tiled=True)
+    projections = first_full[:map_count]
+    output_weight_t = first_full[map_count]
+    key_weight = second_full[0]
+    value_weight_t = second_full[1]
     current = layer_norm(embedded)
     edge_first = layer_norm(edge_rows) * continues[:, None]
     current_pages = current.reshape(SLOTS, PAGE, full_width)
@@ -151,60 +154,57 @@
     attender_extra = present_symbol_extra.reshape(attenders_on_shard, ATTENTION_DEPTH)
     strictly_lower = jnp.arange(BLOCK)[:, None] > jnp.arange(BLOCK)[None, :]
 
-    def decay_block(retained_memory, inputs):
-        sequential_sweep, factor = retained_memory
-        segment_askers, segment_lookups, value_block, decay_rows, keep_one, keep_two = inputs
-        sequential_sweep = sequential_sweep * keep_one
-        factor = factor * keep_two
-        inclusive = jnp.cumsum(decay_rows, axis=1)
-        exclusive = inclusive - decay_rows
-        query_scaled = segment_askers * jnp.exp(exclusive)
-        key_scaled = segment_lookups * jnp.exp(-inclusive)
-        scores = jnp.einsum("hts,hus->htu", query_scaled, key_scaled, precision=EXACT_ARITHMETIC)
-        scores = jnp.where(strictly_lower, scores, 0.0)
-        selfpair_contribution = jnp.sum(
-            segment_askers * attender_extra[:, None, :] * segment_lookups, axis=2
-        )
-        sublevel_result = (
-            jnp.einsum("htu,huj->htj", scores, value_block, precision=EXACT_ARITHMETIC)
-            + selfpair_contribution[:, :, None] * value_block
-            + jnp.einsum("hts,hsj->htj", query_scaled, sequential_sweep, precision=EXACT_ARITHMETIC)
-        )
-        block_total = inclusive[:, -1, :]
-        key_end = segment_lookups * jnp.exp(block_total[:, None, :] - inclusive)
-        sequential_sweep = jnp.exp(block_total)[:, :, None] * sequential_sweep + jnp.einsum(
-            "hts,htj->hsj", key_end, value_block, precision=EXACT_ARITHMETIC
-        )
-        carry_rows = query_scaled * factor[:, None, :]
-        factor = factor * jnp.exp(block_total)
-        return ((sequential_sweep, factor), (sublevel_result, carry_rows, sequential_sweep, factor))
-
-    start_state = jnp.zeros((attenders_on_shard, ATTENTION_DEPTH, ATTENTION_DEPTH), jnp.float32)
-    start_factor = jnp.ones((attenders_on_shard, ATTENTION_DEPTH), jnp.float32)
-    final_carry, (block_out, carry_rows, block_states, block_factors) = lax.scan(
-        decay_block,
-        (start_state, start_factor),
-        (
-            to_blocks(acceptance_lines),
-            to_blocks(present_lookups),
-            to_blocks(present_contents),
-            to_blocks(fading_multipliers),
-            keep_state,
-            keep_factor,
-        ),
-    )
+    askers_b = to_blocks(acceptance_lines)
+    lookups_b = to_blocks(present_lookups)
+    values_b = to_blocks(present_contents)
+    decay_b = to_blocks(fading_multipliers)
+    inclusive = jnp.cumsum(decay_b, axis=2)
+    exclusive = inclusive - decay_b
+    query_scaled = askers_b * jnp.exp(exclusive)
+    key_scaled = lookups_b * jnp.exp(-inclusive)
+    scores = jnp.einsum("bhts,bhus->bhtu", query_scaled, key_scaled, precision=EXACT_ARITHMETIC)
+    scores = jnp.where(strictly_lower, scores, 0.0)
+    selfpair_contribution = jnp.sum(askers_b * attender_extra[None, :, None, :] * lookups_b, axis=3)
+    intra = (
+        jnp.einsum("bhtu,bhuj->bhtj", scores, values_b, precision=EXACT_ARITHMETIC)
+        + selfpair_contribution[..., None] * values_b
+    )
+    block_total = inclusive[:, :, -1, :]
+    block_decay = jnp.exp(block_total)
+    key_end = lookups_b * jnp.exp(block_total[:, :, None, :] - inclusive)
+    block_kv = jnp.einsum("bhts,bhtj->bhsj", key_end, values_b, precision=EXACT_ARITHMETIC)
+    sweep = jnp.zeros((attenders_on_shard, ATTENTION_DEPTH, ATTENTION_DEPTH), jnp.float32)
+    factor = jnp.ones((attenders_on_shard, ATTENTION_DEPTH), jnp.float32)
+    starts, factors_before, ends, factors_after = [], [], [], []
+    for number in range(blocks):
+        sweep = sweep * keep_state[number]
+        factor = factor * keep_factor[number]
+        starts.append(sweep)
+        factors_before.append(factor)
+        sweep = block_decay[number][:, :, None] * sweep + block_kv[number]
+        factor = factor * block_decay[number]
+        ends.append(sweep)
+        factors_after.append(factor)
+    block_out = intra + jnp.einsum(
+        "bhts,bhsj->bhtj", query_scaled, jnp.stack(starts), precision=EXACT_ARITHMETIC
+    )
+    carry_rows = query_scaled * jnp.stack(factors_before)[:, :, None, :]
+    block_states = jnp.stack(ends)
+    block_factors = jnp.stack(factors_after)
     page_end = block_states[per_page - 1 :: per_page]
     page_factor = block_factors[per_page - 1 :: per_page]
     last_pick = (slot_number == live_count - 1).astype(jnp.float32)
     leaving_state = jnp.einsum("s,shij->hij", last_pick, page_end, precision=EXACT_ARITHMETIC)
     leaving_factor = jnp.einsum("s,shi->hi", last_pick, page_factor, precision=EXACT_ARITHMETIC)
 
-    def relay_step(turn_number, incoming):
-        return passed_along(
-            (leaving_factor[:, :, None] * incoming + leaving_state).astype(jnp.bfloat16), "group", 1
-        ).astype(jnp.float32)
-
-    incoming = lax.fori_loop(0, group_count - 1, relay_step, jnp.zeros_like(leaving_state))
+    leaving_pack = jnp.concatenate([leaving_state, leaving_factor[:, None, :]], axis=1)
+    every_pack = lax.all_gather(leaving_pack, "group", axis=0, tiled=False)
+    incoming = jnp.zeros_like(leaving_state)
+    for number in range(group_count - 1):
+        composed = every_pack[number, :, ATTENTION_DEPTH, :][:, :, None] * incoming + every_pack[
+            number, :, :ATTENTION_DEPTH, :
+        ]
+        incoming = jnp.where(number < group_here, composed, incoming)
     block_out = block_out + jnp.einsum(
         "bhts,hsj->bhtj", carry_rows, incoming, precision=EXACT_ARITHMETIC
     )
@@ -212,7 +212,9 @@
     attended = block_out.transpose(0, 2, 1, 3).reshape(slot_rows, features_on_shard)
     normed = (group_norm(attended) * attender_scaling_coefs * gating).astype(jnp.bfloat16)
     mixer_total = lax.psum(
-        jnp.dot(normed, output_weight, preferred_element_type=jnp.float32).astype(jnp.bfloat16),
+        lax.dot_general(
+            normed, output_weight_t, (((1,), (1,)), ((), ())), preferred_element_type=jnp.float32
+        ).astype(jnp.bfloat16),
         "head",
     ).astype(jnp.float32)
     residual = (embedded.astype(jnp.float32) + mixer_total).astype(jnp.bfloat16)
@@ -234,7 +236,9 @@
     key_raw = jnp.dot(key_input, key_weight, preferred_element_type=jnp.float32)
     squared = jnp.square(jax.nn.relu(key_raw)).astype(jnp.bfloat16)
     channel = lax.psum_scatter(
-        jnp.dot(squared, value_weight, preferred_element_type=jnp.float32).astype(jnp.bfloat16),
+        lax.dot_general(
+            squared, value_weight_t, (((1,), (1,)), ((), ())), preferred_element_type=jnp.float32
+        ).astype(jnp.bfloat16),
         "head",
         scatter_dimension=1,
         tiled=True,

time: 678 us -> 561 us (0.83)
  local copies, waits for them, and re-layouts: 78 us -> 42.5 us
  starting transfers between devices: 36.6 us -> 4.3 us
  blocking collectives: 54.1 us -> 28 us
  matrix products: 96 us -> 72.3 us
  waiting for transfers between devices: 317 us -> 326 us
    ppermute x8 -> x1, starting transfers between devices: 36.4 us -> 3.63 us  [passed_along(): lax.ppermute(value, axis, [(source, source + steps) for source in range(i...]
    all_gather x4 -> x3, waiting for transfers between devices: 71.1 us -> 101 us  [the longest x1 55.5 us: per_device(): gathered_rows = lax.all_gather(own_rows, 'head', axis=1, tiled=True)]
    dynamic_slice x56 -> x0, local copies, waits for them, and re-layouts: 27.3 us -> none  [per_device(): lax.scan(decay_block, (start_state, start_factor), (to_blocks(acceptance_...]
    all_gather x2 -> x1, blocking collectives: 54.1 us -> 28 us  [per_device(): every_pack = lax.all_gather(leaving_pack, 'group', axis=0, tiled=False)]
    dot_general x34 -> x6, matrix products: 48.3 us -> 22.8 us  [the longest x1 12.2 us: per_device(): lax.dot_general(squared, value_weight_t, (((1,), (1,)), ((), ())), prefer...]
    ppermute x8 -> x1, waiting for transfers between devices: 13.8 us -> 0.01 us  [passed_along(): lax.ppermute(value, axis, [(source, source + steps) for source in range(i...]
    dynamic_update_slice x16 -> x0, other arithmetic: 10.7 us -> none  [per_device(): lax.scan(decay_block, (start_state, start_factor), (to_blocks(acceptance_...]
    gather x2 -> x1, local copies, waits for them, and re-layouts: 19.5 us -> 10.5 us  [per_device(): own_rows = jnp.take(symbol_lookup_table, all_tokens, axis=0)]
  transfers between devices with their start and end apart: 14 -> 6, of which waited for: 12 -> 5; matrix products, arithmetic and copies ran while one was open for 10% -> 11% of each run, Pallas kernels for 0% -> 0%
where the time goes in v1:
time: 561 us; the launch traced here: 557 us
  waiting for transfers between devices  326 us (58%)
  matrix products  72.3 us (13%)
  other arithmetic  65.4 us (12%)
  local copies, waits for them, and re-layouts  42.5 us (8%)
  blocking collectives  28 us (5%)
  between operations  18.5 us (3%)
    psum x1, waiting for transfers between devices, per_device(): lax.psum(lax.dot_general(normed, output_weight_t, (((1,), (1,)), ((), ())...  148 us
    unnamed x6, waiting for transfers between devices  76.5 us
    all_gather x1, waiting for transfers between devices, per_device(): gathered_rows = lax.all_gather(own_rows, 'head', axis=1, tiled=True)  55.5 us
    all_gather x1, waiting for transfers between devices, per_device(): second_full = lax.all_gather(second_pack, 'group', axis=1, tiled=True)  34.2 us
    all_gather x1, blocking collectives, per_device(): every_pack = lax.all_gather(leaving_pack, 'group', axis=0, tiled=False)  28 us
    dot_general x3, matrix products, mixed_inputs(): jnp.dot(column_part, blend_widening_maps[number], preferred_element_type=...  17.6 us
    unnamed x57, local copies, waits for them, and re-layouts  13.2 us
    dot_general x1, matrix products, per_device(): lax.dot_general(squared, value_weight_t, (((1,), (1,)), ((), ())), prefer...  12.2 us
  transfers between devices with their start and end apart: 6, of which 5 were waited for; matrix products, arithmetic and copies ran while one was open for 11% of the time, Pallas kernels for 0%

profile of v1, /device:TPU:2, one launch (start us, length us, event | category | flops | bytes accessed | tf_op | source)
XLA Modules:
  0.0 556.6 jit_solution(13444309957814497587)
XLA Ops:
  8.3 1.1 convert.17
  11.2 1.3 fusion.130
  12.5 1.3 fusion.132
  13.8 1.3 gather_fusion
  15.1 1.3 compare_and_fusion.2
  16.5 1.3 maximum_bitcast_fusion
  19.3 1.3 fusion.168
  20.8 10.5 %gather_fusion.2 = bf16[1032,128]{1,0:T(8,128)(2,1)S(1)} fusion(bf16[65536,128]{1,0:T(8,128)(2,1)} %param.18, s32[2048]{0:T(1024)S(1)} %pad_clamp_fusion), kind=kCustom, calls=%fused_computation.4 | custom fusion | bytes 532512 | tf_op jit(solution)/shard_map/jit(_take)/gather | solution.py:106
  31.3 1.3 compare_select_fusion.6
  42.5 1.3 fusion.146
  43.8 11.7 %all-gather.7.cloned.1.call-done = bf16[6,2048,128]{2,1,0:T(8,128)(2,1)} async-done(((bf16[6,256,128]{2,1,0:T(8,128)(2,1)}), bf16[6,2048,128]{2,1,0:T(8,128)(2,1)}) %all-gather.7.cloned.1.call-update) | async-done | bytes 3145744 | tf_op jit(solution)/shard_map/all_gather | solution.py:117
  55.5 1.5 slice_bitcast_fusion.15
  60.0 55.5 %all-gather.5.cloned.1.call-done = bf16[1032,2048]{1,0:T(8,128)(2,1)} async-done(((bf16[1032,128]{1,0:T(8,128)(2,1)}), bf16[1032,2048]{1,0:T(8,128)(2,1)}) %all-gather.5.cloned.1.call-update) | async-done | bytes 4227088 | tf_op jit(solution)/shard_map/all_gather | solution.py:107
  115.6 1.0 convert_reduce_fusion.2
  116.6 1.2 fusion.105
  117.8 2.8 convert_reduce_fusion
  120.7 3.1 fusion.4
  123.9 1.2 fusion.2
  125.1 4.7 pad_maximum_fusion
  130.8 4.2 bitcast_subtract_fusion.1
  135.1 2.7 fusion.22
  138.3 8.1 %fusion.29 = bf16[1024,64]{0,1:T(8,128)(2,1)S(1)} fusion(bf16[2048,64]{0,1:T(8,128)(2,1)S(1)} %copy-done.18, f32[1024,2048]{1,0:T(8,128)} %copy-done.2, f32[2048]{0:T(1024)S(1)} %bitcast.330, f32[1024]{0:T(1024)S(1)} %add_rsqrt_fusion.1, f32[1024]{0:T(1024)S(1)} %broadcast_multiply_fusion.2, bf16[5,32,2048]{2,1,0:T(8,128)(2,1)} %param.25, ...), kind=kOutput, calls=%fused_computation.63 | convolution fusion | flops 417398784 | bytes 13189120 | tf_op jit(solution)/shard_map/dot_general | solution.py:50
  149.1 5.0 slice_multiply_fusion.2
  154.8 6.8 %add_convert_fusion.3 = bf16[1024,2048]{1,0:T(8,128)(2,1)S(1)} fusion(f32[1024,2048]{1,0:T(8,128)} %copy-done.2, f32[2048]{0:T(1024)S(1)} %bitcast.323, f32[1024]{0:T(1024)S(1)} %add_rsqrt_fusion.1, f32[1024]{0:T(1024)S(1)} %broadcast_multiply_fusion.2, bf16[5,32,2048]{2,1,0:T(8,128)(2,1)} %param.25, bf16[1024,160]{0,1:T(8,128)(2,1)} %copy-done.15, ...), kind=kOutput, calls=%fused_computation.24 | convolution fusion | flops 148897792 | bytes 16990208 | tf_op jit(solution)/shard_map/dot_general | solution.py:39
  161.7 1.5 fusion.151
  163.2 7.5 %add_convert_fusion.6 = bf16[1024,2048]{1,0:T(8,128)(2,1)S(1)} fusion(f32[1024,2048]{1,0:T(8,128)} %copy-done.2, f32[2048]{0:T(1024)S(1)} %bitcast.322, f32[1024]{0:T(1024)S(1)} %add_rsqrt_fusion.1, f32[1024]{0:T(1024)S(1)} %broadcast_multiply_fusion.2, bf16[5,32,2048]{2,1,0:T(8,128)(2,1)} %param.25, bf16[1024,160]{0,1:T(8,128)(2,1)} %copy-done.15, ...), kind=kOutput, calls=%fused_computation.27 | convolution fusion | flops 148897792 | bytes 16990208 | tf_op jit(solution)/shard_map/dot_general | solution.py:39
  170.8 1.5 convolution_bitcast_fusion.4
  172.4 3.3 add_convert_fusion.4
  175.7 1.5 multiply_reduce_fusion.1
  177.2 1.1 fusion.34
  178.3 2.0 convolution_select_fusion
  187.5 28.0 %all-gather = f32[16,65,64]{1,2,0:T(8,128)S(1)} all-gather(f32[2,65,64]{1,2,0:T(8,128)S(1)} %pad_maximum_fusion.4), channel_id=2, replica_groups=mesh['group'=8,'head'=16] {'group'}, dimensions={0}, use_global_device_ids=true | all-gather | bytes 299520 | tf_op jit(solution)/shard_map/all_gather | solution.py:201
  215.9 2.1 fusion.18
  220.7 7.5 %multiply_convert_fusion.1 = bf16[1024,128]{1,0:T(8,128)(2,1)S(1)} fusion(bf16[6,2048,128]{2,1,0:T(8,128)(2,1)} %all-gather.7.cloned.1.call-done, f32[1024,2048]{1,0:T(8,128)} %copy-done.2, f32[2048]{0:T(1024)S(1)} %bitcast.329, f32[1024]{0:T(1024)S(1)} %add_rsqrt_fusion.1, f32[1024]{0:T(1024)S(1)} %broadcast_multiply_fusion.2, f32[1024,128]{1,0:T(8,128)S(1)} %copy.137, ...), kind=kOutput, calls=%fused_computation.81 | convolution fusion | flops 686948352 | bytes 15155712 | tf_op jit(solution)/shard_map/dot_general | solution.py:138
  228.2 4.3 convolution_convert_fusion.1
  234.2 147.8 %all-reduce.2.cloned.1.call-done = bf16[1024,2048]{1,0:T(8,128)(2,1)} async-done(((bf16[1024,2048]{1,0:T(8,128)(2,1)}), bf16[1024,2048]{1,0:T(8,128)(2,1)}) %all-reduce.2.cloned.1.call-update) | async-done | bytes 4194320 | tf_op jit(solution)/shard_map/psum | solution.py:214
  382.0 4.2 convert_reduce_fusion.1
  386.2 3.6 collective-permute-start
  389.9 1.2 fusion.5
  392.0 3.2 copy-done.5
  398.0 4.7 pad_maximum_fusion.1
  402.7 4.5 bitcast_subtract_fusion
  407.2 34.2 %all-gather.9.cloned.1.call-done = bf16[2,2048,448]{1,2,0:T(8,128)(2,1)} async-done(((bf16[2,256,448]{1,2,0:T(8,128)(2,1)}), bf16[2,2048,448]{1,2,0:T(8,128)(2,1)}) %all-gather.9.cloned.1.call-update) | async-done | bytes 3670032 | tf_op jit(solution)/shard_map/all_gather | solution.py:118
  441.4 12.2 %convolution_convert_fusion = bf16[1024,2048]{1,0:T(8,128)(2,1)} fusion(bf16[2,2048,448]{1,2,0:T(8,128)(2,1)} %all-gather.9.cloned.1.call-done, f32[1024,2048]{1,0:T(8,128)} %bitcast_subtract_fusion, f32[2048]{0:T(1024)S(1)} %bitcast.328, bf16[1024,2048]{1,0:T(8,128)(2,1)} %copy-done.3, f32[1024]{0:T(1024)S(1)} %add_rsqrt_fusion, ...), kind=kOutput, calls=%fused_computation.34 | convolution fusion | flops 3774152704 | bytes 20463616 | tf_op jit(solution)/shard_map/dot_general | solution.py:239
  453.6 6.5 %copy.152 = bf16[1024,2048]{0,1:T(8,128)(2,1)} copy(bf16[1024,2048]{1,0:T(8,128)(2,1)} %convolution_convert_fusion) | data formatting | bytes 8388608
  464.8 76.4 %reduce-scatter.4.cloned.1.call-done = bf16[128,1024]{1,0:T(8,128)(2,1)} async-done(((bf16[2048,1024]{1,0:T(8,128)(2,1)}), bf16[128,1024]{1,0:T(8,128)(2,1)}) %reduce-scatter.4.cloned.1.call-update) | async-done | bytes 262160
  541.2 1.2 copy.153
  542.4 7.3 %fusion.30 = bf16[1024,128]{1,0:T(8,128)(2,1)} fusion(f32[1024,2048]{1,0:T(8,128)} %bitcast_subtract_fusion, f32[2048]{0:T(1024)S(1)} %bitcast.327, bf16[6,2048,128]{2,1,0:T(8,128)(2,1)} %all-gather.7.cloned.1.call-done, bf16[1024,128]{1,0:T(8,128)(2,1)S(1)} %copy.153, bf16[1024,2048]{1,0:T(8,128)(2,1)} %copy-done.3, s32[]{:T(128)S(6)} %select_n.286, ...), kind=kOutput, calls=%fused_computation.65 | convolution fusion | flops 550633472 | bytes 13911044 | tf_op jit(solution)/shard_map/dot_general | solution.py:235
  (172 shorter events, 39.3 us)
Async XLA Ops:
  7.2 127.9 %copy-start = (bf16[2048,160]{0,1:T(8,128)(2,1)S(1)}, bf16[2048,160]{0,1:T(8,128)(2,1)}, u32[]{:S(2)}) copy-start(bf16[2048,160]{0,1:T(8,128)(2,1)} %param.24) | copy-start | bytes 1966084
  7.2 48.3 %all-gather.7.cloned.1.call-start = ((), (), s32[]{:S(2)}) async-start(), calls=%async_computation.2 | async-start | bytes 3538944 | tf_op jit(solution)/shard_map/all_gather | solution.py:117
  10.3 105.3 %all-gather.5.cloned.1.call-start = ((), (), s32[]{:S(2)}) async-start(), calls=%async_computation.1 | async-start | bytes 4491264 | tf_op jit(solution)/shard_map/all_gather | solution.py:107
  33.7 348.3 %all-reduce.2.cloned.1.call-start = ((), (), s32[]{:S(2)}) async-start(), calls=%async_computation.3 | async-start | bytes 8388608 | tf_op jit(solution)/shard_map/psum | solution.py:214
  115.6 8.2 %slice-start = ((s8[4227072]{0:T(1024)(128)(4,1)}), s8[4194304]{0:T(1024)(128)(4,1)S(1)}, s32[]{:S(2)}) async-start(s8[4227072]{0:T(1024)(128)(4,1)} %bitcast.296), calls=%async_computation.6 | async-start | bytes 8388608
  117.8 5.9 %slice-start.1 = ((s8[4227072]{0:T(1024)(128)(4,1)}), s8[32768]{0:T(1024)(128)(4,1)S(1)}, s32[]{:S(2)}) async-start(s8[4227072]{0:T(1024)(128)(4,1)} %bitcast.296), calls=%async_computation.7 | async-start | bytes 65536
  125.1 5.7 %copy-start.6 = (f32[1024,2048]{1,0:T(8,128)}, f32[1024,2048]{1,0:T(8,128)S(1)}, u32[]{:S(2)}) copy-start(f32[1024,2048]{1,0:T(8,128)S(1)} %fusion.2) | copy-start | bytes 25165828
  135.0 3.2 copy-start.2
  135.1 3.2 copy-start.18
  138.3 8.1 %copy-start.15 = (bf16[1024,160]{0,1:T(8,128)(2,1)}, bf16[1024,160]{0,1:T(8,128)(2,1)S(1)}, u32[]{:S(2)}) copy-start(bf16[1024,160]{0,1:T(8,128)(2,1)S(1)} %fusion.22) | copy-start | bytes 983044
  138.3 8.1 %copy-start.16 = (bf16[64,128]{1,0:T(8,128)(2,1)S(1)}, bf16[64,128]{1,0:T(8,128)(2,1)}, u32[]{:S(2)}) copy-start(bf16[64,128]{1,0:T(8,128)(2,1)} %param.27) | copy-start | bytes 49156
  138.3 8.1 %copy-start.17 = (f32[128]{0:T(128)S(1)}, f32[128]{0:T(128)}, u32[]{:S(2)}) copy-start(f32[128]{0:T(128)} %param.28) | copy-start | bytes 1540
  154.8 6.8 %copy-start.9 = (bf16[128,2048]{1,0:T(8,128)(2,1)S(1)}, bf16[128,2048]{1,0:T(8,128)(2,1)}, u32[]{:S(2)}) copy-start(bf16[128,2048]{1,0:T(8,128)(2,1)} %copy.128) | copy-start | bytes 1572868
  161.6 10.7 %slice-start.2 = ((s8[4227072]{0:T(1024)(128)(4,1)}), s8[4194304]{0:T(1024)(128)(4,1)S(1)}, s32[]{:S(2)}) async-start(s8[4227072]{0:T(1024)(128)(4,1)} %bitcast.298), calls=%async_computation.8 | async-start | bytes 8388608
  161.7 10.7 %slice-start.4 = ((s8[8388608]{0:T(1024)(128)(4,1)}), s8[4194304]{0:T(1024)(128)(4,1)S(1)}, s32[]{:S(2)}) async-start(s8[8388608]{0:T(1024)(128)(4,1)} %bitcast.300), calls=%async_computation.10 | async-start | bytes 8388608
  163.2 7.6 %copy-start.8 = (bf16[128,2048]{1,0:T(8,128)(2,1)S(1)}, bf16[128,2048]{1,0:T(8,128)(2,1)}, u32[]{:S(2)}) copy-start(bf16[128,2048]{1,0:T(8,128)(2,1)} %copy.121) | copy-start | bytes 1572868
  163.2 9.1 %slice-start.3 = ((s8[4227072]{0:T(1024)(128)(4,1)}), s8[32768]{0:T(1024)(128)(4,1)S(1)}, s32[]{:S(2)}) async-start(s8[4227072]{0:T(1024)(128)(4,1)} %bitcast.298), calls=%async_computation.9 | async-start | bytes 65536
  163.2 9.1 %slice-start.5 = ((s8[8388608]{0:T(1024)(128)(4,1)}), s8[4194304]{0:T(1024)(128)(4,1)S(1)}, s32[]{:S(2)}) async-start(s8[8388608]{0:T(1024)(128)(4,1)} %bitcast.300), calls=%async_computation.11 | async-start | bytes 8388608
  172.4 3.3 copy-start.7
  175.7 4.7 copy-start.12
  181.9 38.7 %copy-start.19 = (f32[128]{0:T(128)S(1)}, f32[128]{0:T(128)}, u32[]{:S(2)}) copy-start(f32[128]{0:T(128)} %param.30) | copy-start | bytes 1540
  185.5 1.0 copy-start.10
  228.1 4.4 copy-start.13
  228.2 4.5 copy-start.14
  232.5 208.9 %all-gather.9.cloned.1.call-start = ((), (), s32[]{:S(2)}) async-start(), calls=%async_computation.4 | async-start | bytes 4128768 | tf_op jit(solution)/shard_map/all_gather | solution.py:118
  233.5 307.7 %reduce-scatter.4.cloned.1.call-start = ((), (), s32[]{:S(2)}) async-start(), calls=%async_computation.5 | async-start | bytes 4456448
  386.2 5.9 %copy-start.3 = (bf16[1024,2048]{1,0:T(8,128)(2,1)}, bf16[1024,2048]{1,0:T(8,128)(2,1)S(1)}, u32[]{:S(2)}) copy-start(bf16[1024,2048]{1,0:T(8,128)(2,1)S(1)} %get-tuple-element.14) | copy-start | bytes 12582916
  386.2 9.1 %collective-permute-start = (bf16[1,2048]{1,0:T(2,128)(2,1)S(1)}, bf16[1,2048]{1,0:T(2,128)(2,1)S(1)}, u32[]{:S(2)}, u32[]{:S(2)}) collective-permute-start(bf16[1,2048]{1,0:T(2,128)(2,1)S(1)} %constant_dynamic-slice_fusion.2), channel_id=1, source_target_pairs={{0,16},{16,32},{32,48},{48,64},{64,80},{80,96},{96,112},{1,17},{17... | collective-permute-start | bytes 12296 | tf_op jit(solution)/shard_map/ppermute | solution.py:20
  392.0 3.2 copy-start.5
  398.0 4.7 copy-start.4
  453.6 8.4 %copy-start.11 = (f32[7,2,64,64]{3,2,1,0:T(8,128)S(1)}, f32[7,2,64,64]{3,2,1,0:T(8,128)}, u32[]{:S(2)}) copy-start(f32[7,2,64,64]{3,2,1,0:T(8,128)} %copy-done.10) | copy-start | bytes 688132
  541.2 8.5 %copy-start.1 = (bf16[2048,160]{0,1:T(8,128)(2,1)S(1)}, bf16[2048,160]{0,1:T(8,128)(2,1)}, u32[]{:S(2)}) copy-start(bf16[2048,160]{0,1:T(8,128)(2,1)} %param.24) | copy-start | bytes 1966084
Sparse Core Ops, SparseCore 0:
  10.4 45.0 all-gather.6
  57.7 57.7 all-gather.4
  232.6 149.2 all-reduce.1
  383.4 57.9 all-gather.8
  460.3 80.8 reduce-scatter.3

commit v2 on v1

--- a/solution.py
+++ b/solution.py
@@ -114,7 +114,9 @@
     second_pack = jnp.stack(
         [feedforward_lookup_map, feedforward_content_map.T], axis=0
     ).astype(jnp.bfloat16)
+    first_pack, _ = lax.optimization_barrier((first_pack, gathered_rows))
     first_full = lax.all_gather(first_pack, "group", axis=1, tiled=True)
+    second_pack, _ = lax.optimization_barrier((second_pack, first_full))
     second_full = lax.all_gather(second_pack, "group", axis=1, tiled=True)
     projections = first_full[:map_count]
     output_weight_t = first_full[map_count]
@@ -198,25 +200,21 @@
     leaving_factor = jnp.einsum("s,shi->hi", last_pick, page_factor, precision=EXACT_ARITHMETIC)
 
     leaving_pack = jnp.concatenate([leaving_state, leaving_factor[:, None, :]], axis=1)
-    every_pack = lax.all_gather(leaving_pack, "group", axis=0, tiled=False)
+    arrivals = [passed_along(leaving_pack, "group", distance) for distance in range(1, group_count)]
     incoming = jnp.zeros_like(leaving_state)
-    for number in range(group_count - 1):
-        composed = every_pack[number, :, ATTENTION_DEPTH, :][:, :, None] * incoming + every_pack[
-            number, :, :ATTENTION_DEPTH, :
-        ]
-        incoming = jnp.where(number < group_here, composed, incoming)
+    for arrival in reversed(arrivals):
+        incoming = arrival[:, ATTENTION_DEPTH, :][:, :, None] * incoming + arrival[:, :ATTENTION_DEPTH, :]
     block_out = block_out + jnp.einsum(
         "bhts,hsj->bhtj", carry_rows, incoming, precision=EXACT_ARITHMETIC
     )
     page_end = page_end + page_factor[:, :, :, None] * incoming[None]
     attended = block_out.transpose(0, 2, 1, 3).reshape(slot_rows, features_on_shard)
     normed = (group_norm(attended) * attender_scaling_coefs * gating).astype(jnp.bfloat16)
-    mixer_total = lax.psum(
-        lax.dot_general(
-            normed, output_weight_t, (((1,), (1,)), ((), ())), preferred_element_type=jnp.float32
-        ).astype(jnp.bfloat16),
-        "head",
-    ).astype(jnp.float32)
+    mixer_partial = lax.dot_general(
+        normed, output_weight_t, (((1,), (1,)), ((), ())), preferred_element_type=jnp.float32
+    ).astype(jnp.bfloat16)
+    mixer_partial, _ = lax.optimization_barrier((mixer_partial, second_full))
+    mixer_total = lax.psum(mixer_partial, "head").astype(jnp.float32)
     residual = (embedded.astype(jnp.float32) + mixer_total).astype(jnp.bfloat16)
     last_residual = lax.dynamic_slice_in_dim(residual, live_count * PAGE - 1, 1, 0)
     arriving = passed_along(last_residual, "group", 1)

time: 561 us -> 519 us (0.925)
  waiting for transfers between devices: 326 us -> 282 us
  blocking collectives: 28 us -> 0 us
  starting transfers between devices: 4.3 us -> 20.1 us
  matrix products: 72.3 us -> 82.3 us
    all_gather x1, waiting for transfers between devices: 34.2 us -> 0.01 us  [per_device(): second_full = lax.all_gather(second_pack, 'group', axis=1, tiled=True)]
    all_gather x1 -> x0, blocking collectives: 28 us -> none  [per_device(): every_pack = lax.all_gather(leaving_pack, 'group', axis=0, tiled=False)]
    ppermute x1 -> x8, starting transfers between devices: 3.63 us -> 19.4 us  [passed_along(): lax.ppermute(value, axis, [(source, source + steps) for source in range(i...]
    all_gather x1, waiting for transfers between devices: 11.7 us -> 0.01 us  [per_device(): first_full = lax.all_gather(first_pack, 'group', axis=1, tiled=True)]
    all_gather x1, waiting for transfers between devices: 55.5 us -> 44.9 us  [per_device(): gathered_rows = lax.all_gather(own_rows, 'head', axis=1, tiled=True)]
    psum x1, waiting for transfers between devices: 148 us -> 157 us  [per_device(): mixer_total = lax.psum(mixer_partial, 'head').astype(jnp.float32)]
    unnamed x57 -> x47, local copies, waits for them, and re-layouts: 13.2 us -> 13.2 us
  transfers between devices with their start and end apart: 6 -> 13, of which waited for: 5 -> 4; matrix products, arithmetic and copies ran while one was open for 11% -> 22% of each run, Pallas kernels for 0% -> 0%
where the time goes in v2:
time: 519 us; the launch traced here: 513 us
  waiting for transfers between devices  282 us (54%)
  matrix products  82.3 us (16%)
  other arithmetic  69.9 us (13%)
  local copies, waits for them, and re-layouts  40.2 us (8%)
  starting transfers between devices  20.1 us (4%)
  between operations  18.4 us (4%)
    psum x1, waiting for transfers between devices, per_device(): mixer_total = lax.psum(mixer_partial, 'head').astype(jnp.float32)  157 us
    unnamed x6, waiting for transfers between devices  76.7 us
    all_gather x1, waiting for transfers between devices, per_device(): gathered_rows = lax.all_gather(own_rows, 'head', axis=1, tiled=True)  44.9 us
    dot_general x3, matrix products, mixed_inputs(): jnp.dot(column_part, blend_widening_maps[number], preferred_element_type=...  23 us
    ppermute x8, starting transfers between devices, passed_along(): lax.ppermute(value, axis, [(source, source + steps) for source in range(i...  19.4 us
    unnamed x47, local copies, waits for them, and re-layouts  13.2 us
    dot_general x1, matrix products, per_device(): lax.dot_general(squared, value_weight_t, (((1,), (1,)), ((), ())), prefer...  12.1 us
  transfers between devices with their start and end apart: 13, of which 4 were waited for; matrix products, arithmetic and copies ran while one was open for 22% of the time, Pallas kernels for 0%

profile of v2, /device:TPU:2, one launch (start us, length us, event | category | flops | bytes accessed | tf_op | source)
XLA Modules:
  0.0 513.2 jit_solution(7989948690505674291)
XLA Ops:
  8.1 1.3 fusion.95
  9.4 1.3 compare_and_fusion.2
  10.7 1.3 fusion.97
  12.0 1.3 maximum_bitcast_fusion
  14.9 1.3 fusion.132
  16.2 1.3 compare_select_fusion.6
  17.5 1.3 gather_fusion
  19.1 10.4 %gather_fusion.2 = bf16[1032,128]{1,0:T(8,128)(2,1)S(1)} fusion(bf16[65536,128]{1,0:T(8,128)(2,1)} %param.18, s32[2048]{0:T(1024)S(1)} %pad_clamp_fusion), kind=kCustom, calls=%fused_computation.4 | custom fusion | bytes 532512 | tf_op jit(solution)/shard_map/jit(_take)/gather | solution.py:106
  44.8 44.9 %all-gather.4.cloned.1.call-done = bf16[1032,2048]{1,0:T(8,128)(2,1)} async-done(((bf16[1032,128]{1,0:T(8,128)(2,1)}), bf16[1032,2048]{1,0:T(8,128)(2,1)}) %all-gather.4.cloned.1.call-update) | async-done | bytes 4227088 | tf_op jit(solution)/shard_map/all_gather | solution.py:107
  91.6 2.8 convert_reduce_fusion
  94.4 3.1 fusion.4
  98.7 3.0 fusion.2
  101.7 4.7 pad_maximum_fusion
  107.5 4.3 bitcast_subtract_fusion.1
  111.8 2.7 fusion.22
  115.0 8.2 %fusion.29 = bf16[1024,64]{0,1:T(8,128)(2,1)S(1)} fusion(bf16[2048,64]{0,1:T(8,128)(2,1)S(1)} %copy-done.13, f32[1024,2048]{1,0:T(8,128)} %copy-done.2, f32[2048]{0:T(1024)S(1)} %bitcast.275, f32[1024]{0:T(1024)S(1)} %add_rsqrt_fusion.1, f32[1024]{0:T(1024)S(1)} %broadcast_multiply_fusion.2, bf16[5,32,2048]{2,1,0:T(8,128)(2,1)} %param.25, ...), kind=kOutput, calls=%fused_computation.63 | convolution fusion | flops 417398784 | bytes 13189120 | tf_op jit(solution)/shard_map/dot_general | solution.py:50
  124.6 1.2 fusion.31
  126.3 5.0 slice_multiply_fusion.2
  132.3 9.0 %add_convert_fusion.3 = bf16[1024,2048]{1,0:T(8,128)(2,1)} fusion(f32[1024,2048]{1,0:T(8,128)} %copy-done.2, f32[2048]{0:T(1024)S(1)} %bitcast.268, f32[1024]{0:T(1024)S(1)} %add_rsqrt_fusion.1, f32[1024]{0:T(1024)S(1)} %broadcast_multiply_fusion.2, bf16[5,32,2048]{2,1,0:T(8,128)(2,1)} %param.25, bf16[1024,160]{0,1:T(8,128)(2,1)} %copy-done.9, ...), kind=kOutput, calls=%fused_computation.24 | convolution fusion | flops 148897792 | bytes 16990208 | tf_op jit(solution)/shard_map/dot_general | solution.py:39
  141.3 8.8 %add_convert_fusion.4 = bf16[1024,2048]{1,0:T(8,128)(2,1)} fusion(f32[1024,2048]{1,0:T(8,128)} %copy-done.2, f32[2048]{0:T(1024)S(1)} %bitcast.267, f32[1024]{0:T(1024)S(1)} %add_rsqrt_fusion.1, f32[1024]{0:T(1024)S(1)} %broadcast_multiply_fusion.2, bf16[5,32,2048]{2,1,0:T(8,128)(2,1)} %param.25, bf16[1024,160]{0,1:T(8,128)(2,1)} %copy-done.9, ...), kind=kOutput, calls=%fused_computation.25 | convolution fusion | flops 148897792 | bytes 16990208 | tf_op jit(solution)/shard_map/dot_general | solution.py:39
  150.2 5.2 %add_convert_fusion.6 = bf16[1024,2048]{1,0:T(8,128)(2,1)} fusion(f32[1024,2048]{1,0:T(8,128)S(1)} %bitcast.249, f32[2048]{0:T(1024)S(1)} %bitcast.266, f32[1024]{0:T(1024)S(1)} %add_rsqrt_fusion.1, f32[1024]{0:T(1024)S(1)} %broadcast_multiply_fusion.2, bf16[5,32,2048]{2,1,0:T(8,128)(2,1)} %param.25, bf16[1024,160]{0,1:T(8,128)(2,1)} %copy-done.9, ...), kind=kOutput, calls=%fused_computation.27 | convolution fusion | flops 148897792 | bytes 16990208 | tf_op jit(solution)/shard_map/dot_general | solution.py:39
  155.6 1.5 slice_bitcast_fusion.15
  157.8 3.9 fusion.115
  161.7 3.9 convolution_bitcast_fusion.4
  165.6 1.6 multiply_reduce_fusion.1
  174.4 4.6 collective-permute-start.5
  179.0 1.3 collective-permute-start.4
  180.3 1.3 collective-permute-start.3
  181.6 1.3 collective-permute-start.2
  184.0 1.8 convolution_select_fusion
  185.8 2.1 fusion.18
  188.0 3.1 collective-permute-start.1
  191.1 3.6 collective-permute-start
  195.3 4.1 collective-permute-done
  203.6 7.7 %multiply_convert_fusion.1 = bf16[1024,128]{1,0:T(8,128)(2,1)S(1)} fusion(bf16[6,2048,128]{2,1,0:T(8,128)(2,1)} %all-gather.6.cloned.1.call-done, f32[1024,2048]{1,0:T(8,128)} %copy-done.2, f32[2048]{0:T(1024)S(1)} %bitcast.274, f32[1024]{0:T(1024)S(1)} %add_rsqrt_fusion.1, f32[1024]{0:T(1024)S(1)} %broadcast_multiply_fusion.2, f32[1024,128]{1,0:T(8,128)S(1)} %copy.128, ...), kind=kOutput, calls=%fused_computation.80 | convolution fusion | flops 686948352 | bytes 15155712 | tf_op jit(solution)/shard_map/dot_general | solution.py:140
  211.2 4.3 convolution_convert_fusion.1
  216.2 156.8 %all-reduce.2.cloned.1.call-done = bf16[1024,2048]{1,0:T(8,128)(2,1)} async-done(((bf16[1024,2048]{1,0:T(8,128)(2,1)}), bf16[1024,2048]{1,0:T(8,128)(2,1)}) %all-reduce.2.cloned.1.call-update) | async-done | bytes 4194320 | tf_op jit(solution)/shard_map/psum | solution.py:217
  373.1 4.2 convert_reduce_fusion.1
  377.2 1.2 fusion.5
  378.5 3.6 collective-permute-start.7
  383.1 3.3 copy-done.5
  389.1 4.6 pad_maximum_fusion.1
  393.7 4.6 bitcast_subtract_fusion
  398.3 12.1 %convolution_convert_fusion = bf16[1024,2048]{1,0:T(8,128)(2,1)} fusion(bf16[2,2048,448]{1,2,0:T(8,128)(2,1)} %all-gather.8.cloned.1.call-done, f32[1024,2048]{1,0:T(8,128)} %bitcast_subtract_fusion, f32[2048]{0:T(1024)S(1)} %bitcast.273, bf16[1024,2048]{1,0:T(8,128)(2,1)} %copy-done.3, f32[1024]{0:T(1024)S(1)} %add_rsqrt_fusion, ...), kind=kOutput, calls=%fused_computation.34 | convolution fusion | flops 3774152704 | bytes 20463616 | tf_op jit(solution)/shard_map/dot_general | solution.py:237
  410.4 6.4 %copy.143 = bf16[1024,2048]{0,1:T(8,128)(2,1)} copy(bf16[1024,2048]{1,0:T(8,128)(2,1)} %convolution_convert_fusion) | data formatting | bytes 8388608
  421.4 76.6 %reduce-scatter.4.cloned.1.call-done = bf16[128,1024]{1,0:T(8,128)(2,1)} async-done(((bf16[2048,1024]{1,0:T(8,128)(2,1)}), bf16[128,1024]{1,0:T(8,128)(2,1)}) %reduce-scatter.4.cloned.1.call-update) | async-done | bytes 262160
  497.9 1.2 copy.144
  499.1 7.3 %fusion.30 = bf16[1024,128]{1,0:T(8,128)(2,1)} fusion(f32[1024,2048]{1,0:T(8,128)} %bitcast_subtract_fusion, f32[2048]{0:T(1024)S(1)} %bitcast.272, bf16[6,2048,128]{2,1,0:T(8,128)(2,1)} %all-gather.6.cloned.1.call-done, bf16[1024,128]{1,0:T(8,128)(2,1)S(1)} %copy.144, bf16[1024,2048]{1,0:T(8,128)(2,1)} %copy-done.3, s32[]{:T(128)S(6)} %select_n.193, ...), kind=kOutput, calls=%fused_computation.64 | convolution fusion | flops 550633472 | bytes 13911044 | tf_op jit(solution)/shard_map/dot_general | solution.py:233
  (189 shorter events, 44.9 us)
Async XLA Ops:
  7.2 104.7 %copy-start = (bf16[2048,160]{0,1:T(8,128)(2,1)S(1)}, bf16[2048,160]{0,1:T(8,128)(2,1)}, u32[]{:S(2)}) copy-start(bf16[2048,160]{0,1:T(8,128)(2,1)} %param.24) | copy-start | bytes 1966084
  7.2 37.6 %copy-start.10 = (f32[8,2048]{1,0:T(8,128)S(1)}, f32[8,2048]{1,0:T(8,128)}, u32[]{:S(2)}) copy-start(f32[8,2048]{1,0:T(8,128)} %param.23) | copy-start | bytes 196612
  7.2 82.5 %all-gather.4.cloned.1.call-start = ((), (), s32[]{:S(2)}) async-start(), calls=%async_computation.1 | async-start | bytes 4491264 | tf_op jit(solution)/shard_map/all_gather | solution.py:107
  30.5 124.9 %all-gather.6.cloned.1.call-start = ((), (), s32[]{:S(2)}) async-start(), calls=%async_computation.2 | async-start | bytes 3538944 | tf_op jit(solution)/shard_map/all_gather | solution.py:118
  98.4 117.1 %all-gather.8.cloned.1.call-start = ((), (), s32[]{:S(2)}) async-start(), calls=%async_computation.3 | async-start | bytes 4128768 | tf_op jit(solution)/shard_map/all_gather | solution.py:120
  98.7 8.8 %slice-start = ((s8[4227072]{0:T(1024)(128)(4,1)}), s8[4194304]{0:T(1024)(128)(4,1)S(1)}, s32[]{:S(2)}) async-start(s8[4227072]{0:T(1024)(128)(4,1)} %bitcast.244), calls=%async_computation.6 | async-start | bytes 8388608
  101.7 5.8 %copy-start.6 = (f32[1024,2048]{1,0:T(8,128)}, f32[1024,2048]{1,0:T(8,128)S(1)}, u32[]{:S(2)}) copy-start(f32[1024,2048]{1,0:T(8,128)S(1)} %fusion.2) | copy-start | bytes 25165828
  101.7 5.8 %slice-start.1 = ((s8[4227072]{0:T(1024)(128)(4,1)}), s8[32768]{0:T(1024)(128)(4,1)S(1)}, s32[]{:S(2)}) async-start(s8[4227072]{0:T(1024)(128)(4,1)} %bitcast.244), calls=%async_computation.7 | async-start | bytes 65536
  111.8 3.2 copy-start.2
  111.8 3.2 copy-start.13
  115.0 8.2 %copy-start.9 = (bf16[1024,160]{0,1:T(8,128)(2,1)}, bf16[1024,160]{0,1:T(8,128)(2,1)S(1)}, u32[]{:S(2)}) copy-start(bf16[1024,160]{0,1:T(8,128)(2,1)S(1)} %fusion.22) | copy-start | bytes 983044
  115.0 8.2 %copy-start.11 = (bf16[64,128]{1,0:T(8,128)(2,1)S(1)}, bf16[64,128]{1,0:T(8,128)(2,1)}, u32[]{:S(2)}) copy-start(bf16[64,128]{1,0:T(8,128)(2,1)} %param.27) | copy-start | bytes 49156
  115.0 8.2 %copy-start.12 = (f32[128]{0:T(128)S(1)}, f32[128]{0:T(128)}, u32[]{:S(2)}) copy-start(f32[128]{0:T(128)} %param.28) | copy-start | bytes 1540
  132.3 17.9 %slice-start.2 = ((s8[4227072]{0:T(1024)(128)(4,1)}), s8[4194304]{0:T(1024)(128)(4,1)S(1)}, s32[]{:S(2)}) async-start(s8[4227072]{0:T(1024)(128)(4,1)} %bitcast.246), calls=%async_computation.8 | async-start | bytes 8388608
  132.3 17.8 %slice-start.4 = ((s8[8388608]{0:T(1024)(128)(4,1)}), s8[4194304]{0:T(1024)(128)(4,1)S(1)}, s32[]{:S(2)}) async-start(s8[8388608]{0:T(1024)(128)(4,1)} %bitcast.248), calls=%async_computation.10 | async-start | bytes 8388608
  141.3 8.8 %slice-start.3 = ((s8[4227072]{0:T(1024)(128)(4,1)}), s8[32768]{0:T(1024)(128)(4,1)S(1)}, s32[]{:S(2)}) async-start(s8[4227072]{0:T(1024)(128)(4,1)} %bitcast.246), calls=%async_computation.9 | async-start | bytes 65536
  141.3 8.8 %slice-start.5 = ((s8[8388608]{0:T(1024)(128)(4,1)}), s8[4194304]{0:T(1024)(128)(4,1)S(1)}, s32[]{:S(2)}) async-start(s8[8388608]{0:T(1024)(128)(4,1)} %bitcast.248), calls=%async_computation.11 | async-start | bytes 8388608
  155.4 217.6 %all-reduce.2.cloned.1.call-start = ((), (), s32[]{:S(2)}) async-start(), calls=%async_computation.4 | async-start | bytes 8388608 | tf_op jit(solution)/shard_map/psum | solution.py:217
  157.8 7.8 %copy-start.7 = (bf16[1024,2048]{1,0:T(8,128)(2,1)S(1)}, bf16[1024,2048]{1,0:T(8,128)(2,1)}, u32[]{:S(2)}) copy-start(bf16[1024,2048]{1,0:T(8,128)(2,1)} %add_convert_fusion.4) | copy-start | bytes 12582916
  161.7 6.5 %copy-start.8 = (f32[8,2,64,64]{3,2,1,0:T(8,128)S(1)}, f32[8,2,64,64]{3,2,1,0:T(8,128)}, u32[]{:S(2)}) copy-start(f32[8,2,64,64]{3,2,1,0:T(8,128)} %broadcast_dynamic-update-slice_fusion) | copy-start | bytes 786436
  173.6 29.9 %copy-start.14 = (f32[128]{0:T(128)S(1)}, f32[128]{0:T(128)}, u32[]{:S(2)}) copy-start(f32[128]{0:T(128)} %param.30) | copy-start | bytes 1540
  173.8 14.2 %collective-permute-start.6 = (f32[2,65,64]{2,0,1:T(2,128)S(1)}, f32[2,65,64]{2,0,1:T(2,128)S(1)}, u32[]{:S(2)}, u32[]{:S(2)}) collective-permute-start(f32[2,65,64]{2,0,1:T(2,128)S(1)} %pad_maximum_fusion.4), channel_id=1, source_target_pairs={{0,112},{1,113},{2,114},{3,115},{4,116},{5,117},{6,118},{7,119},{8... | collective-permute-start | bytes 99848 | tf_op jit(solution)/shard_map/ppermute | solution.py:20
  174.4 16.6 %collective-permute-start.5 = (f32[2,65,64]{2,0,1:T(2,128)S(1)}, f32[2,65,64]{2,0,1:T(2,128)S(1)}, u32[]{:S(2)}, u32[]{:S(2)}) collective-permute-start(f32[2,65,64]{2,0,1:T(2,128)S(1)} %pad_maximum_fusion.4), channel_id=1, source_target_pairs={{0,96},{16,112},{1,97},{17,113},{2,98},{18,114},{3,99},{19,115},{4... | collective-permute-start | bytes 99848 | tf_op jit(solution)/shard_map/ppermute | solution.py:20
  179.0 15.6 %collective-permute-start.4 = (f32[2,65,64]{2,0,1:T(2,128)S(1)}, f32[2,65,64]{2,0,1:T(2,128)S(1)}, u32[]{:S(2)}, u32[]{:S(2)}) collective-permute-start(f32[2,65,64]{2,0,1:T(2,128)S(1)} %pad_maximum_fusion.4), channel_id=1, source_target_pairs={{0,80},{16,96},{32,112},{1,81},{17,97},{33,113},{2,82},{18,98},{34... | collective-permute-start | bytes 99848 | tf_op jit(solution)/shard_map/ppermute | solution.py:20
  180.3 14.4 %collective-permute-start.3 = (f32[2,65,64]{2,0,1:T(2,128)S(1)}, f32[2,65,64]{2,0,1:T(2,128)S(1)}, u32[]{:S(2)}, u32[]{:S(2)}) collective-permute-start(f32[2,65,64]{2,0,1:T(2,128)S(1)} %pad_maximum_fusion.4), channel_id=1, source_target_pairs={{0,64},{16,80},{32,96},{48,112},{1,65},{17,81},{33,97},{49,113},{2... | collective-permute-start | bytes 99848 | tf_op jit(solution)/shard_map/ppermute | solution.py:20
  181.6 13.1 %collective-permute-start.2 = (f32[2,65,64]{2,0,1:T(2,128)S(1)}, f32[2,65,64]{2,0,1:T(2,128)S(1)}, u32[]{:S(2)}, u32[]{:S(2)}) collective-permute-start(f32[2,65,64]{2,0,1:T(2,128)S(1)} %pad_maximum_fusion.4), channel_id=1, source_target_pairs={{0,48},{16,64},{32,80},{48,96},{64,112},{1,49},{17,65},{33,81},{49... | collective-permute-start | bytes 99848 | tf_op jit(solution)/shard_map/ppermute | solution.py:20
  188.0 6.8 %collective-permute-start.1 = (f32[2,65,64]{2,0,1:T(2,128)S(1)}, f32[2,65,64]{2,0,1:T(2,128)S(1)}, u32[]{:S(2)}, u32[]{:S(2)}) collective-permute-start(f32[2,65,64]{2,0,1:T(2,128)S(1)} %pad_maximum_fusion.4), channel_id=1, source_target_pairs={{0,32},{16,48},{32,64},{48,80},{64,96},{80,112},{1,33},{17,49},{33... | collective-permute-start | bytes 99848 | tf_op jit(solution)/shard_map/ppermute | solution.py:20
  191.1 8.3 %collective-permute-start = (f32[2,65,64]{2,0,1:T(2,128)S(1)}, f32[2,65,64]{2,0,1:T(2,128)S(1)}, u32[]{:S(2)}, u32[]{:S(2)}) collective-permute-start(f32[2,65,64]{2,0,1:T(2,128)S(1)} %pad_maximum_fusion.4), channel_id=1, source_target_pairs={{0,16},{16,32},{32,48},{48,64},{64,80},{80,96},{96,112},{1,17},{17... | collective-permute-start | bytes 99848 | tf_op jit(solution)/shard_map/ppermute | solution.py:20
  215.5 282.4 %reduce-scatter.4.cloned.1.call-start = ((), (), s32[]{:S(2)}) async-start(), calls=%async_computation.5 | async-start | bytes 4456448
  377.2 5.8 %copy-start.3 = (bf16[1024,2048]{1,0:T(8,128)(2,1)}, bf16[1024,2048]{1,0:T(8,128)(2,1)S(1)}, u32[]{:S(2)}) copy-start(bf16[1024,2048]{1,0:T(8,128)(2,1)S(1)} %get-tuple-element.13) | copy-start | bytes 12582916
  378.5 7.9 %collective-permute-start.7 = (bf16[1,2048]{1,0:T(2,128)(2,1)S(1)}, bf16[1,2048]{1,0:T(2,128)(2,1)S(1)}, u32[]{:S(2)}, u32[]{:S(2)}) collective-permute-start(bf16[1,2048]{1,0:T(2,128)(2,1)S(1)} %constant_dynamic-slice_fusion.2), channel_id=1, source_target_pairs={{0,16},{16,32},{32,48},{48,64},{64,80},{80,96},{96,112},{1,17},{17... | collective-permute-start | bytes 12296 | tf_op jit(solution)/shard_map/ppermute | solution.py:20
  383.1 3.3 copy-start.5
  389.1 4.6 copy-start.4
  497.9 8.5 %copy-start.1 = (bf16[2048,160]{0,1:T(8,128)(2,1)S(1)}, bf16[2048,160]{0,1:T(8,128)(2,1)}, u32[]{:S(2)}) copy-start(bf16[2048,160]{0,1:T(8,128)(2,1)} %param.24) | copy-start | bytes 1966084
Sparse Core Ops, SparseCore 0:
  30.6 59.0 all-gather.3
  98.5 40.2 all-gather.5
  155.5 59.2 all-gather.7
  217.2 155.7 all-reduce.1
  417.0 80.9 reduce-scatter.3

commit v3 on v2

--- a/solution.py
+++ b/solution.py
@@ -85,7 +85,8 @@
     head_here = lax.axis_index("head")
     features_on_shard = present_symbol_extra.shape[0]
     attenders_on_shard = features_on_shard // ATTENTION_DEPTH
-    slot_rows = SLOTS * PAGE
+    held = sheet_symbol_indices.shape[0] // group_count
+    slot_rows = held * PAGE
     full_width = lag_blend_coefs.shape[1]
     group_number = jnp.arange(group_count, dtype=jnp.int32)
     pick_group = group_number == group_here
@@ -94,19 +95,19 @@
     first_page = jnp.sum(jnp.where(pick_group, group_first, 0))
     slot_number = jnp.arange(SLOTS, dtype=jnp.int32)
     slot_live = slot_number < live_count
+    held_number = jnp.arange(held, dtype=jnp.int32)
     request_first = jnp.cumsum(sheets_for_inquiry) - sheets_for_inquiry
-    page_here = first_page + slot_number
+    page_here = group_here * held + held_number
     begins = jnp.any(page_here[:, None] == request_first[None, :], axis=1)
-    continues = jnp.where(slot_live & jnp.logical_not(begins), 1.0, 0.0).astype(jnp.float32)
-    safe_page = jnp.where(slot_live, page_here, 0)
-    tokens_here = jnp.take(sheet_symbol_indices, safe_page, axis=0)
-    before_token = jnp.take(sheet_symbol_indices[:, -1], jnp.maximum(safe_page - 1, 0))
-    edge_pad = jnp.concatenate([before_token, jnp.zeros((8 - SLOTS,), before_token.dtype)])
+    continues = jnp.where(jnp.logical_not(begins), 1.0, 0.0).astype(jnp.float32)
+    tokens_here = jnp.take(sheet_symbol_indices, page_here, axis=0)
+    before_token = jnp.take(sheet_symbol_indices[:, -1], jnp.maximum(page_here - 1, 0))
+    edge_pad = jnp.concatenate([before_token, jnp.zeros((8 - held,), before_token.dtype)])
     all_tokens = jnp.concatenate([tokens_here.reshape(-1), edge_pad])
     own_rows = jnp.take(symbol_lookup_table, all_tokens, axis=0)
     gathered_rows = lax.all_gather(own_rows, "head", axis=1, tiled=True)
     embedded = gathered_rows[:slot_rows]
-    edge_rows = gathered_rows[slot_rows : slot_rows + SLOTS]
+    edge_rows = gathered_rows[slot_rows : slot_rows + held]
     map_count = joined_linear_maps.shape[0]
     first_pack = jnp.concatenate(
         [joined_linear_maps, timeblend_result_map.T[None]], axis=0
@@ -124,7 +125,7 @@
     value_weight_t = second_full[1]
     current = layer_norm(embedded)
     edge_first = layer_norm(edge_rows) * continues[:, None]
-    current_pages = current.reshape(SLOTS, PAGE, full_width)
+    current_pages = current.reshape(held, PAGE, full_width)
     previous = jnp.concatenate([edge_first[:, None, :], current_pages[:, :-1, :]], axis=1).reshape(
         slot_rows, full_width
     )
@@ -150,7 +151,7 @@
     block_index = jnp.arange(blocks, dtype=jnp.int32)
     block_start = block_index % per_page == 0
     block_slot = block_index // per_page
-    slot_keep = continues * (slot_number > 0)
+    slot_keep = continues * (held_number > 0)
     keep_state = jnp.where(block_start, jnp.take(slot_keep, block_slot), 1.0)
     keep_factor = jnp.where(block_start, jnp.take(continues, block_slot), 1.0)
     attender_extra = present_symbol_extra.reshape(attenders_on_shard, ATTENTION_DEPTH)
@@ -195,9 +196,8 @@
     block_factors = jnp.stack(factors_after)
     page_end = block_states[per_page - 1 :: per_page]
     page_factor = block_factors[per_page - 1 :: per_page]
-    last_pick = (slot_number == live_count - 1).astype(jnp.float32)
-    leaving_state = jnp.einsum("s,shij->hij", last_pick, page_end, precision=EXACT_ARITHMETIC)
-    leaving_factor = jnp.einsum("s,shi->hi", last_pick, page_factor, precision=EXACT_ARITHMETIC)
+    leaving_state = page_end[-1]
+    leaving_factor = page_factor[-1]
 
     leaving_pack = jnp.concatenate([leaving_state, leaving_factor[:, None, :]], axis=1)
     arrivals = [passed_along(leaving_pack, "group", distance) for distance in range(1, group_count)]
@@ -216,10 +216,10 @@
     mixer_partial, _ = lax.optimization_barrier((mixer_partial, second_full))
     mixer_total = lax.psum(mixer_partial, "head").astype(jnp.float32)
     residual = (embedded.astype(jnp.float32) + mixer_total).astype(jnp.bfloat16)
-    last_residual = lax.dynamic_slice_in_dim(residual, live_count * PAGE - 1, 1, 0)
+    last_residual = residual[slot_rows - 1 : slot_rows]
     arriving = passed_along(last_residual, "group", 1)
     channel_in = layer_norm(residual)
-    channel_pages = channel_in.reshape(SLOTS, PAGE, full_width)
+    channel_pages = channel_in.reshape(held, PAGE, full_width)
     edge_two = (
         jnp.concatenate([layer_norm(arriving), channel_pages[:-1, -1, :]], axis=0)
         * continues[:, None]
@@ -246,17 +246,35 @@
         residual, head_here * features_on_shard, features_on_shard, 1
     )
     hidden = (residual_local.astype(jnp.float32) + gate_two * channel).astype(jnp.bfloat16)
-    row_live = jnp.repeat(slot_live, PAGE)
-    hidden_out = jnp.where(row_live[:, None], hidden, jnp.zeros_like(hidden))
-    state_out = page_end.reshape(SLOTS, attenders_on_shard, ATTENTION_DEPTH * ATTENTION_DEPTH)
-    state_out = jnp.where(slot_live[:, None, None], state_out, jnp.zeros_like(state_out))
+    state_held = page_end.reshape(held, attenders_on_shard, ATTENTION_DEPTH * ATTENTION_DEPTH)
     first_edge = lax.dynamic_slice_in_dim(
         current_pages[:, -1, :], head_here * features_on_shard, features_on_shard, 1
     )
     second_edge = lax.dynamic_slice_in_dim(
         channel_pages[:, -1, :], head_here * features_on_shard, features_on_shard, 1
     )
-    edge_out = jnp.stack([first_edge, second_edge], axis=1)
+    edge_held = jnp.stack([first_edge, second_edge], axis=1)
+    reach = 2
+    shifts = range(-reach, reach + 1)
+
+    def from_neighbours(value):
+        return jnp.concatenate(
+            [value if shift == 0 else passed_along(value, "group", -shift) for shift in shifts], axis=0
+        )
+
+    hidden_near = from_neighbours(hidden.reshape(held, PAGE, features_on_shard))
+    state_near = from_neighbours(state_held)
+    edge_near = from_neighbours(edge_held)
+    slot_page = first_page + slot_number
+    source_group = slot_page // held
+    source_index = (source_group - group_here + reach) * held + slot_page - source_group * held
+    source_index = jnp.clip(source_index, 0, (2 * reach + 1) * held - 1)
+    hidden_out = jnp.take(hidden_near, source_index, axis=0)
+    hidden_out = jnp.where(slot_live[:, None, None], hidden_out, jnp.zeros_like(hidden_out))
+    hidden_out = hidden_out.reshape(SLOTS * PAGE, features_on_shard)
+    state_out = jnp.take(state_near, source_index, axis=0)
+    state_out = jnp.where(slot_live[:, None, None], state_out, jnp.zeros_like(state_out))
+    edge_out = jnp.take(edge_near, source_index, axis=0)
     edge_out = jnp.where(slot_live[:, None, None], edge_out, jnp.zeros_like(edge_out))
     return (hidden_out, state_out, edge_out)
 

time: 519 us -> 496 us (0.956)
  starting transfers between devices: 20.1 us -> 60.7 us
  waiting for transfers between devices: 282 us -> 259 us
  other arithmetic: 69.9 us -> 47.7 us
  matrix products: 82.3 us -> 64.6 us
    ppermute x8 -> x20, starting transfers between devices: 19.4 us -> 59.8 us  [passed_along(): lax.ppermute(value, axis, [(source, source + steps) for source in range(i...]
    unnamed x6, waiting for transfers between devices: 76.7 us -> 37 us
    ppermute x8 -> x20, waiting for transfers between devices: 4.11 us -> 15.6 us  [passed_along(): lax.ppermute(value, axis, [(source, source + steps) for source in range(i...]
    all_gather x1, waiting for transfers between devices: 0.01 us -> 8.6 us  [per_device(): second_full = lax.all_gather(second_pack, 'group', axis=1, tiled=True)]
    dot_general x3, matrix products: 23 us -> 16 us  [mixed_inputs(): jnp.dot(column_part, blend_widening_maps[number], preferred_element_type=...]
    unnamed x47 -> x70, local copies, waits for them, and re-layouts: 13.2 us -> 12.7 us
  transfers between devices with their start and end apart: 13 -> 25, of which waited for: 4 -> 9; matrix products, arithmetic and copies ran while one was open for 22% -> 18% of each run, Pallas kernels for 0% -> 0%
where the time goes in v3:
time: 496 us; the launch traced here: 490 us
  waiting for transfers between devices  259 us (52%)
  matrix products  64.6 us (13%)
  starting transfers between devices  60.7 us (12%)
  other arithmetic  47.7 us (10%)
  local copies, waits for them, and re-layouts  40.3 us (8%)
  between operations  17.4 us (4%)
    psum x1, waiting for transfers between devices, per_device(): mixer_total = lax.psum(mixer_partial, 'head').astype(jnp.float32)  155 us
    ppermute x20, starting transfers between devices, passed_along(): lax.ppermute(value, axis, [(source, source + steps) for source in range(i...  59.8 us
    all_gather x1, waiting for transfers between devices, per_device(): gathered_rows = lax.all_gather(own_rows, 'head', axis=1, tiled=True)  42.2 us
    unnamed x6, waiting for transfers between devices  37 us
    dot_general x3, matrix products, mixed_inputs(): jnp.dot(column_part, blend_widening_maps[number], preferred_element_type=...  16 us
    ppermute x20, waiting for transfers between devices, passed_along(): lax.ppermute(value, axis, [(source, source + steps) for source in range(i...  15.6 us
    unnamed x70, local copies, waits for them, and re-layouts  12.7 us
    dot_general x1, matrix products, per_device(): lax.dot_general(squared, value_weight_t, (((1,), (1,)), ((), ())), prefer...  10.8 us
  transfers between devices with their start and end apart: 25, of which 9 were waited for; matrix products, arithmetic and copies ran while one was open for 18% of the time, Pallas kernels for 0%

profile of v3, /device:TPU:2, one launch (start us, length us, event | category | flops | bytes accessed | tf_op | source)
XLA Modules:
  0.0 489.9 jit_solution(10471187212760984996)
XLA Ops:
  8.3 1.3 gather_fusion
  10.6 9.8 %gather_fusion.2 = bf16[776,128]{1,0:T(8,128)(2,1)S(1)} fusion(bf16[65536,128]{1,0:T(8,128)(2,1)} %param.18, s32[1024]{0:T(1024)S(1)} %pad_clamp_fusion.2), kind=kCustom, calls=%fused_computation.4 | custom fusion | bytes 400416 | tf_op jit(solution)/shard_map/jit(_take)/gather | solution.py:107
  33.5 42.2 %all-gather.4.cloned.1.call-done = bf16[776,2048]{1,0:T(8,128)(2,1)} async-done(((bf16[776,128]{1,0:T(8,128)(2,1)}), bf16[776,2048]{1,0:T(8,128)(2,1)}) %all-gather.4.cloned.1.call-update) | async-done | bytes 3178512 | tf_op jit(solution)/shard_map/all_gather | solution.py:108
  77.6 2.4 convert_reduce_fusion
  79.9 2.8 fusion.4
  84.3 2.6 fusion.2
  86.9 1.3 pad_maximum_fusion
  88.3 1.8 copy-done.8
  92.4 2.0 fusion.25
  95.0 6.2 %fusion.32 = bf16[768,64]{0,1:T(8,128)(2,1)S(1)} fusion(bf16[2048,64]{0,1:T(8,128)(2,1)S(1)} %copy-done.23, f32[768,2048]{1,0:T(8,128)} %copy-done.4, f32[2048]{0:T(1024)S(1)} %bitcast.257, f32[768]{0:T(1024)S(1)} %add_rsqrt_fusion.1, f32[768]{0:T(1024)S(1)} %broadcast_multiply_fusion.2, bf16[5,32,2048]{2,1,0:T(8,128)(2,1)} %param.25, ...), kind=kOutput, calls=%fused_computation.68 | convolution fusion | flops 313049088 | bytes 9994240 | tf_op jit(solution)/shard_map/dot_general | solution.py:50
  107.3 6.5 %add_convert_fusion.3 = bf16[768,2048]{1,0:T(8,128)(2,1)} fusion(f32[768,2048]{1,0:T(8,128)} %copy-done.4, f32[2048]{0:T(1024)S(1)} %bitcast.251, f32[768]{0:T(1024)S(1)} %add_rsqrt_fusion.1, f32[768]{0:T(1024)S(1)} %broadcast_multiply_fusion.2, bf16[5,32,2048]{2,1,0:T(8,128)(2,1)} %param.25, bf16[768,160]{0,1:T(8,128)(2,1)S(1)} %fusion.25, ...), kind=kOutput, calls=%fused_computation.27 | convolution fusion | flops 111673344 | bytes 12779520 | tf_op jit(solution)/shard_map/dot_general | solution.py:39
  113.8 5.4 %add_convert_fusion.4 = bf16[768,2048]{1,0:T(8,128)(2,1)} fusion(f32[768,2048]{1,0:T(8,128)} %copy-done.4, f32[2048]{0:T(1024)S(1)} %bitcast.250, f32[768]{0:T(1024)S(1)} %add_rsqrt_fusion.1, f32[768]{0:T(1024)S(1)} %broadcast_multiply_fusion.2, bf16[5,32,2048]{2,1,0:T(8,128)(2,1)} %param.25, bf16[768,160]{0,1:T(8,128)(2,1)S(1)} %fusion.25, ...), kind=kOutput, calls=%fused_computation.28 | convolution fusion | flops 111673344 | bytes 12779520 | tf_op jit(solution)/shard_map/dot_general | solution.py:39
  119.2 4.2 add_convert_fusion.6
  124.4 1.5 slice_bitcast_fusion.19
  126.5 3.1 fusion.102
  129.6 3.1 convolution_bitcast_fusion.4
  132.8 3.1 multiply_reduce_fusion.1
  140.6 5.5 %collective-permute-start.5 = (f32[2,65,64]{1,2,0:T(8,128)S(1)}, f32[2,65,64]{1,2,0:T(8,128)S(1)}, u32[]{:S(2)}, u32[]{:S(2)}) collective-permute-start(f32[2,65,64]{1,2,0:T(8,128)S(1)} %pad_maximum_fusion.4), channel_id=1, source_target_pairs={{0,96},{16,112},{1,97},{17,113},{2,98},{18,114},{3,99},{19,115},{4... | collective-permute-start | bytes 99848 | tf_op jit(solution)/shard_map/ppermute | solution.py:20
  150.6 1.4 convolution_select_fusion
  152.0 1.6 fusion.24
  153.6 3.1 collective-permute-start.1
  156.9 3.6 collective-permute-start
  161.2 3.4 collective-permute-done
  167.1 6.1 %multiply_convert_fusion = bf16[768,128]{1,0:T(8,128)(2,1)S(1)} fusion(bf16[6,2048,128]{2,1,0:T(8,128)(2,1)} %all-gather.6.cloned.1.call-done, f32[768,2048]{1,0:T(8,128)} %copy-done.4, f32[2048]{0:T(1024)S(1)} %bitcast.256, f32[768]{0:T(1024)S(1)} %add_rsqrt_fusion.1, f32[768]{0:T(1024)S(1)} %broadcast_multiply_fusion.2, f32[768,128]{1,0:T(8,128)S(1)} %copy.84, ...), kind=kOutput, calls=%fused_computation.85 | convolution fusion | flops 515211264 | bytes 11532800 | tf_op jit(solution)/shard_map/dot_general | solution.py:141
  173.2 3.7 convolution_convert_fusion.1
  176.9 8.6 %all-gather.8.cloned.1.call-done = bf16[2,2048,448]{1,2,0:T(8,128)(2,1)} async-done(((bf16[2,256,448]{1,2,0:T(8,128)(2,1)}), bf16[2,2048,448]{1,2,0:T(8,128)(2,1)}) %all-gather.8.cloned.1.call-update) | async-done | bytes 3670032 | tf_op jit(solution)/shard_map/all_gather | solution.py:121
  185.8 155.2 %all-reduce.2.cloned.1.call-done = bf16[768,2048]{1,0:T(8,128)(2,1)} async-done(((bf16[768,2048]{1,0:T(8,128)(2,1)}), bf16[768,2048]{1,0:T(8,128)(2,1)}) %all-reduce.2.cloned.1.call-update) | async-done | bytes 3145744 | tf_op jit(solution)/shard_map/psum | solution.py:217
  341.0 3.8 convert_reduce_fusion.1
  345.8 3.6 collective-permute-start.7
  350.2 2.6 copy-done.7
  355.5 3.7 pad_maximum_fusion.1
  359.2 3.5 bitcast_subtract_fusion
  362.8 10.8 %convolution_convert_fusion = bf16[768,2048]{1,0:T(8,128)(2,1)} fusion(bf16[2,2048,448]{1,2,0:T(8,128)(2,1)} %all-gather.8.cloned.1.call-done, f32[768,2048]{1,0:T(8,128)} %bitcast_subtract_fusion, f32[2048]{0:T(1024)S(1)} %bitcast.255, bf16[768,2048]{1,0:T(8,128)(2,1)} %copy-done.5, f32[768]{0:T(1024)S(1)} %add_rsqrt_fusion, ...), kind=kOutput, calls=%fused_computation.32 | convolution fusion | flops 2830614528 | bytes 16267264 | tf_op jit(solution)/shard_map/dot_general | solution.py:237
  373.6 4.6 copy.93
  378.9 1.3 compare_and_fusion.3
  382.3 3.1 collective-permute-start.12
  386.7 4.0 collective-permute-start.14
  390.7 4.0 collective-permute-start.13
  394.7 2.5 collective-permute-done.13
  399.0 5.7 %collective-permute-start.16 = (f32[3,2,128]{2,1,0:T(2,128)S(1)}, f32[3,2,128]{2,1,0:T(2,128)S(1)}, u32[]{:S(2)}, u32[]{:S(2)}) collective-permute-start(f32[3,2,128]{2,1,0:T(2,128)S(1)} %pad_maximum_fusion.5), channel_id=1, source_target_pairs={{0,32},{16,48},{32,64},{48,80},{64,96},{80,112},{1,33},{17,49},{33... | collective-permute-start | bytes 9224 | tf_op jit(solution)/shard_map/ppermute | solution.py:20
  406.8 2.3 collective-permute-start.18
  409.1 6.1 %collective-permute-start.17 = (f32[3,2,128]{2,1,0:T(2,128)S(1)}, f32[3,2,128]{2,1,0:T(2,128)S(1)}, u32[]{:S(2)}, u32[]{:S(2)}) collective-permute-start(f32[3,2,128]{2,1,0:T(2,128)S(1)} %pad_maximum_fusion.5), channel_id=1, source_target_pairs={{0,16},{16,32},{32,48},{48,64},{64,80},{80,96},{96,112},{1,17},{17... | collective-permute-start | bytes 9224 | tf_op jit(solution)/shard_map/ppermute | solution.py:20
  417.1 36.9 %reduce-scatter.4.cloned.1.call-done = bf16[128,768]{1,0:T(8,128)(2,1)} async-done(((bf16[2048,768]{1,0:T(8,128)(2,1)}), bf16[128,768]{1,0:T(8,128)(2,1)}) %reduce-scatter.4.cloned.1.call-update) | async-done | bytes 196624
  455.1 5.3 %fusion.30 = bf16[768,128]{1,0:T(8,128)(2,1)S(1)} fusion(f32[768,2048]{1,0:T(8,128)} %bitcast_subtract_fusion, f32[2048]{0:T(1024)S(1)} %bitcast.254, bf16[6,2048,128]{2,1,0:T(8,128)(2,1)} %all-gather.6.cloned.1.call-done, bf16[768,128]{1,0:T(8,128)(2,1)S(1)} %copy.94, bf16[768,2048]{1,0:T(8,128)(2,1)} %copy-done.5, s32[]{:T(128)S(6)} %select_n.206, ...), kind=kOutput, calls=%fused_computation.66 | convolution fusion | flops 412876800 | bytes 10565636 | tf_op jit(solution)/shard_map/dot_general | solution.py:233
  460.4 3.4 collective-permute-start.9
  463.8 3.1 collective-permute-start.8
  468.9 3.9 collective-permute-start.10
  473.0 8.4 %collective-permute-done.10 = bf16[3,256,128]{2,1,0:T(8,128)(2,1)S(1)} collective-permute-done((bf16[3,256,128]{2,1,0:T(8,128)(2,1)S(1)}, bf16[3,256,128]{2,1,0:T(8,128)(2,1)S(1)}, u32[]{:S(2)}, u32[]{:S(2)}) %collective-permute-start.10) | collective-permute-done | bytes 196640 | tf_op jit(solution)/shard_map/ppermute | solution.py:20
  (234 shorter events, 58.4 us)
Async XLA Ops:
  7.2 85.2 %copy-start = (bf16[2048,160]{0,1:T(8,128)(2,1)S(1)}, bf16[2048,160]{0,1:T(8,128)(2,1)}, u32[]{:S(2)}) copy-start(bf16[2048,160]{0,1:T(8,128)(2,1)} %param.24) | copy-start | bytes 1966084
  7.2 24.8 %copy-start.9 = (f32[256,448]{0,1:T(8,128)S(1)}, f32[256,448]{0,1:T(8,128)}, u32[]{:S(2)}) copy-start(f32[256,448]{0,1:T(8,128)} %param.20) | copy-start | bytes 1376260
  7.2 24.8 %copy-start.10 = (f32[448,256]{1,0:T(8,128)S(1)}, f32[448,256]{1,0:T(8,128)}, u32[]{:S(2)}) copy-start(f32[448,256]{1,0:T(8,128)} %param.22) | copy-start | bytes 1376260
  7.2 25.7 %copy-start.13 = (f32[8,2048]{1,0:T(8,128)S(1)}, f32[8,2048]{1,0:T(8,128)}, u32[]{:S(2)}) copy-start(f32[8,2048]{1,0:T(8,128)} %param.23) | copy-start | bytes 196612
  7.2 68.5 %all-gather.4.cloned.1.call-start = ((), (), s32[]{:S(2)}) async-start(), calls=%async_computation.1 | async-start | bytes 3377152 | tf_op jit(solution)/shard_map/all_gather | solution.py:108
  21.3 102.8 %all-gather.6.cloned.1.call-start = ((), (), s32[]{:S(2)}) async-start(), calls=%async_computation.2 | async-start | bytes 3538944 | tf_op jit(solution)/shard_map/all_gather | solution.py:119
  83.7 101.8 %all-gather.8.cloned.1.call-start = ((), (), s32[]{:S(2)}) async-start(), calls=%async_computation.3 | async-start | bytes 4128768 | tf_op jit(solution)/shard_map/all_gather | solution.py:121
  86.9 4.2 copy-start.2
  94.9 24.3 %copy-start.11 = (bf16[768,160]{0,1:T(8,128)(2,1)}, bf16[768,160]{0,1:T(8,128)(2,1)S(1)}, u32[]{:S(2)}) copy-start(bf16[768,160]{0,1:T(8,128)(2,1)S(1)} %fusion.25) | copy-start | bytes 737284
  94.9 6.2 %copy-start.14 = (bf16[64,128]{1,0:T(8,128)(2,1)S(1)}, bf16[64,128]{1,0:T(8,128)(2,1)}, u32[]{:S(2)}) copy-start(bf16[64,128]{1,0:T(8,128)(2,1)} %param.27) | copy-start | bytes 49156
  94.9 6.2 %copy-start.21 = (f32[128]{0:T(128)S(1)}, f32[128]{0:T(128)}, u32[]{:S(2)}) copy-start(f32[128]{0:T(128)} %param.28) | copy-start | bytes 1540
  107.2 6.6 %copy-start.18 = (f32[6,2,64]{2,1,0:T(2,128)}, f32[6,2,64]{2,1,0:T(2,128)S(1)}, u32[]{:S(2)}) copy-start(f32[6,2,64]{2,1,0:T(2,128)S(1)} %get-tuple-element.61) | copy-start | bytes 9220
  107.3 6.5 %copy-start.3 = (bf16[776,2048]{1,0:T(8,128)(2,1)S(1)}, bf16[776,2048]{1,0:T(8,128)(2,1)}, u32[]{:S(2)}) copy-start(bf16[776,2048]{1,0:T(8,128)(2,1)} %all-gather.4.cloned.1.call-done) | copy-start | bytes 9535492
  107.3 11.9 %slice-start = ((s8[6291456]{0:T(1024)(128)(4,1)}), s8[4194304]{0:T(1024)(128)(4,1)S(1)}, s32[]{:S(2)}) async-start(s8[6291456]{0:T(1024)(128)(4,1)} %bitcast.224), calls=%async_computation.6 | async-start | bytes 8388608
  113.8 5.4 %slice-start.1 = ((s8[6291456]{0:T(1024)(128)(4,1)}), s8[2097152]{0:T(1024)(128)(4,1)S(1)}, s32[]{:S(2)}) async-start(s8[6291456]{0:T(1024)(128)(4,1)} %bitcast.224), calls=%async_computation.7 | async-start | bytes 4194304
  124.1 216.8 %all-reduce.2.cloned.1.call-start = ((), (), s32[]{:S(2)}) async-start(), calls=%async_computation.4 | async-start | bytes 6291456 | tf_op jit(solution)/shard_map/psum | solution.py:217
  125.8 6.9 %copy-start.20 = (f32[2,64]{1,0:T(2,128)S(1)}, f32[2,64]{1,0:T(2,128)}, u32[]{:S(2)}) copy-start(f32[2,64]{1,0:T(2,128)} %mul.596) | copy-start | bytes 1540
  132.7 17.8 %copy-start.12 = (pred[128,128]{1,0:T(8,128)(4,1)S(1)}, pred[128,128]{1,0:T(8,128)(4,1)}, u32[]{:S(2)}) copy-start(pred[128,128]{1,0:T(8,128)(4,1)} %iota_compare_fusion) | copy-start | bytes 49156
  135.9 29.1 %copy-start.19 = (f32[6,2,64]{2,1,0:T(2,128)S(1)}, f32[6,2,64]{2,1,0:T(2,128)}, u32[]{:S(2)}) copy-start(f32[6,2,64]{2,1,0:T(2,128)} %copy-done.18) | copy-start | bytes 9220
  139.9 27.1 %copy-start.17 = (f32[1,2048]{1,0:T(1,128)S(1)}, f32[1,2048]{1,0:T(1,128)}, u32[]{:S(2)}) copy-start(f32[1,2048]{1,0:T(1,128)} %get-tuple-element.37) | copy-start | bytes 24580
  140.0 27.1 %copy-start.24 = (f32[128]{0:T(128)S(1)}, f32[128]{0:T(128)}, u32[]{:S(2)}) copy-start(f32[128]{0:T(128)} %param.30) | copy-start | bytes 1540
  140.0 24.8 %collective-permute-start.6 = (f32[2,65,64]{1,2,0:T(8,128)S(1)}, f32[2,65,64]{1,2,0:T(8,128)S(1)}, u32[]{:S(2)}, u32[]{:S(2)}) collective-permute-start(f32[2,65,64]{1,2,0:T(8,128)S(1)} %pad_maximum_fusion.4), channel_id=1, source_target_pairs={{0,112},{1,113},{2,114},{3,115},{4,116},{5,117},{6,118},{7,119},{8... | collective-permute-start | bytes 99848 | tf_op jit(solution)/shard_map/ppermute | solution.py:20
  140.6 13.0 %collective-permute-start.5 = (f32[2,65,64]{1,2,0:T(8,128)S(1)}, f32[2,65,64]{1,2,0:T(8,128)S(1)}, u32[]{:S(2)}, u32[]{:S(2)}) collective-permute-start(f32[2,65,64]{1,2,0:T(8,128)S(1)} %pad_maximum_fusion.4), channel_id=1, source_target_pairs={{0,96},{16,112},{1,97},{17,113},{2,98},{18,114},{3,99},{19,115},{4... | collective-permute-start | bytes 99848 | tf_op jit(solution)/shard_map/ppermute | solution.py:20
  146.2 10.8 %collective-permute-start.4 = (f32[2,65,64]{1,2,0:T(8,128)S(1)}, f32[2,65,64]{1,2,0:T(8,128)S(1)}, u32[]{:S(2)}, u32[]{:S(2)}) collective-permute-start(f32[2,65,64]{1,2,0:T(8,128)S(1)} %pad_maximum_fusion.4), channel_id=1, source_target_pairs={{0,80},{16,96},{32,112},{1,81},{17,97},{33,113},{2,82},{18,98},{34... | collective-permute-start | bytes 99848 | tf_op jit(solution)/shard_map/ppermute | solution.py:20
  147.5 13.2 %collective-permute-start.3 = (f32[2,65,64]{1,2,0:T(8,128)S(1)}, f32[2,65,64]{1,2,0:T(8,128)S(1)}, u32[]{:S(2)}, u32[]{:S(2)}) collective-permute-start(f32[2,65,64]{1,2,0:T(8,128)S(1)} %pad_maximum_fusion.4), channel_id=1, source_target_pairs={{0,64},{16,80},{32,96},{48,112},{1,65},{17,81},{33,97},{49,113},{2... | collective-permute-start | bytes 99848 | tf_op jit(solution)/shard_map/ppermute | solution.py:20
  148.8 12.1 %collective-permute-start.2 = (f32[2,65,64]{1,2,0:T(8,128)S(1)}, f32[2,65,64]{1,2,0:T(8,128)S(1)}, u32[]{:S(2)}, u32[]{:S(2)}) collective-permute-start(f32[2,65,64]{1,2,0:T(8,128)S(1)} %pad_maximum_fusion.4), channel_id=1, source_target_pairs={{0,48},{16,64},{32,80},{48,96},{64,112},{1,49},{17,65},{33,81},{49... | collective-permute-start | bytes 99848 | tf_op jit(solution)/shard_map/ppermute | solution.py:20
  153.6 7.4 %collective-permute-start.1 = (f32[2,65,64]{1,2,0:T(8,128)S(1)}, f32[2,65,64]{1,2,0:T(8,128)S(1)}, u32[]{:S(2)}, u32[]{:S(2)}) collective-permute-start(f32[2,65,64]{1,2,0:T(8,128)S(1)} %pad_maximum_fusion.4), channel_id=1, source_target_pairs={{0,32},{16,48},{32,64},{48,80},{64,96},{80,112},{1,33},{17,49},{33... | collective-permute-start | bytes 99848 | tf_op jit(solution)/shard_map/ppermute | solution.py:20
  156.9 7.7 %collective-permute-start = (f32[2,65,64]{1,2,0:T(8,128)S(1)}, f32[2,65,64]{1,2,0:T(8,128)S(1)}, u32[]{:S(2)}, u32[]{:S(2)}) collective-permute-start(f32[2,65,64]{1,2,0:T(8,128)S(1)} %pad_maximum_fusion.4), channel_id=1, source_target_pairs={{0,16},{16,32},{32,48},{48,64},{64,80},{80,96},{96,112},{1,17},{17... | collective-permute-start | bytes 99848 | tf_op jit(solution)/shard_map/ppermute | solution.py:20
  173.2 12.4 %copy-start.22 = (s32[8]{0:T(128)S(1)}, s32[8]{0:T(128)}, u32[]{:S(2)}) copy-start(s32[8]{0:T(128)} %param.31) | copy-start | bytes 100
  185.5 268.5 %reduce-scatter.4.cloned.1.call-start = ((), (), s32[]{:S(2)}) async-start(), calls=%async_computation.5 | async-start | bytes 3342336
  344.8 5.4 %copy-start.5 = (bf16[768,2048]{1,0:T(8,128)(2,1)}, bf16[768,2048]{1,0:T(8,128)(2,1)S(1)}, u32[]{:S(2)}) copy-start(bf16[768,2048]{1,0:T(8,128)(2,1)S(1)} %get-tuple-element.13) | copy-start | bytes 9437188
  345.8 7.0 %collective-permute-start.7 = (bf16[1,2048]{1,0:T(2,128)(2,1)S(1)}, bf16[1,2048]{1,0:T(2,128)(2,1)S(1)}, u32[]{:S(2)}, u32[]{:S(2)}) collective-permute-start(bf16[1,2048]{1,0:T(2,128)(2,1)S(1)} %slice.382), channel_id=1, source_target_pairs={{0,16},{16,32},{32,48},{48,64},{64,80},{80,96},{96,112},{1,17},{17... | collective-permute-start | bytes 12296 | tf_op jit(solution)/shard_map/ppermute | solution.py:20
  355.5 3.7 copy-start.6
  359.2 3.6 copy-start.16
  373.6 81.5 %copy-start.15 = (f32[1,2048]{1,0:T(1,128)S(1)}, f32[1,2048]{1,0:T(1,128)}, u32[]{:S(2)}) copy-start(f32[1,2048]{1,0:T(1,128)} %get-tuple-element.43) | copy-start | bytes 24580
  382.3 12.4 %collective-permute-start.12 = (f32[3,2,4096]{2,1,0:T(2,128)S(1)}, f32[3,2,4096]{2,1,0:T(2,128)S(1)}, u32[]{:S(2)}, u32[]{:S(2)}) collective-permute-start(f32[3,2,4096]{2,1,0:T(2,128)S(1)} %reshape.491), channel_id=1, source_target_pairs={{0,32},{16,48},{32,64},{48,80},{64,96},{80,112},{1,33},{17,49},{33... | collective-permute-start | bytes 294920 | tf_op jit(solution)/shard_map/ppermute | solution.py:20
  385.4 11.9 %collective-permute-start.15 = (f32[3,2,4096]{2,1,0:T(2,128)S(1)}, f32[3,2,4096]{2,1,0:T(2,128)S(1)}, u32[]{:S(2)}, u32[]{:S(2)}) collective-permute-start(f32[3,2,4096]{2,1,0:T(2,128)S(1)} %reshape.491), channel_id=1, source_target_pairs={{32,0},{48,16},{64,32},{80,48},{96,64},{112,80},{33,1},{49,17},{65... | collective-permute-start | bytes 294920 | tf_op jit(solution)/shard_map/ppermute | solution.py:20
  386.7 10.5 %collective-permute-start.14 = (f32[3,2,4096]{2,1,0:T(2,128)S(1)}, f32[3,2,4096]{2,1,0:T(2,128)S(1)}, u32[]{:S(2)}, u32[]{:S(2)}) collective-permute-start(f32[3,2,4096]{2,1,0:T(2,128)S(1)} %reshape.491), channel_id=1, source_target_pairs={{16,0},{32,16},{48,32},{64,48},{80,64},{96,80},{112,96},{17,1},{33... | collective-permute-start | bytes 294920 | tf_op jit(solution)/shard_map/ppermute | solution.py:20
  390.7 6.5 %collective-permute-start.13 = (f32[3,2,4096]{2,1,0:T(2,128)S(1)}, f32[3,2,4096]{2,1,0:T(2,128)S(1)}, u32[]{:S(2)}, u32[]{:S(2)}) collective-permute-start(f32[3,2,4096]{2,1,0:T(2,128)S(1)} %reshape.491), channel_id=1, source_target_pairs={{0,16},{16,32},{32,48},{48,64},{64,80},{80,96},{96,112},{1,17},{17... | collective-permute-start | bytes 294920 | tf_op jit(solution)/shard_map/ppermute | solution.py:20
  399.0 16.2 %collective-permute-start.16 = (f32[3,2,128]{2,1,0:T(2,128)S(1)}, f32[3,2,128]{2,1,0:T(2,128)S(1)}, u32[]{:S(2)}, u32[]{:S(2)}) collective-permute-start(f32[3,2,128]{2,1,0:T(2,128)S(1)} %pad_maximum_fusion.5), channel_id=1, source_target_pairs={{0,32},{16,48},{32,64},{48,80},{64,96},{80,112},{1,33},{17,49},{33... | collective-permute-start | bytes 9224 | tf_op jit(solution)/shard_map/ppermute | solution.py:20
  405.5 11.0 %collective-permute-start.19 = (f32[3,2,128]{2,1,0:T(2,128)S(1)}, f32[3,2,128]{2,1,0:T(2,128)S(1)}, u32[]{:S(2)}, u32[]{:S(2)}) collective-permute-start(f32[3,2,128]{2,1,0:T(2,128)S(1)} %pad_maximum_fusion.5), channel_id=1, source_target_pairs={{32,0},{48,16},{64,32},{80,48},{96,64},{112,80},{33,1},{49,17},{65... | collective-permute-start | bytes 9224 | tf_op jit(solution)/shard_map/ppermute | solution.py:20
  406.8 9.7 %collective-permute-start.18 = (f32[3,2,128]{2,1,0:T(2,128)S(1)}, f32[3,2,128]{2,1,0:T(2,128)S(1)}, u32[]{:S(2)}, u32[]{:S(2)}) collective-permute-start(f32[3,2,128]{2,1,0:T(2,128)S(1)} %pad_maximum_fusion.5), channel_id=1, source_target_pairs={{16,0},{32,16},{48,32},{64,48},{80,64},{96,80},{112,96},{17,1},{33... | collective-permute-start | bytes 9224 | tf_op jit(solution)/shard_map/ppermute | solution.py:20
  409.1 7.4 %collective-permute-start.17 = (f32[3,2,128]{2,1,0:T(2,128)S(1)}, f32[3,2,128]{2,1,0:T(2,128)S(1)}, u32[]{:S(2)}, u32[]{:S(2)}) collective-permute-start(f32[3,2,128]{2,1,0:T(2,128)S(1)} %pad_maximum_fusion.5), channel_id=1, source_target_pairs={{0,16},{16,32},{32,48},{48,64},{64,80},{80,96},{96,112},{1,17},{17... | collective-permute-start | bytes 9224 | tf_op jit(solution)/shard_map/ppermute | solution.py:20
  455.1 28.0 %copy-start.1 = (bf16[2048,160]{0,1:T(8,128)(2,1)S(1)}, bf16[2048,160]{0,1:T(8,128)(2,1)}, u32[]{:S(2)}) copy-start(bf16[2048,160]{0,1:T(8,128)(2,1)} %param.24) | copy-start | bytes 1966084
  460.4 12.5 %collective-permute-start.9 = (bf16[3,256,128]{2,1,0:T(8,128)(2,1)S(1)}, bf16[3,256,128]{2,1,0:T(8,128)(2,1)S(1)}, u32[]{:S(2)}, u32[]{:S(2)}) collective-permute-start(bf16[3,256,128]{2,1,0:T(8,128)(2,1)S(1)} %bitcast.242), channel_id=1, source_target_pairs={{0,16},{16,32},{32,48},{48,64},{64,80},{80,96},{96,112},{1,17},{17... | collective-permute-start | bytes 589832 | tf_op jit(solution)/shard_map/ppermute | solution.py:20
  463.8 9.1 %collective-permute-start.8 = (bf16[3,256,128]{2,1,0:T(8,128)(2,1)S(1)}, bf16[3,256,128]{2,1,0:T(8,128)(2,1)S(1)}, u32[]{:S(2)}, u32[]{:S(2)}) collective-permute-start(bf16[3,256,128]{2,1,0:T(8,128)(2,1)S(1)} %bitcast.243), channel_id=1, source_target_pairs={{0,32},{16,48},{32,64},{48,80},{64,96},{80,112},{1,33},{17,49},{33... | collective-permute-start | bytes 589832 | tf_op jit(solution)/shard_map/ppermute | solution.py:20
  467.6 13.8 %collective-permute-start.11 = (bf16[3,256,128]{2,1,0:T(8,128)(2,1)S(1)}, bf16[3,256,128]{2,1,0:T(8,128)(2,1)S(1)}, u32[]{:S(2)}, u32[]{:S(2)}) collective-permute-start(bf16[3,256,128]{2,1,0:T(8,128)(2,1)S(1)} %bitcast.244), channel_id=1, source_target_pairs={{32,0},{48,16},{64,32},{80,48},{96,64},{112,80},{33,1},{49,17},{65... | collective-permute-start | bytes 589832 | tf_op jit(solution)/shard_map/ppermute | solution.py:20
  468.9 12.5 %collective-permute-start.10 = (bf16[3,256,128]{2,1,0:T(8,128)(2,1)S(1)}, bf16[3,256,128]{2,1,0:T(8,128)(2,1)S(1)}, u32[]{:S(2)}, u32[]{:S(2)}) collective-permute-start(bf16[3,256,128]{2,1,0:T(8,128)(2,1)S(1)} %bitcast.245), channel_id=1, source_target_pairs={{16,0},{32,16},{48,32},{64,48},{80,64},{96,80},{112,96},{17,1},{33... | collective-permute-start | bytes 589832 | tf_op jit(solution)/shard_map/ppermute | solution.py:20
  (4 other events, 11.1 us)
Sparse Core Ops, SparseCore 0:
  21.5 54.1 all-gather.3
  83.8 40.2 all-gather.5
  125.7 59.7 all-gather.7
  187.9 153.0 all-reduce.1
  378.4 75.6 reduce-scatter.3

commit v4 on v3

--- a/solution.py
+++ b/solution.py
@@ -18,6 +18,60 @@
     count = lax.axis_size(axis)
     initial, last = (max(0, -steps), min(count, count - steps))
     return lax.ppermute(value, axis, [(source, source + steps) for source in range(initial, last)])
+
+
+def _swap(value, axis, flip):
+    count = lax.axis_size(axis)
+    return lax.ppermute(value, axis, [(s, s ^ flip) for s in range(count)])
+
+
+def _ring(value, axis, step):
+    count = lax.axis_size(axis)
+    pairs = []
+    for s in range(count):
+        z = (s // 2) % 4
+        target = s - z * 2 + ((z + step) % 4) * 2
+        pairs.append((s, target))
+    return lax.ppermute(value, axis, pairs)
+
+
+def hier_reduce_scatter(partial, axis):
+    h = lax.axis_index(axis)
+    rows, width = partial.shape
+    W = width // 16
+    core = h % 2
+    z = (h // 2) % 4
+    yh = h // 8
+    blocks = partial.reshape(rows, 2, 4, 2, W)
+    mine = jnp.where(core == 0, blocks[:, :, :, 0], blocks[:, :, :, 1])
+    other = jnp.where(core == 0, blocks[:, :, :, 1], blocks[:, :, :, 0])
+    acc = mine.astype(jnp.float32) + _swap(other, axis, 1).astype(jnp.float32)
+    acc = acc.astype(jnp.bfloat16)
+    zsel = lambda a, k: jnp.take(a, k, axis=2)
+    total = zsel(acc, z).astype(jnp.float32)
+    for step in (1, 2, 3):
+        send = zsel(acc, (z + step) % 4)
+        total = total + _ring(send, axis, step).astype(jnp.float32)
+    total = total.astype(jnp.bfloat16)
+    keep = jnp.where(yh == 0, total[:, 0], total[:, 1])
+    give = jnp.where(yh == 0, total[:, 1], total[:, 0])
+    result = keep.astype(jnp.float32) + _swap(give, axis, 8).astype(jnp.float32)
+    return result
+
+
+def hier_all_gather(piece, axis):
+    h = lax.axis_index(axis)
+    core = h % 2
+    z = (h // 2) % 4
+    yh = h // 8
+    got = _swap(piece, axis, 8)
+    pair = jnp.where(yh == 0, jnp.stack([piece, got], 1), jnp.stack([got, piece], 1))
+    ring_parts = [pair] + [_ring(pair, axis, -step % 4) for step in (1, 2, 3)]
+    stacked = jnp.stack(ring_parts, 2)
+    by_z = jnp.take(stacked, (jnp.arange(4) - z) % 4, axis=2)
+    partner = _swap(by_z, axis, 1)
+    both = jnp.where(core == 0, jnp.stack([by_z, partner], 3), jnp.stack([partner, by_z], 3))
+    return both.reshape(piece.shape[0], 16 * piece.shape[1])
 
 
 def layer_norm(value_rows):
@@ -213,8 +267,8 @@
     mixer_partial = lax.dot_general(
         normed, output_weight_t, (((1,), (1,)), ((), ())), preferred_element_type=jnp.float32
     ).astype(jnp.bfloat16)
-    mixer_partial, _ = lax.optimization_barrier((mixer_partial, second_full))
-    mixer_total = lax.psum(mixer_partial, "head").astype(jnp.float32)
+    mixer_owned = hier_reduce_scatter(mixer_partial, "head").astype(jnp.bfloat16)
+    mixer_total = hier_all_gather(mixer_owned, "head").astype(jnp.float32)
     residual = (embedded.astype(jnp.float32) + mixer_total).astype(jnp.bfloat16)
     last_residual = residual[slot_rows - 1 : slot_rows]
     arriving = passed_along(last_residual, "group", 1)
@@ -233,14 +287,12 @@
     gate_raw_two = jnp.dot(gate_input, projections[4], preferred_element_type=jnp.float32)
     key_raw = jnp.dot(key_input, key_weight, preferred_element_type=jnp.float32)
     squared = jnp.square(jax.nn.relu(key_raw)).astype(jnp.bfloat16)
-    channel = lax.psum_scatter(
+    channel = hier_reduce_scatter(
         lax.dot_general(
             squared, value_weight_t, (((1,), (1,)), ((), ())), preferred_element_type=jnp.float32
         ).astype(jnp.bfloat16),
         "head",
-        scatter_dimension=1,
-        tiled=True,
-    ).astype(jnp.float32)
+    )
     gate_two = jax.nn.sigmoid(gate_raw_two)
     residual_local = lax.dynamic_slice_in_dim(
         residual, head_here * features_on_shard, features_on_shard, 1

time: 496 us -> 425 us (0.86)
  waiting for transfers between devices: 259 us -> 121 us
  local copies, waits for them, and re-layouts: 40.3 us -> 76.4 us
  starting transfers between devices: 60.7 us -> 77.9 us
  other arithmetic: 47.7 us -> 62.4 us
    psum x1 -> x0, waiting for transfers between devices: 155 us -> none  [per_device(): mixer_total = lax.psum(mixer_partial, 'head').astype(jnp.float32)]
    ppermute x0 -> x15, waiting for transfers between devices: none -> 57.5 us  [the longest x9 39.3 us: _ring(): return lax.ppermute(value, axis, pairs)]
    unnamed x6 -> x3, waiting for transfers between devices: 37 us -> 0.05 us
    convert_element_type x0 -> x4, local copies, waits for them, and re-layouts: none -> 22.8 us  [the longest x2 13.3 us: per_device(): mixer_total = hier_all_gather(mixer_owned, 'head').astype(jnp.float32)]
    ppermute x0 -> x15, starting transfers between devices: none -> 21.1 us  [the longest x9 12.7 us: _ring(): return lax.ppermute(value, axis, pairs)]
    convert_element_type x0 -> x6, other arithmetic: none -> 9.57 us  [the longest x1 4.97 us: per_device(): mixer_total = hier_all_gather(mixer_owned, 'head').astype(jnp.float32)]
    all_gather x1, waiting for transfers between devices: 8.6 us -> 0.01 us  [per_device(): second_full = lax.all_gather(second_pack, 'group', axis=1, tiled=True)]
    slice x1 -> x3, local copies, waits for them, and re-layouts: 0.66 us -> 8.3 us  [the longest x2 7.65 us: hier_reduce_scatter(): mine = jnp.where(core == 0, blocks[:, :, :, 0], blocks[:, :, :, 1])]
  transfers between devices with their start and end apart: 25 -> 38, of which waited for: 9 -> 17; matrix products, arithmetic and copies ran while one was open for 18% -> 30% of each run, Pallas kernels for 0% -> 0%
where the time goes in v4:
time: 425 us; the launch traced here: 419 us
  waiting for transfers between devices  121 us (28%)
  starting transfers between devices  77.9 us (18%)
  local copies, waits for them, and re-layouts  76.4 us (18%)
  matrix products  63.1 us (15%)
  other arithmetic  62.4 us (15%)
  between operations  17.5 us (4%)
    ppermute x20, starting transfers between devices, passed_along(): lax.ppermute(value, axis, [(source, source + steps) for source in range(i...  56.3 us
    all_gather x1, waiting for transfers between devices, per_device(): gathered_rows = lax.all_gather(own_rows, 'head', axis=1, tiled=True)  45.1 us
    ppermute x9, waiting for transfers between devices, _ring(): return lax.ppermute(value, axis, pairs)  39.3 us
    ppermute x6, waiting for transfers between devices, _swap(): return lax.ppermute(value, axis, [(s, s ^ flip) for s in range(count)])  18.2 us
    ppermute x20, waiting for transfers between devices, passed_along(): lax.ppermute(value, axis, [(source, source + steps) for source in range(i...  17.9 us
    dot_general x3, matrix products, mixed_inputs(): jnp.dot(column_part, blend_widening_maps[number], preferred_element_type=...  16.2 us
    unnamed x80, local copies, waits for them, and re-layouts  16 us
    convert_element_type x2, local copies, waits for them, and re-layouts, per_device(): mixer_total = hier_all_gather(mixer_owned, 'head').astype(jnp.float32)  13.3 us
  transfers between devices with their start and end apart: 38, of which 17 were waited for; matrix products, arithmetic and copies ran while one was open for 30% of the time, Pallas kernels for 0%

profile of v4, /device:TPU:2, one launch (start us, length us, event | category | flops | bytes accessed | tf_op | source)
XLA Modules:
  0.0 418.7 jit_solution(18182406605088366057)
XLA Ops:
  10.6 9.8 %gather_fusion.2 = bf16[776,128]{1,0:T(8,128)(2,1)S(1)} fusion(bf16[65536,128]{1,0:T(8,128)(2,1)} %param.20, s32[1024]{0:T(1024)S(1)} %pad_clamp_fusion.3), kind=kCustom, calls=%fused_computation.4 | custom fusion | bytes 400416 | tf_op jit(solution)/shard_map/jit(_take)/gather | solution.py:161
  30.6 45.1 %all-gather.4.cloned.1.call-done = bf16[776,2048]{1,0:T(8,128)(2,1)} async-done(((bf16[776,128]{1,0:T(8,128)(2,1)}), bf16[776,2048]{1,0:T(8,128)(2,1)}) %all-gather.4.cloned.1.call-update) | async-done | bytes 3178512 | tf_op jit(solution)/shard_map/all_gather | solution.py:162
  92.2 6.2 %fusion.32 = bf16[768,64]{0,1:T(8,128)(2,1)S(1)} fusion(bf16[2048,64]{0,1:T(8,128)(2,1)S(1)} %copy-done.27, f32[768,2048]{1,0:T(8,128)} %copy-done.5, f32[2048]{0:T(1024)S(1)} %bitcast.319, f32[768]{0:T(1024)S(1)} %add_rsqrt_fusion.1, f32[768]{0:T(1024)S(1)} %broadcast_multiply_fusion.2, bf16[5,32,2048]{2,1,0:T(8,128)(2,1)} %param.27, ...), kind=kOutput, calls=%fused_computation.77 | convolution fusion | flops 313049088 | bytes 9994240 | tf_op jit(solution)/shard_map/dot_general | solution.py:104
  104.5 6.3 %add_convert_fusion.3 = bf16[768,2048]{1,0:T(8,128)(2,1)} fusion(f32[768,2048]{1,0:T(8,128)} %copy-done.5, f32[2048]{0:T(1024)S(1)} %bitcast.313, f32[768]{0:T(1024)S(1)} %add_rsqrt_fusion.1, f32[768]{0:T(1024)S(1)} %broadcast_multiply_fusion.2, bf16[5,32,2048]{2,1,0:T(8,128)(2,1)} %param.27, bf16[768,160]{0,1:T(8,128)(2,1)S(1)} %fusion.28, ...), kind=kOutput, calls=%fused_computation.28 | convolution fusion | flops 111673344 | bytes 12779520 | tf_op jit(solution)/shard_map/dot_general | solution.py:93
  110.8 5.3 %add_convert_fusion.4 = bf16[768,2048]{1,0:T(8,128)(2,1)} fusion(f32[768,2048]{1,0:T(8,128)} %copy-done.5, f32[2048]{0:T(1024)S(1)} %bitcast.312, f32[768]{0:T(1024)S(1)} %add_rsqrt_fusion.1, f32[768]{0:T(1024)S(1)} %broadcast_multiply_fusion.2, bf16[5,32,2048]{2,1,0:T(8,128)(2,1)} %param.27, bf16[768,160]{0,1:T(8,128)(2,1)S(1)} %fusion.28, ...), kind=kOutput, calls=%fused_computation.29 | convolution fusion | flops 111673344 | bytes 12779520 | tf_op jit(solution)/shard_map/dot_general | solution.py:93
  116.1 4.7 %add_convert_fusion.6 = bf16[768,2048]{1,0:T(8,128)(2,1)} fusion(f32[768,2048]{1,0:T(8,128)S(1)} %bitcast.279, f32[2048]{0:T(1024)S(1)} %bitcast.311, f32[768]{0:T(1024)S(1)} %add_rsqrt_fusion.1, f32[768]{0:T(1024)S(1)} %broadcast_multiply_fusion.2, bf16[5,32,2048]{2,1,0:T(8,128)(2,1)} %param.27, bf16[768,160]{0,1:T(8,128)(2,1)S(1)} %fusion.28, ...), kind=kOutput, calls=%fused_computation.31 | convolution fusion | flops 111673344 | bytes 12779520 | tf_op jit(solution)/shard_map/dot_general | solution.py:93
  123.8 3.2 fusion.111
  127.0 3.1 convolution_bitcast_fusion.4
  136.2 5.5 %collective-permute-start.5 = (f32[2,65,64]{1,2,0:T(8,128)S(1)}, f32[2,65,64]{1,2,0:T(8,128)S(1)}, u32[]{:S(2)}, u32[]{:S(2)}) collective-permute-start(f32[2,65,64]{1,2,0:T(8,128)S(1)} %pad_maximum_fusion.5), channel_id=1, source_target_pairs={{0,96},{16,112},{1,97},{17,113},{2,98},{18,114},{3,99},{19,115},{4... | collective-permute-start | bytes 99848 | tf_op jit(solution)/shard_map/ppermute | solution.py:20
  149.2 3.1 collective-permute-start.1
  152.5 3.4 collective-permute-start
  161.2 6.0 %multiply_convert_fusion = bf16[768,128]{1,0:T(8,128)(2,1)S(1)} fusion(bf16[6,2048,128]{2,1,0:T(8,128)(2,1)} %all-gather.6.cloned.1.call-done, f32[768,2048]{1,0:T(8,128)} %copy-done.5, f32[2048]{0:T(1024)S(1)} %bitcast.318, f32[768]{0:T(1024)S(1)} %add_rsqrt_fusion.1, f32[768]{0:T(1024)S(1)} %broadcast_multiply_fusion.2, f32[768,128]{1,0:T(8,128)S(1)} %copy.100, ...), kind=kOutput, calls=%fused_computation.110 | convolution fusion | flops 515211264 | bytes 11532800 | tf_op jit(solution)/shard_map/dot_general | solution.py:195
  167.2 3.7 convolution_convert_fusion.1
  170.8 4.7 %copy.101 = bf16[768,2048]{0,1:T(8,128)(2,1)} copy(bf16[768,2048]{1,0:T(8,128)(2,1)} %convolution_convert_fusion.1) | data formatting | bytes 6291456 | tf_op jit(solution)/shard_map/convert_element_type | solution.py:269
  175.6 3.8 fusion.106
  184.0 2.8 select_bitcast_fusion.1
  186.9 3.6 collective-permute-done.7
  199.2 6.3 %collective-permute-done.8 = bf16[768,2,128]{2,0,1:T(8,128)(2,1)S(1)} collective-permute-done((bf16[768,2,128]{2,0,1:T(8,128)(2,1)S(1)}, bf16[768,2,128]{2,0,1:T(8,128)(2,1)S(1)}, u32[]{:S(2)}, u32[]{:S(2)}) %collective-permute-start.8) | collective-permute-done | bytes 393248 | tf_op jit(solution)/shard_map/ppermute | solution.py:35
  205.6 7.8 %collective-permute-done.10 = bf16[768,2,128]{2,0,1:T(8,128)(2,1)S(1)} collective-permute-done((bf16[768,2,128]{2,0,1:T(8,128)(2,1)S(1)}, bf16[768,2,128]{2,0,1:T(8,128)(2,1)S(1)}, u32[]{:S(2)}, u32[]{:S(2)}) %collective-permute-start.10) | collective-permute-done | bytes 393248 | tf_op jit(solution)/shard_map/ppermute | solution.py:35
  215.4 2.8 collective-permute-start.11
  218.3 5.3 %collective-permute-done.11 = bf16[768,128]{1,0:T(8,128)(2,1)S(1)} collective-permute-done((bf16[768,128]{1,0:T(8,128)(2,1)S(1)}, bf16[768,128]{1,0:T(8,128)(2,1)S(1)}, u32[]{:S(2)}, u32[]{:S(2)}) %collective-permute-start.11) | collective-permute-done | bytes 196640 | tf_op jit(solution)/shard_map/ppermute | solution.py:25
  223.7 2.8 collective-permute-start.12
  226.5 4.5 %collective-permute-done.12 = bf16[768,128]{1,0:T(8,128)(2,1)S(1)} collective-permute-done((bf16[768,128]{1,0:T(8,128)(2,1)S(1)}, bf16[768,128]{1,0:T(8,128)(2,1)S(1)}, u32[]{:S(2)}, u32[]{:S(2)}) %collective-permute-start.12) | collective-permute-done | bytes 196640 | tf_op jit(solution)/shard_map/ppermute | solution.py:25
  235.6 14.2 %collective-permute-done.15 = bf16[768,2,128]{2,0,1:T(8,128)(2,1)S(1)} collective-permute-done((bf16[768,2,128]{2,0,1:T(8,128)(2,1)S(1)}, bf16[768,2,128]{2,0,1:T(8,128)(2,1)S(1)}, u32[]{:S(2)}, u32[]{:S(2)}) %collective-permute-start.15) | collective-permute-done | bytes 393248 | tf_op jit(solution)/shard_map/ppermute | solution.py:35
  258.2 2.8 collective-permute-start.27
  262.3 4.6 %collective-permute-start.29 = (f32[3,2,4096]{2,1,0:T(2,128)S(1)}, f32[3,2,4096]{2,1,0:T(2,128)S(1)}, u32[]{:S(2)}, u32[]{:S(2)}) collective-permute-start(f32[3,2,4096]{2,1,0:T(2,128)S(1)} %reshape.651), channel_id=1, source_target_pairs={{16,0},{32,16},{48,32},{64,48},{80,64},{96,80},{112,96},{17,1},{33... | collective-permute-start | bytes 294920 | tf_op jit(solution)/shard_map/ppermute | solution.py:20
  266.8 4.0 collective-permute-start.28
  270.9 5.2 %collective-permute-done.28 = f32[3,2,4096]{2,1,0:T(2,128)S(1)} collective-permute-done((f32[3,2,4096]{2,1,0:T(2,128)S(1)}, f32[3,2,4096]{2,1,0:T(2,128)S(1)}, u32[]{:S(2)}, u32[]{:S(2)}) %collective-permute-start.28) | collective-permute-done | bytes 98336 | tf_op jit(solution)/shard_map/ppermute | solution.py:20
  276.4 5.0 %fusion.9 = f32[768,2,4,2,128]{4,0,1,2,3:T(8,128)} fusion(bf16[768,2,4,1,128]{4,0,1,2,3:T(8,128)(2,1)} %bitcast.100, bf16[768,2,4,1,128]{4,0,1,2,3:T(8,128)(2,1)S(1)} %bitcast_select_fusion, pred[]{:T(512)S(6)} %eq.57), kind=kLoop, calls=%fused_computation.38 | loop fusion | flops 6291456 | bytes 9437185 | tf_op jit(solution)/shard_map/convert_element_type | solution.py:271
  281.3 6.6 %copy.104 = f32[768,2,4,2,128]{0,4,3,2,1:T(8,128)} copy(f32[768,2,4,2,128]{4,0,1,2,3:T(8,128)} %fusion.9) | data formatting | bytes 12582912 | tf_op jit(solution)/shard_map/convert_element_type | solution.py:271
  288.0 6.7 %copy.105 = f32[768,2048]{1,0:T(8,128)} copy(f32[768,2048]{0,1:T(8,128)} %bitcast.285) | data formatting | bytes 12582912 | tf_op jit(solution)/shard_map/convert_element_type | solution.py:271
  294.6 4.6 %convert_reduce_fusion.1 = (f32[768]{0:T(1024)S(1)}, bf16[768,2048]{1,0:T(8,128)(2,1)S(1)}) fusion(f32[768,2048]{1,0:T(8,128)} %copy.105, bf16[776,2048]{1,0:T(8,128)(2,1)} %all-gather.4.cloned.1.call-done), kind=kLoop, calls=%fused_computation.13 | loop fusion | flops 7863552 | bytes 12585984 | tf_op jit(solution)/shard_map/reduce_sum | solution.py:79
  299.3 3.1 collective-permute-start.17
  309.5 3.7 pad_maximum_fusion.1
  313.2 3.6 bitcast_subtract_fusion
  316.8 10.9 %convolution_convert_fusion = bf16[768,2048]{1,0:T(8,128)(2,1)} fusion(bf16[2,2048,448]{1,2,0:T(8,128)(2,1)} %all-gather.8.cloned.1.call-done, f32[768,2048]{1,0:T(8,128)} %bitcast_subtract_fusion, f32[2048]{0:T(1024)S(1)} %bitcast.317, bf16[768,2048]{1,0:T(8,128)(2,1)} %copy-done.6, f32[768]{0:T(1024)S(1)} %add_rsqrt_fusion, ...), kind=kOutput, calls=%fused_computation.33 | convolution fusion | flops 2830614528 | bytes 16267264 | tf_op jit(solution)/shard_map/dot_general | solution.py:291
  327.7 4.7 %copy.106 = bf16[768,2048]{0,1:T(8,128)(2,1)} copy(bf16[768,2048]{1,0:T(8,128)(2,1)} %convolution_convert_fusion) | data formatting | bytes 6291456 | tf_op jit(solution)/shard_map/convert_element_type | solution.py:293
  332.4 3.8 fusion.105
  345.3 7.4 %collective-permute-start.31 = (f32[3,2,128]{2,1,0:T(2,128)S(1)}, f32[3,2,128]{2,1,0:T(2,128)S(1)}, u32[]{:S(2)}, u32[]{:S(2)}) collective-permute-start(f32[3,2,128]{2,1,0:T(2,128)S(1)} %pad_maximum_fusion.6), channel_id=1, source_target_pairs={{0,32},{16,48},{32,64},{48,80},{64,96},{80,112},{1,33},{17,49},{33... | collective-permute-start | bytes 9224 | tf_op jit(solution)/shard_map/ppermute | solution.py:20
  355.3 2.9 collective-permute-start.21
  360.8 3.4 collective-permute-start.32
  368.2 7.3 %collective-permute-done.21 = bf16[768,2,128]{2,0,1:T(8,128)(2,1)S(1)} collective-permute-done((bf16[768,2,128]{2,0,1:T(8,128)(2,1)S(1)}, bf16[768,2,128]{2,0,1:T(8,128)(2,1)S(1)}, u32[]{:S(2)}, u32[]{:S(2)}) %collective-permute-start.21) | collective-permute-done | bytes 393248 | tf_op jit(solution)/shard_map/ppermute | solution.py:35
  377.1 2.8 collective-permute-start.22
  380.5 4.8 %collective-permute-done.22 = bf16[768,128]{1,0:T(8,128)(2,1)S(1)} collective-permute-done((bf16[768,128]{1,0:T(8,128)(2,1)S(1)}, bf16[768,128]{1,0:T(8,128)(2,1)S(1)}, u32[]{:S(2)}, u32[]{:S(2)}) %collective-permute-start.22) | collective-permute-done | bytes 196640 | tf_op jit(solution)/shard_map/ppermute | solution.py:25
  385.3 5.3 %fusion.36 = bf16[768,128]{1,0:T(8,128)(2,1)S(1)} fusion(bf16[768,128]{1,0:T(8,128)(2,1)S(1)} %collective-permute-done.22, bf16[768,2048]{1,0:T(8,128)(2,1)} %copy-done.6, s32[]{:T(128)S(6)} %select_n.416, pred[]{:T(512)S(6)} %eq.58, bf16[768,2,128]{2,0,1:T(8,128)(2,1)S(1)} %add_convert_fusion.31, bf16[6,2048,128]{2,1,0:T(8,128)(2,1)} %all-gather.6.cloned.1.call-done, ...), kind=kOutput, calls=%fused_computation.95 | convolution fusion | flops 413171712 | bytes 10958853 | tf_op jit(solution)/shard_map/dot_general | solution.py:287
  393.3 3.1 collective-permute-start.23
  398.3 3.2 collective-permute-start.25
  401.6 8.5 %collective-permute-done.25 = bf16[3,256,128]{2,1,0:T(8,128)(2,1)S(1)} collective-permute-done((bf16[3,256,128]{2,1,0:T(8,128)(2,1)S(1)}, bf16[3,256,128]{2,1,0:T(8,128)(2,1)S(1)}, u32[]{:S(2)}, u32[]{:S(2)}) %collective-permute-start.25) | collective-permute-done | bytes 196640 | tf_op jit(solution)/shard_map/ppermute | solution.py:20
  (295 shorter events, 119.3 us)
Async XLA Ops:
  7.2 82.5 %copy-start = (bf16[2048,160]{0,1:T(8,128)(2,1)S(1)}, bf16[2048,160]{0,1:T(8,128)(2,1)}, u32[]{:S(2)}) copy-start(bf16[2048,160]{0,1:T(8,128)(2,1)} %param.26) | copy-start | bytes 1966084
  7.2 18.5 %copy-start.14 = (f32[128,256]{1,0:T(8,128)S(1)}, f32[128,256]{1,0:T(8,128)}, u32[]{:S(2)}) copy-start(f32[128,256]{1,0:T(8,128)} %param.23) | copy-start | bytes 393220
  7.2 18.6 %copy-start.11 = (f32[5,256,128]{2,1,0:T(8,128)S(1)}, f32[5,256,128]{2,1,0:T(8,128)}, u32[]{:S(2)}) copy-start(f32[5,256,128]{2,1,0:T(8,128)} %param.21) | copy-start | bytes 1966084
  7.2 68.5 %all-gather.4.cloned.1.call-start = ((), (), s32[]{:S(2)}) async-start(), calls=%async_computation | async-start | bytes 3377152 | tf_op jit(solution)/shard_map/all_gather | solution.py:162
  8.3 21.6 %copy-start.17 = (f32[8,2048]{1,0:T(8,128)S(1)}, f32[8,2048]{1,0:T(8,128)}, u32[]{:S(2)}) copy-start(f32[8,2048]{1,0:T(8,128)} %param.25) | copy-start | bytes 196612
  21.3 100.3 %all-gather.6.cloned.1.call-start = ((), (), s32[]{:S(2)}) async-start(), calls=%async_computation.1 | async-start | bytes 3538944 | tf_op jit(solution)/shard_map/all_gather | solution.py:173
  81.2 235.5 %all-gather.8.cloned.1.call-start = ((), (), s32[]{:S(2)}) async-start(), calls=%async_computation.2 | async-start | bytes 4128768 | tf_op jit(solution)/shard_map/all_gather | solution.py:175
  92.2 23.9 %copy-start.15 = (bf16[768,160]{0,1:T(8,128)(2,1)}, bf16[768,160]{0,1:T(8,128)(2,1)S(1)}, u32[]{:S(2)}) copy-start(bf16[768,160]{0,1:T(8,128)(2,1)S(1)} %fusion.28) | copy-start | bytes 737284
  135.5 23.4 %copy-start.23 = (f32[6,2,64]{2,1,0:T(2,128)S(1)}, f32[6,2,64]{2,1,0:T(2,128)}, u32[]{:S(2)}) copy-start(f32[6,2,64]{2,1,0:T(2,128)} %copy-done.22) | copy-start | bytes 9220
  135.6 13.7 %collective-permute-start.6 = (f32[2,65,64]{1,2,0:T(8,128)S(1)}, f32[2,65,64]{1,2,0:T(8,128)S(1)}, u32[]{:S(2)}, u32[]{:S(2)}) collective-permute-start(f32[2,65,64]{1,2,0:T(8,128)S(1)} %pad_maximum_fusion.5), channel_id=1, source_target_pairs={{0,112},{1,113},{2,114},{3,115},{4,116},{5,117},{6,118},{7,119},{8... | collective-permute-start | bytes 99848 | tf_op jit(solution)/shard_map/ppermute | solution.py:20
  136.2 16.3 %collective-permute-start.5 = (f32[2,65,64]{1,2,0:T(8,128)S(1)}, f32[2,65,64]{1,2,0:T(8,128)S(1)}, u32[]{:S(2)}, u32[]{:S(2)}) collective-permute-start(f32[2,65,64]{1,2,0:T(8,128)S(1)} %pad_maximum_fusion.5), channel_id=1, source_target_pairs={{0,96},{16,112},{1,97},{17,113},{2,98},{18,114},{3,99},{19,115},{4... | collective-permute-start | bytes 99848 | tf_op jit(solution)/shard_map/ppermute | solution.py:20
  141.7 14.3 %collective-permute-start.4 = (f32[2,65,64]{1,2,0:T(8,128)S(1)}, f32[2,65,64]{1,2,0:T(8,128)S(1)}, u32[]{:S(2)}, u32[]{:S(2)}) collective-permute-start(f32[2,65,64]{1,2,0:T(8,128)S(1)} %pad_maximum_fusion.5), channel_id=1, source_target_pairs={{0,80},{16,96},{32,112},{1,81},{17,97},{33,113},{2,82},{18,98},{34... | collective-permute-start | bytes 99848 | tf_op jit(solution)/shard_map/ppermute | solution.py:20
  143.0 13.2 %collective-permute-start.3 = (f32[2,65,64]{1,2,0:T(8,128)S(1)}, f32[2,65,64]{1,2,0:T(8,128)S(1)}, u32[]{:S(2)}, u32[]{:S(2)}) collective-permute-start(f32[2,65,64]{1,2,0:T(8,128)S(1)} %pad_maximum_fusion.5), channel_id=1, source_target_pairs={{0,64},{16,80},{32,96},{48,112},{1,65},{17,81},{33,97},{49,113},{2... | collective-permute-start | bytes 99848 | tf_op jit(solution)/shard_map/ppermute | solution.py:20
  144.3 12.0 %collective-permute-start.2 = (f32[2,65,64]{1,2,0:T(8,128)S(1)}, f32[2,65,64]{1,2,0:T(8,128)S(1)}, u32[]{:S(2)}, u32[]{:S(2)}) collective-permute-start(f32[2,65,64]{1,2,0:T(8,128)S(1)} %pad_maximum_fusion.5), channel_id=1, source_target_pairs={{0,48},{16,64},{32,80},{48,96},{64,112},{1,49},{17,65},{33,81},{49... | collective-permute-start | bytes 99848 | tf_op jit(solution)/shard_map/ppermute | solution.py:20
  149.2 7.3 %collective-permute-start.1 = (f32[2,65,64]{1,2,0:T(8,128)S(1)}, f32[2,65,64]{1,2,0:T(8,128)S(1)}, u32[]{:S(2)}, u32[]{:S(2)}) collective-permute-start(f32[2,65,64]{1,2,0:T(8,128)S(1)} %pad_maximum_fusion.5), channel_id=1, source_target_pairs={{0,32},{16,48},{32,64},{48,80},{64,96},{80,112},{1,33},{17,49},{33... | collective-permute-start | bytes 99848 | tf_op jit(solution)/shard_map/ppermute | solution.py:20
  152.5 6.2 %collective-permute-start = (f32[2,65,64]{1,2,0:T(8,128)S(1)}, f32[2,65,64]{1,2,0:T(8,128)S(1)}, u32[]{:S(2)}, u32[]{:S(2)}) collective-permute-start(f32[2,65,64]{1,2,0:T(8,128)S(1)} %pad_maximum_fusion.5), channel_id=1, source_target_pairs={{0,16},{16,32},{32,48},{48,64},{64,80},{80,96},{96,112},{1,17},{17... | collective-permute-start | bytes 99848 | tf_op jit(solution)/shard_map/ppermute | solution.py:20
  186.7 3.8 collective-permute-start.7
  192.5 25.7 %copy-start.12 = (f32[256,448]{0,1:T(8,128)S(1)}, f32[256,448]{0,1:T(8,128)}, u32[]{:S(2)}) copy-start(f32[256,448]{0,1:T(8,128)} %param.22) | copy-start | bytes 1376260
  192.5 33.9 %copy-start.13 = (f32[448,256]{1,0:T(8,128)S(1)}, f32[448,256]{1,0:T(8,128)}, u32[]{:S(2)}) copy-start(f32[448,256]{1,0:T(8,128)} %param.24) | copy-start | bytes 1376260
  192.7 12.9 %collective-permute-start.8 = (bf16[768,2,128]{2,0,1:T(8,128)(2,1)S(1)}, bf16[768,2,128]{2,0,1:T(8,128)(2,1)S(1)}, u32[]{:S(2)}, u32[]{:S(2)}) collective-permute-start(bf16[768,2,128]{2,0,1:T(8,128)(2,1)S(1)} %get-tuple-element.50), channel_id=1, source_target_pairs={{0,2},{1,3},{2,4},{3,5},{4,6},{5,7},{6,0},{7,1},{8,10},{9,11},{10,... | collective-permute-start | bytes 1179656 | tf_op jit(solution)/shard_map/ppermute | solution.py:35
  194.3 19.1 %collective-permute-start.10 = (bf16[768,2,128]{2,0,1:T(8,128)(2,1)S(1)}, bf16[768,2,128]{2,0,1:T(8,128)(2,1)S(1)}, u32[]{:S(2)}, u32[]{:S(2)}) collective-permute-start(bf16[768,2,128]{2,0,1:T(8,128)(2,1)S(1)} %get-tuple-element.51), channel_id=1, source_target_pairs={{0,6},{1,7},{2,0},{3,1},{4,2},{5,3},{6,4},{7,5},{8,14},{9,15},{10,... | collective-permute-start | bytes 1179656 | tf_op jit(solution)/shard_map/ppermute | solution.py:35
  196.0 19.2 %collective-permute-start.9 = (bf16[768,2,128]{2,0,1:T(8,128)(2,1)S(1)}, bf16[768,2,128]{2,0,1:T(8,128)(2,1)S(1)}, u32[]{:S(2)}, u32[]{:S(2)}) collective-permute-start(bf16[768,2,128]{2,0,1:T(8,128)(2,1)S(1)} %get-tuple-element.52), channel_id=1, source_target_pairs={{0,4},{1,5},{2,6},{3,7},{4,0},{5,1},{6,2},{7,3},{8,12},{9,13},{10,... | collective-permute-start | bytes 1179656 | tf_op jit(solution)/shard_map/ppermute | solution.py:35
  215.4 8.1 %collective-permute-start.11 = (bf16[768,128]{1,0:T(8,128)(2,1)S(1)}, bf16[768,128]{1,0:T(8,128)(2,1)S(1)}, u32[]{:S(2)}, u32[]{:S(2)}) collective-permute-start(bf16[768,128]{1,0:T(8,128)(2,1)S(1)} %select_bitcast_fusion.9), channel_id=1, source_target_pairs={{0,8},{1,9},{2,10},{3,11},{4,12},{5,13},{6,14},{7,15},{8,0},{9,1},... | collective-permute-start | bytes 589832 | tf_op jit(solution)/shard_map/ppermute | solution.py:25
  223.7 7.3 %collective-permute-start.12 = (bf16[768,128]{1,0:T(8,128)(2,1)S(1)}, bf16[768,128]{1,0:T(8,128)(2,1)S(1)}, u32[]{:S(2)}, u32[]{:S(2)}) collective-permute-start(bf16[768,128]{1,0:T(8,128)(2,1)S(1)} %fusion.37), channel_id=1, source_target_pairs={{0,8},{1,9},{2,10},{3,11},{4,12},{5,13},{6,14},{7,15},{8,0},{9,1},... | collective-permute-start | bytes 589832 | tf_op jit(solution)/shard_map/ppermute | solution.py:25
  231.0 18.8 %collective-permute-start.15 = (bf16[768,2,128]{2,0,1:T(8,128)(2,1)S(1)}, bf16[768,2,128]{2,0,1:T(8,128)(2,1)S(1)}, u32[]{:S(2)}, u32[]{:S(2)}) collective-permute-start(bf16[768,2,128]{2,0,1:T(8,128)(2,1)S(1)} %maximum_select_fusion.2), channel_id=1, source_target_pairs={{0,2},{1,3},{2,4},{3,5},{4,6},{5,7},{6,0},{7,1},{8,10},{9,11},{10,... | collective-permute-start | bytes 1179656 | tf_op jit(solution)/shard_map/ppermute | solution.py:35
  231.9 17.9 %collective-permute-start.14 = (bf16[768,2,128]{2,0,1:T(8,128)(2,1)S(1)}, bf16[768,2,128]{2,0,1:T(8,128)(2,1)S(1)}, u32[]{:S(2)}, u32[]{:S(2)}) collective-permute-start(bf16[768,2,128]{2,0,1:T(8,128)(2,1)S(1)} %maximum_select_fusion.2), channel_id=1, source_target_pairs={{0,4},{1,5},{2,6},{3,7},{4,0},{5,1},{6,2},{7,3},{8,12},{9,13},{10,... | collective-permute-start | bytes 1179656 | tf_op jit(solution)/shard_map/ppermute | solution.py:35
  233.8 16.6 %collective-permute-start.13 = (bf16[768,2,128]{2,0,1:T(8,128)(2,1)S(1)}, bf16[768,2,128]{2,0,1:T(8,128)(2,1)S(1)}, u32[]{:S(2)}, u32[]{:S(2)}) collective-permute-start(bf16[768,2,128]{2,0,1:T(8,128)(2,1)S(1)} %maximum_select_fusion.2), channel_id=1, source_target_pairs={{0,6},{1,7},{2,0},{3,1},{4,2},{5,3},{6,4},{7,5},{8,14},{9,15},{10,... | collective-permute-start | bytes 1179656 | tf_op jit(solution)/shard_map/ppermute | solution.py:35
  255.4 20.9 %collective-permute-start.16 = (bf16[768,2,4,128]{3,0,1,2:T(8,128)(2,1)}, bf16[768,2,4,128]{3,0,1,2:T(8,128)(2,1)}, u32[]{:S(2)}, u32[]{:S(2)}) collective-permute-start(bf16[768,2,4,128]{3,0,1,2:T(8,128)(2,1)} %bitcast_select_fusion.1), channel_id=1, source_target_pairs={{0,1},{1,0},{2,3},{3,2},{4,5},{5,4},{6,7},{7,6},{8,9},{9,8},{10,11... | collective-permute-start | bytes 4718600 | tf_op jit(solution)/shard_map/ppermute | solution.py:25
  258.2 12.7 %collective-permute-start.27 = (f32[3,2,4096]{2,1,0:T(2,128)S(1)}, f32[3,2,4096]{2,1,0:T(2,128)S(1)}, u32[]{:S(2)}, u32[]{:S(2)}) collective-permute-start(f32[3,2,4096]{2,1,0:T(2,128)S(1)} %reshape.651), channel_id=1, source_target_pairs={{0,32},{16,48},{32,64},{48,80},{64,96},{80,112},{1,33},{17,49},{33... | collective-permute-start | bytes 294920 | tf_op jit(solution)/shard_map/ppermute | solution.py:20
  261.0 82.6 %collective-permute-start.30 = (f32[3,2,4096]{2,1,0:T(2,128)S(1)}, f32[3,2,4096]{2,1,0:T(2,128)S(1)}, u32[]{:S(2)}, u32[]{:S(2)}) collective-permute-start(f32[3,2,4096]{2,1,0:T(2,128)S(1)} %reshape.651), channel_id=1, source_target_pairs={{32,0},{48,16},{64,32},{80,48},{96,64},{112,80},{33,1},{49,17},{65... | collective-permute-start | bytes 294920 | tf_op jit(solution)/shard_map/ppermute | solution.py:20
  262.3 81.3 %collective-permute-start.29 = (f32[3,2,4096]{2,1,0:T(2,128)S(1)}, f32[3,2,4096]{2,1,0:T(2,128)S(1)}, u32[]{:S(2)}, u32[]{:S(2)}) collective-permute-start(f32[3,2,4096]{2,1,0:T(2,128)S(1)} %reshape.651), channel_id=1, source_target_pairs={{16,0},{32,16},{48,32},{64,48},{80,64},{96,80},{112,96},{17,1},{33... | collective-permute-start | bytes 294920 | tf_op jit(solution)/shard_map/ppermute | solution.py:20
  266.8 9.3 %collective-permute-start.28 = (f32[3,2,4096]{2,1,0:T(2,128)S(1)}, f32[3,2,4096]{2,1,0:T(2,128)S(1)}, u32[]{:S(2)}, u32[]{:S(2)}) collective-permute-start(f32[3,2,4096]{2,1,0:T(2,128)S(1)} %reshape.651), channel_id=1, source_target_pairs={{0,16},{16,32},{32,48},{48,64},{64,80},{80,96},{96,112},{1,17},{17... | collective-permute-start | bytes 294920 | tf_op jit(solution)/shard_map/ppermute | solution.py:20
  299.3 7.5 %collective-permute-start.17 = (bf16[1,2048]{1,0:T(2,128)(2,1)S(1)}, bf16[1,2048]{1,0:T(2,128)(2,1)S(1)}, u32[]{:S(2)}, u32[]{:S(2)}) collective-permute-start(bf16[1,2048]{1,0:T(2,128)(2,1)S(1)} %slice.439), channel_id=1, source_target_pairs={{0,16},{16,32},{32,48},{48,64},{64,80},{80,96},{96,112},{1,17},{17... | collective-permute-start | bytes 12296 | tf_op jit(solution)/shard_map/ppermute | solution.py:20
  343.5 9.2 %collective-permute-start.18 = (bf16[768,2,4,128]{3,0,1,2:T(8,128)(2,1)}, bf16[768,2,4,128]{3,0,1,2:T(8,128)(2,1)}, u32[]{:S(2)}, u32[]{:S(2)}) collective-permute-start(bf16[768,2,4,128]{3,0,1,2:T(8,128)(2,1)} %select_bitcast_fusion), channel_id=1, source_target_pairs={{0,1},{1,0},{2,3},{3,2},{4,5},{5,4},{6,7},{7,6},{8,9},{9,8},{10,11... | collective-permute-start | bytes 4718600 | tf_op jit(solution)/shard_map/ppermute | solution.py:25
  345.3 15.5 %collective-permute-start.31 = (f32[3,2,128]{2,1,0:T(2,128)S(1)}, f32[3,2,128]{2,1,0:T(2,128)S(1)}, u32[]{:S(2)}, u32[]{:S(2)}) collective-permute-start(f32[3,2,128]{2,1,0:T(2,128)S(1)} %pad_maximum_fusion.6), channel_id=1, source_target_pairs={{0,32},{16,48},{32,64},{48,80},{64,96},{80,112},{1,33},{17,49},{33... | collective-permute-start | bytes 9224 | tf_op jit(solution)/shard_map/ppermute | solution.py:20
  354.7 30.6 %copy-start.19 = (f32[1,2048]{1,0:T(1,128)S(1)}, f32[1,2048]{1,0:T(1,128)}, u32[]{:S(2)}) copy-start(f32[1,2048]{1,0:T(1,128)} %get-tuple-element.56) | copy-start | bytes 24580
  354.9 13.4 %collective-permute-start.19 = (bf16[768,2,128]{2,0,1:T(8,128)(2,1)S(1)}, bf16[768,2,128]{2,0,1:T(8,128)(2,1)S(1)}, u32[]{:S(2)}, u32[]{:S(2)}) collective-permute-start(bf16[768,2,128]{2,0,1:T(8,128)(2,1)S(1)} %get-tuple-element.47), channel_id=1, source_target_pairs={{0,2},{1,3},{2,4},{3,5},{4,6},{5,7},{6,0},{7,1},{8,10},{9,11},{10,... | collective-permute-start | bytes 1179656 | tf_op jit(solution)/shard_map/ppermute | solution.py:35
  355.3 20.3 %collective-permute-start.21 = (bf16[768,2,128]{2,0,1:T(8,128)(2,1)S(1)}, bf16[768,2,128]{2,0,1:T(8,128)(2,1)S(1)}, u32[]{:S(2)}, u32[]{:S(2)}) collective-permute-start(bf16[768,2,128]{2,0,1:T(8,128)(2,1)S(1)} %get-tuple-element.48), channel_id=1, source_target_pairs={{0,6},{1,7},{2,0},{3,1},{4,2},{5,3},{6,4},{7,5},{8,14},{9,15},{10,... | collective-permute-start | bytes 1179656 | tf_op jit(solution)/shard_map/ppermute | solution.py:35
  358.2 18.6 %collective-permute-start.20 = (bf16[768,2,128]{2,0,1:T(8,128)(2,1)S(1)}, bf16[768,2,128]{2,0,1:T(8,128)(2,1)S(1)}, u32[]{:S(2)}, u32[]{:S(2)}) collective-permute-start(bf16[768,2,128]{2,0,1:T(8,128)(2,1)S(1)} %get-tuple-element.49), channel_id=1, source_target_pairs={{0,4},{1,5},{2,6},{3,7},{4,0},{5,1},{6,2},{7,3},{8,12},{9,13},{10,... | collective-permute-start | bytes 1179656 | tf_op jit(solution)/shard_map/ppermute | solution.py:35
  359.5 20.4 %collective-permute-start.34 = (f32[3,2,128]{2,1,0:T(2,128)S(1)}, f32[3,2,128]{2,1,0:T(2,128)S(1)}, u32[]{:S(2)}, u32[]{:S(2)}) collective-permute-start(f32[3,2,128]{2,1,0:T(2,128)S(1)} %pad_maximum_fusion.6), channel_id=1, source_target_pairs={{32,0},{48,16},{64,32},{80,48},{96,64},{112,80},{33,1},{49,17},{65... | collective-permute-start | bytes 9224 | tf_op jit(solution)/shard_map/ppermute | solution.py:20
  360.8 5.5 %collective-permute-start.32 = (f32[3,2,128]{2,1,0:T(2,128)S(1)}, f32[3,2,128]{2,1,0:T(2,128)S(1)}, u32[]{:S(2)}, u32[]{:S(2)}) collective-permute-start(f32[3,2,128]{2,1,0:T(2,128)S(1)} %pad_maximum_fusion.6), channel_id=1, source_target_pairs={{0,16},{16,32},{32,48},{48,64},{64,80},{80,96},{96,112},{1,17},{17... | collective-permute-start | bytes 9224 | tf_op jit(solution)/shard_map/ppermute | solution.py:20
  366.3 13.6 %collective-permute-start.33 = (f32[3,2,128]{2,1,0:T(2,128)S(1)}, f32[3,2,128]{2,1,0:T(2,128)S(1)}, u32[]{:S(2)}, u32[]{:S(2)}) collective-permute-start(f32[3,2,128]{2,1,0:T(2,128)S(1)} %pad_maximum_fusion.6), channel_id=1, source_target_pairs={{16,0},{32,16},{48,32},{64,48},{80,64},{96,80},{112,96},{17,1},{33... | collective-permute-start | bytes 9224 | tf_op jit(solution)/shard_map/ppermute | solution.py:20
  377.1 8.2 %collective-permute-start.22 = (bf16[768,128]{1,0:T(8,128)(2,1)S(1)}, bf16[768,128]{1,0:T(8,128)(2,1)S(1)}, u32[]{:S(2)}, u32[]{:S(2)}) collective-permute-start(bf16[768,128]{1,0:T(8,128)(2,1)S(1)} %select_bitcast_fusion.8), channel_id=1, source_target_pairs={{0,8},{1,9},{2,10},{3,11},{4,12},{5,13},{6,14},{7,15},{8,0},{9,1},... | collective-permute-start | bytes 589832 | tf_op jit(solution)/shard_map/ppermute | solution.py:25
  385.3 26.5 %copy-start.1 = (bf16[2048,160]{0,1:T(8,128)(2,1)S(1)}, bf16[2048,160]{0,1:T(8,128)(2,1)}, u32[]{:S(2)}) copy-start(bf16[2048,160]{0,1:T(8,128)(2,1)} %param.26) | copy-start | bytes 1966084
  390.6 10.9 %collective-permute-start.24 = (bf16[3,256,128]{2,1,0:T(8,128)(2,1)S(1)}, bf16[3,256,128]{2,1,0:T(8,128)(2,1)S(1)}, u32[]{:S(2)}, u32[]{:S(2)}) collective-permute-start(bf16[3,256,128]{2,1,0:T(8,128)(2,1)S(1)} %bitcast.304), channel_id=1, source_target_pairs={{0,16},{16,32},{32,48},{48,64},{64,80},{80,96},{96,112},{1,17},{17... | collective-permute-start | bytes 589832 | tf_op jit(solution)/shard_map/ppermute | solution.py:20
  393.3 8.2 %collective-permute-start.23 = (bf16[3,256,128]{2,1,0:T(8,128)(2,1)S(1)}, bf16[3,256,128]{2,1,0:T(8,128)(2,1)S(1)}, u32[]{:S(2)}, u32[]{:S(2)}) collective-permute-start(bf16[3,256,128]{2,1,0:T(8,128)(2,1)S(1)} %bitcast.305), channel_id=1, source_target_pairs={{0,32},{16,48},{32,64},{48,80},{64,96},{80,112},{1,33},{17,49},{33... | collective-permute-start | bytes 589832 | tf_op jit(solution)/shard_map/ppermute | solution.py:20
  397.0 13.1 %collective-permute-start.26 = (bf16[3,256,128]{2,1,0:T(8,128)(2,1)S(1)}, bf16[3,256,128]{2,1,0:T(8,128)(2,1)S(1)}, u32[]{:S(2)}, u32[]{:S(2)}) collective-permute-start(bf16[3,256,128]{2,1,0:T(8,128)(2,1)S(1)} %bitcast.306), channel_id=1, source_target_pairs={{32,0},{48,16},{64,32},{80,48},{96,64},{112,80},{33,1},{49,17},{65... | collective-permute-start | bytes 589832 | tf_op jit(solution)/shard_map/ppermute | solution.py:20
  398.3 11.8 %collective-permute-start.25 = (bf16[3,256,128]{2,1,0:T(8,128)(2,1)S(1)}, bf16[3,256,128]{2,1,0:T(8,128)(2,1)S(1)}, u32[]{:S(2)}, u32[]{:S(2)}) collective-permute-start(bf16[3,256,128]{2,1,0:T(8,128)(2,1)S(1)} %bitcast.307), channel_id=1, source_target_pairs={{16,0},{32,16},{48,32},{64,48},{80,64},{96,80},{112,96},{17,1},{33... | collective-permute-start | bytes 589832 | tf_op jit(solution)/shard_map/ppermute | solution.py:20
  (21 other events, 108.4 us)
Sparse Core Ops, SparseCore 0:
  21.5 54.1 all-gather.3
  81.3 40.2 all-gather.5
  235.7 62.7 all-gather.7

commit v5 on v4

--- a/solution.py
+++ b/solution.py
@@ -162,19 +162,23 @@
     gathered_rows = lax.all_gather(own_rows, "head", axis=1, tiled=True)
     embedded = gathered_rows[:slot_rows]
     edge_rows = gathered_rows[slot_rows : slot_rows + held]
-    map_count = joined_linear_maps.shape[0]
-    first_pack = jnp.concatenate(
-        [joined_linear_maps, timeblend_result_map.T[None]], axis=0
-    ).astype(jnp.bfloat16)
+    first_pack = joined_linear_maps.astype(jnp.bfloat16)
     second_pack = jnp.stack(
         [feedforward_lookup_map, feedforward_content_map.T], axis=0
     ).astype(jnp.bfloat16)
     first_pack, _ = lax.optimization_barrier((first_pack, gathered_rows))
     first_full = lax.all_gather(first_pack, "group", axis=1, tiled=True)
-    second_pack, _ = lax.optimization_barrier((second_pack, first_full))
+    output_pack, _ = lax.optimization_barrier((timeblend_result_map.astype(jnp.bfloat16), first_full))
+    output_pieces = lax.all_gather(output_pack, ("group", "head"), axis=0, tiled=False)
+    output_rows, output_cols = timeblend_result_map.shape
+    output_weight = (
+        output_pieces.reshape(group_count, -1, output_rows, output_cols)
+        .transpose(1, 2, 0, 3)
+        .reshape(-1, group_count * output_cols)
+    )
+    second_pack, _ = lax.optimization_barrier((second_pack, output_pieces))
     second_full = lax.all_gather(second_pack, "group", axis=1, tiled=True)
-    projections = first_full[:map_count]
-    output_weight_t = first_full[map_count]
+    projections = first_full
     key_weight = second_full[0]
     value_weight_t = second_full[1]
     current = layer_norm(embedded)
@@ -264,11 +268,8 @@
     page_end = page_end + page_factor[:, :, :, None] * incoming[None]
     attended = block_out.transpose(0, 2, 1, 3).reshape(slot_rows, features_on_shard)
     normed = (group_norm(attended) * attender_scaling_coefs * gating).astype(jnp.bfloat16)
-    mixer_partial = lax.dot_general(
-        normed, output_weight_t, (((1,), (1,)), ((), ())), preferred_element_type=jnp.float32
-    ).astype(jnp.bfloat16)
-    mixer_owned = hier_reduce_scatter(mixer_partial, "head").astype(jnp.bfloat16)
-    mixer_total = hier_all_gather(mixer_owned, "head").astype(jnp.float32)
+    normed_full = hier_all_gather(normed, "head")
+    mixer_total = jnp.dot(normed_full, output_weight, preferred_element_type=jnp.float32)
     residual = (embedded.astype(jnp.float32) + mixer_total).astype(jnp.bfloat16)
     last_residual = residual[slot_rows - 1 : slot_rows]
     arriving = passed_along(last_residual, "group", 1)

time: 425 us -> 491 us (1.16)
  waiting for transfers between devices: 121 us -> 197 us
  matrix products: 63.1 us -> 73.6 us
  other arithmetic: 62.4 us -> 54.2 us
  starting transfers between devices: 77.9 us -> 70 us
    all_gather x0 -> x1, waiting for transfers between devices: none -> 56.6 us  [per_device(): lax.all_gather(output_pack, ('group', 'head'), axis=0, tiled=False)]
    all_gather x1, waiting for transfers between devices: 0.83 us -> 38.1 us  [per_device(): first_full = lax.all_gather(first_pack, 'group', axis=1, tiled=True)]
    ppermute x9 -> x6, waiting for transfers between devices: 39.3 us -> 20.5 us  [_ring(): return lax.ppermute(value, axis, pairs)]
    convert_element_type x3 -> x0, local copies, waits for them, and re-layouts: 18 us -> none  [the longest x2 13.3 us: per_device(): mixer_total = hier_all_gather(mixer_owned, 'head').astype(jnp.float32)]
    reshape x0 -> x1, local copies, waits for them, and re-layouts: none -> 12.3 us  [per_device(): output_pieces.reshape(group_count, -1, output_rows, output_cols)]
    all_gather x1, waiting for transfers between devices: 0.01 us -> 10.1 us  [per_device(): second_full = lax.all_gather(second_pack, 'group', axis=1, tiled=True)]
    ppermute x6 -> x4, waiting for transfers between devices: 18.2 us -> 8.67 us  [_swap(): return lax.ppermute(value, axis, [(s, s ^ flip) for s in range(count)])]
    all_gather x1, waiting for transfers between devices: 45.1 us -> 52.4 us  [per_device(): gathered_rows = lax.all_gather(own_rows, 'head', axis=1, tiled=True)]
  transfers between devices with their start and end apart: 38 -> 34, of which waited for: 17 -> 14; matrix products, arithmetic and copies ran while one was open for 30% -> 36% of each run, Pallas kernels for 0% -> 0%
where the time goes in v5:
time: 491 us; the launch traced here: 487 us
  waiting for transfers between devices  197 us (40%)
  local copies, waits for them, and re-layouts  74.7 us (15%)
  matrix products  73.6 us (15%)
  starting transfers between devices  70 us (14%)
  other arithmetic  54.2 us (11%)
  between operations  17.6 us (4%)
    all_gather x1, waiting for transfers between devices, per_device(): lax.all_gather(output_pack, ('group', 'head'), axis=0, tiled=False)  56.6 us
    ppermute x20, starting transfers between devices, passed_along(): lax.ppermute(value, axis, [(source, source + steps) for source in range(i...  54.8 us
    all_gather x1, waiting for transfers between devices, per_device(): gathered_rows = lax.all_gather(own_rows, 'head', axis=1, tiled=True)  52.4 us
    all_gather x1, waiting for transfers between devices, per_device(): first_full = lax.all_gather(first_pack, 'group', axis=1, tiled=True)  38.1 us
    unnamed x89, local copies, waits for them, and re-layouts  21.2 us
    ppermute x6, waiting for transfers between devices, _ring(): return lax.ppermute(value, axis, pairs)  20.5 us
    dot_general x3, matrix products, mixed_inputs(): jnp.dot(column_part, blend_widening_maps[number], preferred_element_type=...  18.1 us
    reshape x1, local copies, waits for them, and re-layouts, per_device(): output_pieces.reshape(group_count, -1, output_rows, output_cols)  12.3 us
  transfers between devices with their start and end apart: 34, of which 14 were waited for; matrix products, arithmetic and copies ran while one was open for 36% of the time, Pallas kernels for 0%

profile of v5, /device:TPU:2, one launch (start us, length us, event | category | flops | bytes accessed | tf_op | source)
XLA Modules:
  0.0 487.5 jit_solution(687753315220276661)
XLA Ops:
  10.5 9.8 %gather_fusion.2 = bf16[776,128]{1,0:T(8,128)(2,1)S(1)} fusion(bf16[65536,128]{1,0:T(8,128)(2,1)} %param.20, s32[1024]{0:T(1024)S(1)} %pad_clamp_fusion.3), kind=kCustom, calls=%fused_computation.4 | custom fusion | bytes 400416 | tf_op jit(solution)/shard_map/jit(_take)/gather | solution.py:161
  23.2 52.4 %all-gather.6.cloned.1.call-done = bf16[776,2048]{1,0:T(8,128)(2,1)} async-done(((bf16[776,128]{1,0:T(8,128)(2,1)}), bf16[776,2048]{1,0:T(8,128)(2,1)}) %all-gather.6.cloned.1.call-update) | async-done | bytes 3178512 | tf_op jit(solution)/shard_map/all_gather | solution.py:162
  77.3 38.1 %all-gather.8.cloned.1.call-done = bf16[5,2048,128]{2,1,0:T(8,128)(2,1)} async-done(((bf16[5,256,128]{2,1,0:T(8,128)(2,1)}), bf16[5,2048,128]{2,1,0:T(8,128)(2,1)}) %all-gather.8.cloned.1.call-update) | async-done | bytes 2621456 | tf_op jit(solution)/shard_map/all_gather | solution.py:170
  129.1 2.8 fusion.4
  140.0 6.2 %fusion.30 = bf16[768,64]{0,1:T(8,128)(2,1)S(1)} fusion(bf16[2048,64]{0,1:T(8,128)(2,1)S(1)} %copy-done.30, f32[768,2048]{1,0:T(8,128)} %copy-done.4, f32[2048]{0:T(1024)S(1)} %bitcast.301, f32[768]{0:T(1024)S(1)} %add_rsqrt_fusion.1, f32[768]{0:T(1024)S(1)} %broadcast_multiply_fusion.2, bf16[5,32,2048]{2,1,0:T(8,128)(2,1)} %param.27, ...), kind=kOutput, calls=%fused_computation.72 | convolution fusion | flops 313049088 | bytes 9994240 | tf_op jit(solution)/shard_map/dot_general | solution.py:104
  152.4 7.1 %add_convert_fusion.3 = bf16[768,2048]{1,0:T(8,128)(2,1)} fusion(f32[768,2048]{1,0:T(8,128)} %copy-done.4, f32[2048]{0:T(1024)S(1)} %bitcast.295, f32[768]{0:T(1024)S(1)} %add_rsqrt_fusion.1, f32[768]{0:T(1024)S(1)} %broadcast_multiply_fusion.2, bf16[5,32,2048]{2,1,0:T(8,128)(2,1)} %param.27, bf16[768,160]{0,1:T(8,128)(2,1)} %copy-done.11, ...), kind=kOutput, calls=%fused_computation.28 | convolution fusion | flops 111673344 | bytes 12777472 | tf_op jit(solution)/shard_map/dot_general | solution.py:93
  159.6 6.4 %add_convert_fusion.4 = bf16[768,2048]{1,0:T(8,128)(2,1)} fusion(f32[768,2048]{1,0:T(8,128)} %copy-done.4, f32[2048]{0:T(1024)S(1)} %bitcast.294, f32[768]{0:T(1024)S(1)} %add_rsqrt_fusion.1, f32[768]{0:T(1024)S(1)} %broadcast_multiply_fusion.2, bf16[5,32,2048]{2,1,0:T(8,128)(2,1)} %param.27, bf16[768,160]{0,1:T(8,128)(2,1)} %copy-done.11, ...), kind=kOutput, calls=%fused_computation.29 | convolution fusion | flops 111673344 | bytes 12777472 | tf_op jit(solution)/shard_map/dot_general | solution.py:93
  166.0 4.5 add_convert_fusion.6
  171.3 3.1 fusion.106
  174.5 3.2 convolution_bitcast_fusion.4
  177.7 3.1 multiply_reduce_fusion.1
  185.7 5.4 %collective-permute-start.5 = (f32[2,65,64]{1,2,0:T(8,128)S(1)}, f32[2,65,64]{1,2,0:T(8,128)S(1)}, u32[]{:S(2)}, u32[]{:S(2)}) collective-permute-start(f32[2,65,64]{1,2,0:T(8,128)S(1)} %pad_maximum_fusion.4), channel_id=1, source_target_pairs={{0,96},{16,112},{1,97},{17,113},{2,98},{18,114},{3,99},{19,115},{4... | collective-permute-start | bytes 99848 | tf_op jit(solution)/shard_map/ppermute | solution.py:20
  199.0 3.1 collective-permute-start.1
  202.3 3.4 collective-permute-start
  211.0 6.0 %multiply_convert_fusion = bf16[768,128]{1,0:T(8,128)(2,1)S(1)} fusion(bf16[5,2048,128]{2,1,0:T(8,128)(2,1)} %all-gather.8.cloned.1.call-done, f32[768,2048]{1,0:T(8,128)} %copy-done.4, f32[2048]{0:T(1024)S(1)} %bitcast.300, f32[768]{0:T(1024)S(1)} %add_rsqrt_fusion.1, f32[768]{0:T(1024)S(1)} %broadcast_multiply_fusion.2, f32[768,128]{1,0:T(8,128)S(1)} %copy.90, ...), kind=kOutput, calls=%fused_computation.97 | convolution fusion | flops 515211264 | bytes 11532800 | tf_op jit(solution)/shard_map/dot_general | solution.py:199
  217.0 2.7 collective-permute-start.7
  220.4 3.9 collective-permute-done.7
  224.3 3.1 collective-permute-start.8
  229.6 7.5 %collective-permute-done.8 = bf16[768,2,128]{2,0,1:T(8,128)(2,1)S(1)} collective-permute-done((bf16[768,2,128]{2,0,1:T(8,128)(2,1)S(1)}, bf16[768,2,128]{2,0,1:T(8,128)(2,1)S(1)}, u32[]{:S(2)}, u32[]{:S(2)}) %collective-permute-start.8) | collective-permute-done | bytes 393248 | tf_op jit(solution)/shard_map/ppermute | solution.py:35
  237.1 3.8 collective-permute-done.10
  248.8 4.2 collective-permute-start.22
  253.1 6.3 %collective-permute-start.23 = (f32[3,2,4096]{2,1,0:T(2,128)S(1)}, f32[3,2,4096]{2,1,0:T(2,128)S(1)}, u32[]{:S(2)}, u32[]{:S(2)}) collective-permute-start(f32[3,2,4096]{2,1,0:T(2,128)S(1)} %reshape.649), channel_id=1, source_target_pairs={{0,16},{16,32},{32,48},{48,64},{64,80},{80,96},{96,112},{1,17},{17... | collective-permute-start | bytes 294920 | tf_op jit(solution)/shard_map/ppermute | solution.py:20
  263.1 3.8 maximum_select_fusion
  266.9 4.7 copy.91
  271.5 56.6 %all-gather.12.cloned.1.call-done = bf16[16384,256]{1,0:T(8,128)(2,1)} async-done(((bf16[128,256]{1,0:T(8,128)(2,1)}), bf16[16384,256]{1,0:T(8,128)(2,1)}) %all-gather.12.cloned.1.call-update) | async-done | bytes 8388624 | tf_op jit(solution)/shard_map/all_gather | solution.py:172
  328.1 12.3 %copy.92 = bf16[8,16,128,256]{3,0,2,1:T(8,128)(2,1)} copy(bf16[8,16,128,256]{3,2,1,0:T(8,128)(2,1)} %bitcast.270) | data formatting | bytes 16777216 | tf_op jit(solution)/shard_map/reshape | solution.py:175
  340.5 10.5 %copy.108 = bf16[256,8,8,256]{3,1,2,0:T(8,128)(2,1)} copy(bf16[256,8,8,256]{3,2,1,0:T(8,128)(2,1)} %bitcast.260) | data formatting | bytes 16777216
  351.0 10.3 %convert_reduce_fusion.1 = (f32[768]{0:T(1024)S(1)}, bf16[768,2048]{1,0:T(8,128)(2,1)S(1)}) fusion(bf16[768,2048]{0,1:T(8,128)(2,1)S(1)} %bitcast.272, bf16[2048,2048]{1,0:T(8,128)(2,1)} %bitcast.271, bf16[776,2048]{1,0:T(8,128)(2,1)} %all-gather.6.cloned.1.call-done), kind=kOutput, calls=%fused_computation.13 | convolution fusion | flops 6450314240 | bytes 17828864 | tf_op jit(solution)/shard_map/dot_general | solution.py:272
  370.3 3.7 pad_maximum_fusion.1
  374.1 3.6 bitcast_subtract_fusion
  377.7 10.1 %all-gather.10.cloned.1.call-done = bf16[2,2048,448]{1,2,0:T(8,128)(2,1)} async-done(((bf16[2,256,448]{1,2,0:T(8,128)(2,1)}), bf16[2,2048,448]{1,2,0:T(8,128)(2,1)}) %all-gather.10.cloned.1.call-update) | async-done | bytes 3670032 | tf_op jit(solution)/shard_map/all_gather | solution.py:180
  387.8 11.0 %convolution_convert_fusion = bf16[768,2048]{1,0:T(8,128)(2,1)} fusion(bf16[2,2048,448]{1,2,0:T(8,128)(2,1)} %all-gather.10.cloned.1.call-done, f32[768,2048]{1,0:T(8,128)} %bitcast_subtract_fusion, f32[2048]{0:T(1024)S(1)} %bitcast.299, bf16[768,2048]{1,0:T(8,128)(2,1)} %copy-done.5, f32[768]{0:T(1024)S(1)} %add_rsqrt_fusion, ...), kind=kOutput, calls=%fused_computation.33 | convolution fusion | flops 2830614528 | bytes 16267264 | tf_op jit(solution)/shard_map/dot_general | solution.py:292
  398.8 4.9 copy.93
  403.6 3.8 fusion.101
  409.4 2.6 copy.106
  412.0 2.7 select_bitcast_fusion
  416.4 4.5 collective-permute-start.26
  423.8 3.2 collective-permute-start.15
  430.7 3.9 collective-permute-start.28
  436.1 9.0 %collective-permute-done.15 = bf16[768,2,128]{2,0,1:T(8,128)(2,1)S(1)} collective-permute-done((bf16[768,2,128]{2,0,1:T(8,128)(2,1)S(1)}, bf16[768,2,128]{2,0,1:T(8,128)(2,1)S(1)}, u32[]{:S(2)}, u32[]{:S(2)}) %collective-permute-start.15) | collective-permute-done | bytes 393248 | tf_op jit(solution)/shard_map/ppermute | solution.py:35
  445.5 2.8 collective-permute-start.17
  448.9 4.8 collective-permute-done.17
  453.7 5.3 %fusion.34 = bf16[768,128]{1,0:T(8,128)(2,1)S(1)} fusion(bf16[768,128]{1,0:T(8,128)(2,1)S(1)} %collective-permute-done.17, bf16[768,2048]{1,0:T(8,128)(2,1)} %copy-done.5, s32[]{:T(128)S(6)} %select_n.378, pred[]{:T(512)S(6)} %eq.49, bf16[768,2,128]{2,0,1:T(8,128)(2,1)S(1)} %add_convert_fusion.31, bf16[5,2048,128]{2,1,0:T(8,128)(2,1)} %all-gather.8.cloned.1.call-done, ...), kind=kOutput, calls=%fused_computation.87 | convolution fusion | flops 413171712 | bytes 10958853 | tf_op jit(solution)/shard_map/dot_general | solution.py:288
  458.9 3.4 collective-permute-start.18
  462.3 3.0 collective-permute-start.19
  466.0 2.8 collective-permute-start.20
  471.0 3.2 collective-permute-done.20
  474.2 4.7 collective-permute-done.21
  (286 shorter events, 92.1 us)
Async XLA Ops:
  7.2 130.3 %copy-start = (bf16[2048,160]{0,1:T(8,128)(2,1)S(1)}, bf16[2048,160]{0,1:T(8,128)(2,1)}, u32[]{:S(2)}) copy-start(bf16[2048,160]{0,1:T(8,128)(2,1)} %param.26) | copy-start | bytes 1966084
  7.2 112.1 %copy-start.31 = (s32[7]{0:T(128)S(1)}, s32[7]{0:T(128)}, u32[]{:S(2)}) copy-start(s32[7]{0:T(128)} %param.34) | copy-start | bytes 88
  7.2 112.4 %copy-start.13 = (f32[8,2048]{1,0:T(8,128)S(1)}, f32[8,2048]{1,0:T(8,128)}, u32[]{:S(2)}) copy-start(f32[8,2048]{1,0:T(8,128)} %param.25) | copy-start | bytes 196612
  7.2 116.8 %copy-start.32 = (f32[128]{0:T(128)S(1)}, f32[128]{0:T(128)}, u32[]{:S(2)}) copy-start(f32[128]{0:T(128)} %param.31) | copy-start | bytes 1540
  7.2 118.6 %copy-start.26 = (s32[8]{0:T(128)S(1)}, s32[8]{0:T(128)}, u32[]{:S(2)}) copy-start(s32[8]{0:T(128)} %param.33) | copy-start | bytes 100
  7.2 68.4 %all-gather.6.cloned.1.call-start = ((), (), s32[]{:S(2)}) async-start(), calls=%async_computation | async-start | bytes 3377152 | tf_op jit(solution)/shard_map/all_gather | solution.py:162
  21.3 94.1 %all-gather.8.cloned.1.call-start = ((), (), s32[]{:S(2)}) async-start(), calls=%async_computation.1 | async-start | bytes 2949120 | tf_op jit(solution)/shard_map/all_gather | solution.py:170
  75.7 252.4 %all-gather.12.cloned.1.call-start = ((), (), s32[]{:S(2)}) async-start(), calls=%async_computation.3 | async-start | bytes 8454144 | tf_op jit(solution)/shard_map/all_gather | solution.py:172
  115.4 272.4 %all-gather.10.cloned.1.call-start = ((), (), s32[]{:S(2)}) async-start(), calls=%async_computation.2 | async-start | bytes 4128768 | tf_op jit(solution)/shard_map/all_gather | solution.py:180
  152.4 13.6 %slice-start = ((s8[6291456]{0:T(1024)(128)(4,1)}), s8[4194304]{0:T(1024)(128)(4,1)S(1)}, s32[]{:S(2)}) async-start(s8[6291456]{0:T(1024)(128)(4,1)} %bitcast.258), calls=%async_computation.4 | async-start | bytes 8388608
  174.5 21.0 %copy-start.12 = (pred[128,128]{1,0:T(8,128)(4,1)S(1)}, pred[128,128]{1,0:T(8,128)(4,1)}, u32[]{:S(2)}) copy-start(pred[128,128]{1,0:T(8,128)(4,1)} %iota_compare_fusion) | copy-start | bytes 49156
  180.8 28.1 %copy-start.23 = (f32[6,2,64]{2,1,0:T(2,128)S(1)}, f32[6,2,64]{2,1,0:T(2,128)}, u32[]{:S(2)}) copy-start(f32[6,2,64]{2,1,0:T(2,128)} %copy-done.22) | copy-start | bytes 9220
  185.0 25.9 %copy-start.20 = (f32[1,2048]{1,0:T(1,128)S(1)}, f32[1,2048]{1,0:T(1,128)}, u32[]{:S(2)}) copy-start(f32[1,2048]{1,0:T(1,128)} %get-tuple-element.52) | copy-start | bytes 24580
  185.0 25.9 %copy-start.33 = (f32[128]{0:T(128)S(1)}, f32[128]{0:T(128)}, u32[]{:S(2)}) copy-start(f32[128]{0:T(128)} %param.32) | copy-start | bytes 1540
  185.1 14.0 %collective-permute-start.6 = (f32[2,65,64]{1,2,0:T(8,128)S(1)}, f32[2,65,64]{1,2,0:T(8,128)S(1)}, u32[]{:S(2)}, u32[]{:S(2)}) collective-permute-start(f32[2,65,64]{1,2,0:T(8,128)S(1)} %pad_maximum_fusion.4), channel_id=1, source_target_pairs={{0,112},{1,113},{2,114},{3,115},{4,116},{5,117},{6,118},{7,119},{8... | collective-permute-start | bytes 99848 | tf_op jit(solution)/shard_map/ppermute | solution.py:20
  185.7 16.6 %collective-permute-start.5 = (f32[2,65,64]{1,2,0:T(8,128)S(1)}, f32[2,65,64]{1,2,0:T(8,128)S(1)}, u32[]{:S(2)}, u32[]{:S(2)}) collective-permute-start(f32[2,65,64]{1,2,0:T(8,128)S(1)} %pad_maximum_fusion.4), channel_id=1, source_target_pairs={{0,96},{16,112},{1,97},{17,113},{2,98},{18,114},{3,99},{19,115},{4... | collective-permute-start | bytes 99848 | tf_op jit(solution)/shard_map/ppermute | solution.py:20
  191.2 14.7 %collective-permute-start.4 = (f32[2,65,64]{1,2,0:T(8,128)S(1)}, f32[2,65,64]{1,2,0:T(8,128)S(1)}, u32[]{:S(2)}, u32[]{:S(2)}) collective-permute-start(f32[2,65,64]{1,2,0:T(8,128)S(1)} %pad_maximum_fusion.4), channel_id=1, source_target_pairs={{0,80},{16,96},{32,112},{1,81},{17,97},{33,113},{2,82},{18,98},{34... | collective-permute-start | bytes 99848 | tf_op jit(solution)/shard_map/ppermute | solution.py:20
  192.5 13.6 %collective-permute-start.3 = (f32[2,65,64]{1,2,0:T(8,128)S(1)}, f32[2,65,64]{1,2,0:T(8,128)S(1)}, u32[]{:S(2)}, u32[]{:S(2)}) collective-permute-start(f32[2,65,64]{1,2,0:T(8,128)S(1)} %pad_maximum_fusion.4), channel_id=1, source_target_pairs={{0,64},{16,80},{32,96},{48,112},{1,65},{17,81},{33,97},{49,113},{2... | collective-permute-start | bytes 99848 | tf_op jit(solution)/shard_map/ppermute | solution.py:20
  193.8 12.4 %collective-permute-start.2 = (f32[2,65,64]{1,2,0:T(8,128)S(1)}, f32[2,65,64]{1,2,0:T(8,128)S(1)}, u32[]{:S(2)}, u32[]{:S(2)}) collective-permute-start(f32[2,65,64]{1,2,0:T(8,128)S(1)} %pad_maximum_fusion.4), channel_id=1, source_target_pairs={{0,48},{16,64},{32,80},{48,96},{64,112},{1,49},{17,65},{33,81},{49... | collective-permute-start | bytes 99848 | tf_op jit(solution)/shard_map/ppermute | solution.py:20
  199.0 7.3 %collective-permute-start.1 = (f32[2,65,64]{1,2,0:T(8,128)S(1)}, f32[2,65,64]{1,2,0:T(8,128)S(1)}, u32[]{:S(2)}, u32[]{:S(2)}) collective-permute-start(f32[2,65,64]{1,2,0:T(8,128)S(1)} %pad_maximum_fusion.4), channel_id=1, source_target_pairs={{0,32},{16,48},{32,64},{48,80},{64,96},{80,112},{1,33},{17,49},{33... | collective-permute-start | bytes 99848 | tf_op jit(solution)/shard_map/ppermute | solution.py:20
  202.3 6.3 %collective-permute-start = (f32[2,65,64]{1,2,0:T(8,128)S(1)}, f32[2,65,64]{1,2,0:T(8,128)S(1)}, u32[]{:S(2)}, u32[]{:S(2)}) collective-permute-start(f32[2,65,64]{1,2,0:T(8,128)S(1)} %pad_maximum_fusion.4), channel_id=1, source_target_pairs={{0,16},{16,32},{32,48},{48,64},{64,80},{80,96},{96,112},{1,17},{17... | collective-permute-start | bytes 99848 | tf_op jit(solution)/shard_map/ppermute | solution.py:20
  211.0 18.5 %copy-start.28 = (s32[4]{0:T(128)S(1)}, s32[4]{0:T(128)}, u32[]{:S(2)}) copy-start(s32[4]{0:T(128)} %fusion.91) | copy-start | bytes 52
  217.0 7.3 %collective-permute-start.7 = (bf16[768,128]{1,0:T(8,128)(2,1)S(1)}, bf16[768,128]{1,0:T(8,128)(2,1)S(1)}, u32[]{:S(2)}, u32[]{:S(2)}) collective-permute-start(bf16[768,128]{1,0:T(8,128)(2,1)S(1)} %multiply_convert_fusion), channel_id=1, source_target_pairs={{0,8},{1,9},{2,10},{3,11},{4,12},{5,13},{6,14},{7,15},{8,0},{9,1},... | collective-permute-start | bytes 589832 | tf_op jit(solution)/shard_map/ppermute | solution.py:25
  224.3 12.8 %collective-permute-start.8 = (bf16[768,2,128]{2,0,1:T(8,128)(2,1)S(1)}, bf16[768,2,128]{2,0,1:T(8,128)(2,1)S(1)}, u32[]{:S(2)}, u32[]{:S(2)}) collective-permute-start(bf16[768,2,128]{2,0,1:T(8,128)(2,1)S(1)} %maximum_select_fusion.2), channel_id=1, source_target_pairs={{0,6},{1,7},{2,0},{3,1},{4,2},{5,3},{6,4},{7,5},{8,14},{9,15},{10,... | collective-permute-start | bytes 1179656 | tf_op jit(solution)/shard_map/ppermute | solution.py:35
  227.5 9.7 %collective-permute-start.9 = (bf16[768,2,128]{2,0,1:T(8,128)(2,1)S(1)}, bf16[768,2,128]{2,0,1:T(8,128)(2,1)S(1)}, u32[]{:S(2)}, u32[]{:S(2)}) collective-permute-start(bf16[768,2,128]{2,0,1:T(8,128)(2,1)S(1)} %maximum_select_fusion.2), channel_id=1, source_target_pairs={{0,4},{1,5},{2,6},{3,7},{4,0},{5,1},{6,2},{7,3},{8,12},{9,13},{10,... | collective-permute-start | bytes 1179656 | tf_op jit(solution)/shard_map/ppermute | solution.py:35
  227.9 13.1 %collective-permute-start.10 = (bf16[768,2,128]{2,0,1:T(8,128)(2,1)S(1)}, bf16[768,2,128]{2,0,1:T(8,128)(2,1)S(1)}, u32[]{:S(2)}, u32[]{:S(2)}) collective-permute-start(bf16[768,2,128]{2,0,1:T(8,128)(2,1)S(1)} %maximum_select_fusion.2), channel_id=1, source_target_pairs={{0,2},{1,3},{2,4},{3,5},{4,6},{5,7},{6,0},{7,1},{8,10},{9,11},{10,... | collective-permute-start | bytes 1179656 | tf_op jit(solution)/shard_map/ppermute | solution.py:35
  246.0 17.1 %collective-permute-start.11 = (bf16[768,2,4,128]{3,0,1,2:T(8,128)(2,1)}, bf16[768,2,4,128]{3,0,1,2:T(8,128)(2,1)}, u32[]{:S(2)}, u32[]{:S(2)}) collective-permute-start(bf16[768,2,4,128]{3,0,1,2:T(8,128)(2,1)} %bitcast_select_fusion.1), channel_id=1, source_target_pairs={{0,1},{1,0},{2,3},{3,2},{4,5},{5,4},{6,7},{7,6},{8,9},{9,8},{10,11... | collective-permute-start | bytes 4718600 | tf_op jit(solution)/shard_map/ppermute | solution.py:25
  248.8 14.0 %collective-permute-start.22 = (f32[3,2,4096]{2,1,0:T(2,128)S(1)}, f32[3,2,4096]{2,1,0:T(2,128)S(1)}, u32[]{:S(2)}, u32[]{:S(2)}) collective-permute-start(f32[3,2,4096]{2,1,0:T(2,128)S(1)} %reshape.649), channel_id=1, source_target_pairs={{0,32},{16,48},{32,64},{48,80},{64,96},{80,112},{1,33},{17,49},{33... | collective-permute-start | bytes 294920 | tf_op jit(solution)/shard_map/ppermute | solution.py:20
  253.1 9.7 %collective-permute-start.23 = (f32[3,2,4096]{2,1,0:T(2,128)S(1)}, f32[3,2,4096]{2,1,0:T(2,128)S(1)}, u32[]{:S(2)}, u32[]{:S(2)}) collective-permute-start(f32[3,2,4096]{2,1,0:T(2,128)S(1)} %reshape.649), channel_id=1, source_target_pairs={{0,16},{16,32},{32,48},{48,64},{64,80},{80,96},{96,112},{1,17},{17... | collective-permute-start | bytes 294920 | tf_op jit(solution)/shard_map/ppermute | solution.py:20
  259.4 155.3 %collective-permute-start.24 = (f32[3,2,4096]{2,1,0:T(2,128)S(1)}, f32[3,2,4096]{2,1,0:T(2,128)S(1)}, u32[]{:S(2)}, u32[]{:S(2)}) collective-permute-start(f32[3,2,4096]{2,1,0:T(2,128)S(1)} %reshape.649), channel_id=1, source_target_pairs={{16,0},{32,16},{48,32},{64,48},{80,64},{96,80},{112,96},{17,1},{33... | collective-permute-start | bytes 294920 | tf_op jit(solution)/shard_map/ppermute | solution.py:20
  261.3 153.4 %collective-permute-start.25 = (f32[3,2,4096]{2,1,0:T(2,128)S(1)}, f32[3,2,4096]{2,1,0:T(2,128)S(1)}, u32[]{:S(2)}, u32[]{:S(2)}) collective-permute-start(f32[3,2,4096]{2,1,0:T(2,128)S(1)} %reshape.649), channel_id=1, source_target_pairs={{32,0},{48,16},{64,32},{80,48},{96,64},{112,80},{33,1},{49,17},{65... | collective-permute-start | bytes 294920 | tf_op jit(solution)/shard_map/ppermute | solution.py:20
  361.3 6.3 %collective-permute-start.12 = (bf16[1,2048]{1,0:T(2,128)(2,1)S(1)}, bf16[1,2048]{1,0:T(2,128)(2,1)S(1)}, u32[]{:S(2)}, u32[]{:S(2)}) collective-permute-start(bf16[1,2048]{1,0:T(2,128)(2,1)S(1)} %slice.404), channel_id=1, source_target_pairs={{0,16},{16,32},{32,48},{48,64},{64,80},{80,96},{96,112},{1,17},{17... | collective-permute-start | bytes 12296 | tf_op jit(solution)/shard_map/ppermute | solution.py:20
  374.1 13.7 %copy-start.19 = (f32[1,2048]{1,0:T(1,128)S(1)}, f32[1,2048]{1,0:T(1,128)}, u32[]{:S(2)}) copy-start(f32[1,2048]{1,0:T(1,128)} %get-tuple-element.58) | copy-start | bytes 24580
  414.7 39.0 %copy-start.18 = (f32[1,2048]{1,0:T(1,128)S(1)}, f32[1,2048]{1,0:T(1,128)}, u32[]{:S(2)}) copy-start(f32[1,2048]{1,0:T(1,128)} %get-tuple-element.51) | copy-start | bytes 24580
  414.7 6.3 %collective-permute-start.13 = (bf16[768,2,4,128]{3,0,1,2:T(8,128)(2,1)}, bf16[768,2,4,128]{3,0,1,2:T(8,128)(2,1)}, u32[]{:S(2)}, u32[]{:S(2)}) collective-permute-start(bf16[768,2,4,128]{3,0,1,2:T(8,128)(2,1)} %select_bitcast_fusion), channel_id=1, source_target_pairs={{0,1},{1,0},{2,3},{3,2},{4,5},{5,4},{6,7},{7,6},{8,9},{9,8},{10,11... | collective-permute-start | bytes 4718600 | tf_op jit(solution)/shard_map/ppermute | solution.py:25
  416.4 14.3 %collective-permute-start.26 = (f32[3,2,128]{2,1,0:T(2,128)S(1)}, f32[3,2,128]{2,1,0:T(2,128)S(1)}, u32[]{:S(2)}, u32[]{:S(2)}) collective-permute-start(f32[3,2,128]{2,1,0:T(2,128)S(1)} %pad_maximum_fusion.5), channel_id=1, source_target_pairs={{0,32},{16,48},{32,64},{48,80},{64,96},{80,112},{1,33},{17,49},{33... | collective-permute-start | bytes 9224 | tf_op jit(solution)/shard_map/ppermute | solution.py:20
  423.1 13.0 %collective-permute-start.14 = (bf16[768,2,128]{2,0,1:T(8,128)(2,1)S(1)}, bf16[768,2,128]{2,0,1:T(8,128)(2,1)S(1)}, u32[]{:S(2)}, u32[]{:S(2)}) collective-permute-start(bf16[768,2,128]{2,0,1:T(8,128)(2,1)S(1)} %get-tuple-element.45), channel_id=1, source_target_pairs={{0,2},{1,3},{2,4},{3,5},{4,6},{5,7},{6,0},{7,1},{8,10},{9,11},{10,... | collective-permute-start | bytes 1179656 | tf_op jit(solution)/shard_map/ppermute | solution.py:35
  423.8 21.3 %collective-permute-start.15 = (bf16[768,2,128]{2,0,1:T(8,128)(2,1)S(1)}, bf16[768,2,128]{2,0,1:T(8,128)(2,1)S(1)}, u32[]{:S(2)}, u32[]{:S(2)}) collective-permute-start(bf16[768,2,128]{2,0,1:T(8,128)(2,1)S(1)} %get-tuple-element.47), channel_id=1, source_target_pairs={{0,4},{1,5},{2,6},{3,7},{4,0},{5,1},{6,2},{7,3},{8,12},{9,13},{10,... | collective-permute-start | bytes 1179656 | tf_op jit(solution)/shard_map/ppermute | solution.py:35
  427.0 18.2 %collective-permute-start.16 = (bf16[768,2,128]{2,0,1:T(8,128)(2,1)S(1)}, bf16[768,2,128]{2,0,1:T(8,128)(2,1)S(1)}, u32[]{:S(2)}, u32[]{:S(2)}) collective-permute-start(bf16[768,2,128]{2,0,1:T(8,128)(2,1)S(1)} %get-tuple-element.46), channel_id=1, source_target_pairs={{0,6},{1,7},{2,0},{3,1},{4,2},{5,3},{6,4},{7,5},{8,14},{9,15},{10,... | collective-permute-start | bytes 1179656 | tf_op jit(solution)/shard_map/ppermute | solution.py:35
  428.8 5.9 %collective-permute-start.27 = (f32[3,2,128]{2,1,0:T(2,128)S(1)}, f32[3,2,128]{2,1,0:T(2,128)S(1)}, u32[]{:S(2)}, u32[]{:S(2)}) collective-permute-start(f32[3,2,128]{2,1,0:T(2,128)S(1)} %pad_maximum_fusion.5), channel_id=1, source_target_pairs={{0,16},{16,32},{32,48},{48,64},{64,80},{80,96},{96,112},{1,17},{17... | collective-permute-start | bytes 9224 | tf_op jit(solution)/shard_map/ppermute | solution.py:20
  430.7 17.5 %collective-permute-start.28 = (f32[3,2,128]{2,1,0:T(2,128)S(1)}, f32[3,2,128]{2,1,0:T(2,128)S(1)}, u32[]{:S(2)}, u32[]{:S(2)}) collective-permute-start(f32[3,2,128]{2,1,0:T(2,128)S(1)} %pad_maximum_fusion.5), channel_id=1, source_target_pairs={{16,0},{32,16},{48,32},{64,48},{80,64},{96,80},{112,96},{17,1},{33... | collective-permute-start | bytes 9224 | tf_op jit(solution)/shard_map/ppermute | solution.py:20
  434.7 13.6 %collective-permute-start.29 = (f32[3,2,128]{2,1,0:T(2,128)S(1)}, f32[3,2,128]{2,1,0:T(2,128)S(1)}, u32[]{:S(2)}, u32[]{:S(2)}) collective-permute-start(f32[3,2,128]{2,1,0:T(2,128)S(1)} %pad_maximum_fusion.5), channel_id=1, source_target_pairs={{32,0},{48,16},{64,32},{80,48},{96,64},{112,80},{33,1},{49,17},{65... | collective-permute-start | bytes 9224 | tf_op jit(solution)/shard_map/ppermute | solution.py:20
  445.5 8.2 %collective-permute-start.17 = (bf16[768,128]{1,0:T(8,128)(2,1)S(1)}, bf16[768,128]{1,0:T(8,128)(2,1)S(1)}, u32[]{:S(2)}, u32[]{:S(2)}) collective-permute-start(bf16[768,128]{1,0:T(8,128)(2,1)S(1)} %select_bitcast_fusion.4), channel_id=1, source_target_pairs={{0,8},{1,9},{2,10},{3,11},{4,12},{5,13},{6,14},{7,15},{8,0},{9,1},... | collective-permute-start | bytes 589832 | tf_op jit(solution)/shard_map/ppermute | solution.py:25
  453.6 27.0 %copy-start.1 = (bf16[2048,160]{0,1:T(8,128)(2,1)S(1)}, bf16[2048,160]{0,1:T(8,128)(2,1)}, u32[]{:S(2)}) copy-start(bf16[2048,160]{0,1:T(8,128)(2,1)} %param.26) | copy-start | bytes 1966084
  458.9 11.2 %collective-permute-start.18 = (bf16[3,256,128]{2,1,0:T(8,128)(2,1)S(1)}, bf16[3,256,128]{2,1,0:T(8,128)(2,1)S(1)}, u32[]{:S(2)}, u32[]{:S(2)}) collective-permute-start(bf16[3,256,128]{2,1,0:T(8,128)(2,1)S(1)} %bitcast.286), channel_id=1, source_target_pairs={{0,32},{16,48},{32,64},{48,80},{64,96},{80,112},{1,33},{17,49},{33... | collective-permute-start | bytes 589832 | tf_op jit(solution)/shard_map/ppermute | solution.py:20
  462.3 8.6 %collective-permute-start.19 = (bf16[3,256,128]{2,1,0:T(8,128)(2,1)S(1)}, bf16[3,256,128]{2,1,0:T(8,128)(2,1)S(1)}, u32[]{:S(2)}, u32[]{:S(2)}) collective-permute-start(bf16[3,256,128]{2,1,0:T(8,128)(2,1)S(1)} %bitcast.287), channel_id=1, source_target_pairs={{0,16},{16,32},{32,48},{48,64},{64,80},{80,96},{96,112},{1,17},{17... | collective-permute-start | bytes 589832 | tf_op jit(solution)/shard_map/ppermute | solution.py:20
  466.0 8.2 %collective-permute-start.20 = (bf16[3,256,128]{2,1,0:T(8,128)(2,1)S(1)}, bf16[3,256,128]{2,1,0:T(8,128)(2,1)S(1)}, u32[]{:S(2)}, u32[]{:S(2)}) collective-permute-start(bf16[3,256,128]{2,1,0:T(8,128)(2,1)S(1)} %bitcast.288), channel_id=1, source_target_pairs={{16,0},{32,16},{48,32},{64,48},{80,64},{96,80},{112,96},{17,1},{33... | collective-permute-start | bytes 589832 | tf_op jit(solution)/shard_map/ppermute | solution.py:20
  468.9 10.1 %collective-permute-start.21 = (bf16[3,256,128]{2,1,0:T(8,128)(2,1)S(1)}, bf16[3,256,128]{2,1,0:T(8,128)(2,1)S(1)}, u32[]{:S(2)}, u32[]{:S(2)}) collective-permute-start(bf16[3,256,128]{2,1,0:T(8,128)(2,1)S(1)} %bitcast.289), channel_id=1, source_target_pairs={{32,0},{48,16},{64,32},{80,48},{96,64},{112,80},{33,1},{49,17},{65... | collective-permute-start | bytes 589832 | tf_op jit(solution)/shard_map/ppermute | solution.py:20
  (22 other events, 124.9 us)
Sparse Core Ops, SparseCore 0:
  21.4 54.1 all-gather.5
  77.3 38.0 all-gather.7
  117.7 210.3 all-gather.11
  329.5 58.2 all-gather.9

commit v6 on v4

--- a/solution.py
+++ b/solution.py
@@ -159,7 +159,7 @@
     edge_pad = jnp.concatenate([before_token, jnp.zeros((8 - held,), before_token.dtype)])
     all_tokens = jnp.concatenate([tokens_here.reshape(-1), edge_pad])
     own_rows = jnp.take(symbol_lookup_table, all_tokens, axis=0)
-    gathered_rows = lax.all_gather(own_rows, "head", axis=1, tiled=True)
+    gathered_rows = hier_all_gather(own_rows, "head")
     embedded = gathered_rows[:slot_rows]
     edge_rows = gathered_rows[slot_rows : slot_rows + held]
     map_count = joined_linear_maps.shape[0]
@@ -315,8 +315,10 @@
         )
 
     hidden_near = from_neighbours(hidden.reshape(held, PAGE, features_on_shard))
-    state_near = from_neighbours(state_held)
-    edge_near = from_neighbours(edge_held)
+    state_width = state_held.shape[2]
+    record_near = from_neighbours(jnp.concatenate([state_held, edge_held], axis=2))
+    state_near = record_near[:, :, :state_width]
+    edge_near = record_near[:, :, state_width:]
     slot_page = first_page + slot_number
     source_group = slot_page // held
     source_index = (source_group - group_here + reach) * held + slot_page - source_group * held

time: 425 us -> 518 us (1.22)
  local copies, waits for them, and re-layouts: 76.4 us -> 157 us
  other arithmetic: 62.4 us -> 103 us
  waiting for transfers between devices: 121 us -> 95.4 us
    all_gather x1 -> x0, waiting for transfers between devices: 45.1 us -> none  [per_device(): gathered_rows = lax.all_gather(own_rows, 'head', axis=1, tiled=True)]
    convert_element_type x0 -> x6, local copies, waits for them, and re-layouts: none -> 37.8 us  [the longest x3 28.4 us: per_device(): residual = (embedded.astype(jnp.float32) + mixer_total).astype(jnp.bfloat16)]
    ppermute x9 -> x12, waiting for transfers between devices: 39.3 us -> 64.3 us  [_ring(): return lax.ppermute(value, axis, pairs)]
    convert_element_type x0 -> x5, other arithmetic: none -> 19.5 us  [the longest x2 9.08 us: per_device(): residual = (embedded.astype(jnp.float32) + mixer_total).astype(jnp.bfloat16)]
    convert_element_type x2 -> x4, local copies, waits for them, and re-layouts: 13.3 us -> 32.7 us  [per_device(): mixer_total = hier_all_gather(mixer_owned, 'head').astype(jnp.float32)]
    ppermute x20 -> x16, starting transfers between devices: 56.3 us -> 46.7 us  [passed_along(): lax.ppermute(value, axis, [(source, source + steps) for source in range(i...]
    reshape x0 -> x1, local copies, waits for them, and re-layouts: none -> 9.17 us  [per_device(): channel_prev = jnp.concatenate([edge_two[:, None, :], channel_pages[:, :-...]
    ppermute x20 -> x16, waiting for transfers between devices: 17.9 us -> 8.91 us  [passed_along(): lax.ppermute(value, axis, [(source, source + steps) for source in range(i...]
  transfers between devices with their start and end apart: 38 -> 38, of which waited for: 17 -> 18; matrix products, arithmetic and copies ran while one was open for 30% -> 46% of each run, Pallas kernels for 0% -> 0%
where the time goes in v6:
time: 518 us; the launch traced here: 510 us
  local copies, waits for them, and re-layouts  157 us (30%)
  other arithmetic  103 us (20%)
  waiting for transfers between devices  95.4 us (18%)
  starting transfers between devices  78.4 us (15%)
  matrix products  59 us (11%)
  between operations  18 us (3%)
    ppermute x12, waiting for transfers between devices, _ring(): return lax.ppermute(value, axis, pairs)  64.3 us
    ppermute x16, starting transfers between devices, passed_along(): lax.ppermute(value, axis, [(source, source + steps) for source in range(i...  46.7 us
    convert_element_type x4, local copies, waits for them, and re-layouts, per_device(): mixer_total = hier_all_gather(mixer_owned, 'head').astype(jnp.float32)  32.7 us
    convert_element_type x3, local copies, waits for them, and re-layouts, per_device(): residual = (embedded.astype(jnp.float32) + mixer_total).astype(jnp.bfloat16)  28.4 us
    unnamed x136, local copies, waits for them, and re-layouts  24.3 us
    ppermute x8, waiting for transfers between devices, _swap(): return lax.ppermute(value, axis, [(s, s ^ flip) for s in range(count)])  22 us
    ppermute x12, starting transfers between devices, _ring(): return lax.ppermute(value, axis, pairs)  18.8 us
    dot_general x3, matrix products, mixed_inputs(): jnp.dot(column_part, blend_widening_maps[number], preferred_element_type=...  14.2 us
  transfers between devices with their start and end apart: 38, of which 18 were waited for; matrix products, arithmetic and copies ran while one was open for 46% of the time, Pallas kernels for 0%

profile of v6, /device:TPU:2, one launch (start us, length us, event | category | flops | bytes accessed | tf_op | source)
XLA Modules:
  0.0 510.0 jit_solution(13561099807392389637)
XLA Ops:
  10.6 9.8 %gather_fusion.2 = bf16[776,128]{1,0:T(8,128)(2,1)S(1)} fusion(bf16[65536,128]{1,0:T(8,128)(2,1)} %param.20, s32[1024]{0:T(1024)S(1)} %pad_clamp_fusion.3), kind=kCustom, calls=%fused_computation.4 | custom fusion | bytes 400416 | tf_op jit(solution)/shard_map/jit(_take)/gather | solution.py:161
  31.0 3.6 collective-permute-start.2
  35.9 6.4 %collective-permute-done.3 = bf16[776,2,128]{2,0,1:T(8,128)(2,1)S(1)} collective-permute-done((bf16[776,2,128]{2,0,1:T(8,128)(2,1)S(1)}, bf16[776,2,128]{2,0,1:T(8,128)(2,1)S(1)}, u32[]{:S(2)}, u32[]{:S(2)}) %collective-permute-start.3) | collective-permute-done | bytes 397344 | tf_op jit(solution)/shard_map/ppermute | solution.py:35
  42.3 8.9 %collective-permute-done.2 = bf16[776,2,128]{2,0,1:T(8,128)(2,1)S(1)} collective-permute-done((bf16[776,2,128]{2,0,1:T(8,128)(2,1)S(1)}, bf16[776,2,128]{2,0,1:T(8,128)(2,1)S(1)}, u32[]{:S(2)}, u32[]{:S(2)}) %collective-permute-start.2) | collective-permute-done | bytes 397344 | tf_op jit(solution)/shard_map/ppermute | solution.py:35
  75.7 10.2 %copy.105 = f32[768,2,4,2,128]{4,3,2,1,0:T(2,128)} copy(f32[768,2,4,2,128]{4,0,1,2,3:T(8,128)} %slice_convert_fusion) | data formatting | bytes 12582912 | tf_op jit(solution)/shard_map/convert_element_type | solution.py:272
  85.9 9.0 %reshape.1028 = f32[768,2048]{1,0:T(8,128)} reshape(f32[768,2,4,2,128]{4,3,2,1,0:T(2,128)} %copy.105) | data formatting | bytes 12582912 | tf_op jit(solution)/shard_map/convert_element_type | solution.py:272
  95.0 9.1 %reshape.1030 = f32[3,256,2048]{2,1,0:T(8,128)} reshape(f32[768,2,4,2,128]{4,3,2,1,0:T(2,128)} %copy.105) | data formatting | bytes 12582912 | tf_op jit(solution)/shard_map/convert_element_type | solution.py:272
  105.2 3.5 subtract_multiply_fusion.1
  114.8 3.6 bitcast_subtract_fusion
  121.2 7.2 %fusion.30 = bf16[768,64]{0,1:T(8,128)(2,1)S(1)} fusion(bf16[2048,64]{0,1:T(8,128)(2,1)S(1)} %copy-done.20, f32[768,2048]{1,0:T(8,128)} %copy-done.2, f32[2048]{0:T(1024)S(1)} %bitcast.340, bf16[5,32,2048]{2,1,0:T(8,128)(2,1)} %param.27, bf16[768,160]{0,1:T(8,128)(2,1)S(1)} %fusion.28, f32[768,2048]{1,0:T(8,128)} %reshape.1028, ...), kind=kOutput, calls=%fused_computation.84 | convolution fusion | flops 311476224 | bytes 13139968 | tf_op jit(solution)/shard_map/dot_general | solution.py:104
  140.7 7.4 %add_convert_fusion.4 = bf16[768,2048]{1,0:T(8,128)(2,1)} fusion(f32[768,2048]{1,0:T(8,128)} %copy-done.2, f32[2048]{0:T(1024)} %bitcast.339, bf16[5,32,2048]{2,1,0:T(8,128)(2,1)} %param.27, bf16[768,160]{0,1:T(8,128)(2,1)S(1)} %copy-done.14, f32[768]{0:T(1024)S(1)} %add_rsqrt_fusion.1, f32[768,2048]{1,0:T(8,128)} %reshape.1028, ...), kind=kOutput, calls=%fused_computation.28 | convolution fusion | flops 110100480 | bytes 15925248 | tf_op jit(solution)/shard_map/dot_general | solution.py:93
  153.0 3.5 add_convert_fusion.7
  171.4 5.7 %collective-permute-start.10 = (f32[2,65,64]{1,2,0:T(8,128)S(1)}, f32[2,65,64]{1,2,0:T(8,128)S(1)}, u32[]{:S(2)}, u32[]{:S(2)}) collective-permute-start(f32[2,65,64]{1,2,0:T(8,128)S(1)} %pad_maximum_fusion.6), channel_id=1, source_target_pairs={{0,96},{16,112},{1,97},{17,113},{2,98},{18,114},{3,99},{19,115},{4... | collective-permute-start | bytes 99848 | tf_op jit(solution)/shard_map/ppermute | solution.py:20
  196.8 6.8 %multiply_convert_fusion = bf16[768,128]{1,0:T(8,128)(2,1)S(1)} fusion(bf16[6,2048,128]{2,1,0:T(8,128)(2,1)} %all-gather.3.cloned.1.call-done, f32[768,2048]{1,0:T(8,128)} %copy-done.2, f32[2048]{0:T(1024)S(1)} %bitcast.336, f32[768,128]{1,0:T(8,128)S(1)} %copy.123, f32[768,128]{1,0:T(8,128)S(1)} %reshape.1195, f32[768,128]{1,0:T(8,128)S(1)} %copy.122, ...), kind=kOutput, calls=%fused_computation.119 | convolution fusion | flops 513638400 | bytes 14680576 | tf_op jit(solution)/shard_map/dot_general | solution.py:195
  203.5 3.7 convolution_convert_fusion.1
  207.3 4.7 copy.124
  212.0 3.8 fusion.94
  223.1 3.7 collective-permute-done.12
  234.6 8.6 %collective-permute-done.13 = bf16[768,2,128]{2,0,1:T(8,128)(2,1)S(1)} collective-permute-done((bf16[768,2,128]{2,0,1:T(8,128)(2,1)S(1)}, bf16[768,2,128]{2,0,1:T(8,128)(2,1)S(1)}, u32[]{:S(2)}, u32[]{:S(2)}) %collective-permute-start.13) | collective-permute-done | bytes 393248 | tf_op jit(solution)/shard_map/ppermute | solution.py:35
  243.2 7.7 %collective-permute-done.15 = bf16[768,2,128]{2,0,1:T(8,128)(2,1)S(1)} collective-permute-done((bf16[768,2,128]{2,0,1:T(8,128)(2,1)S(1)}, bf16[768,2,128]{2,0,1:T(8,128)(2,1)S(1)}, u32[]{:S(2)}, u32[]{:S(2)}) %collective-permute-start.15) | collective-permute-done | bytes 393248 | tf_op jit(solution)/shard_map/ppermute | solution.py:35
  256.4 5.2 %collective-permute-done.16 = bf16[768,128]{1,0:T(8,128)(2,1)S(1)} collective-permute-done((bf16[768,128]{1,0:T(8,128)(2,1)S(1)}, bf16[768,128]{1,0:T(8,128)(2,1)S(1)}, u32[]{:S(2)}, u32[]{:S(2)}) %collective-permute-start.16) | collective-permute-done | bytes 196640 | tf_op jit(solution)/shard_map/ppermute | solution.py:25
  264.6 4.3 collective-permute-done.17
  273.6 14.1 %collective-permute-done.20 = bf16[768,2,128]{2,0,1:T(8,128)(2,1)S(1)} collective-permute-done((bf16[768,2,128]{2,0,1:T(8,128)(2,1)S(1)}, bf16[768,2,128]{2,0,1:T(8,128)(2,1)S(1)}, u32[]{:S(2)}, u32[]{:S(2)}) %collective-permute-start.20) | collective-permute-done | bytes 393248 | tf_op jit(solution)/shard_map/ppermute | solution.py:35
  300.4 5.2 %convert_reduce_fusion = (f32[768]{0:T(1024)S(1)}, bf16[768,2,4,2,128]{4,0,1,2,3:T(8,128)(2,1)}) fusion(bf16[768,2,4,1,128]{4,0,1,2,3:T(8,128)(2,1)S(1)} %bitcast_select_fusion.2, bf16[768,2,4,1,128]{4,0,1,2,3:T(8,128)(2,1)} %bitcast.109, pred[]{:T(512)S(6)} %eq.62, bf16[776,2,4,2,128]{4,0,1,2,3:T(8,128)(2,1)} %copy-done.3), kind=kLoop, calls=%fused_computation.11 | loop fusion | flops 14155008 | bytes 9440257 | tf_op jit(solution)/shard_map/reduce_sum | solution.py:79
  305.7 5.1 %fusion.9 = f32[768,2,4,2,128]{4,0,1,2,3:T(8,128)} fusion(bf16[768,2,4,1,128]{4,0,1,2,3:T(8,128)(2,1)} %bitcast.109, bf16[768,2,4,1,128]{4,0,1,2,3:T(8,128)(2,1)S(1)} %bitcast_select_fusion.2, pred[]{:T(512)S(6)} %eq.62), kind=kLoop, calls=%fused_computation.42 | loop fusion | flops 6291456 | bytes 9437185 | tf_op jit(solution)/shard_map/convert_element_type | solution.py:271
  310.8 10.3 %copy.129 = f32[768,2,4,2,128]{4,3,2,1,0:T(2,128)} copy(f32[768,2,4,2,128]{4,0,1,2,3:T(8,128)} %fusion.9) | data formatting | bytes 12582912 | tf_op jit(solution)/shard_map/convert_element_type | solution.py:271
  321.1 6.6 %copy.127 = f32[768,2,4,2,128]{0,4,3,2,1:T(8,128)} copy(f32[768,2,4,2,128]{4,0,1,2,3:T(8,128)} %fusion.9) | data formatting | bytes 12582912 | tf_op jit(solution)/shard_map/convert_element_type | solution.py:271
  330.6 6.6 %copy.128 = f32[768,2048]{1,0:T(8,128)} copy(f32[768,2048]{0,1:T(8,128)} %bitcast.302) | data formatting | bytes 12582912 | tf_op jit(solution)/shard_map/convert_element_type | solution.py:271
  337.2 9.2 %reshape.1034 = f32[3,256,2048]{2,1,0:T(8,128)} reshape(f32[768,2,4,2,128]{4,3,2,1,0:T(2,128)} %copy.129) | data formatting | bytes 12582912 | tf_op jit(solution)/shard_map/convert_element_type | solution.py:271
  346.4 5.8 %add_convert_fusion.2 = bf16[768,2048]{1,0:T(8,128)(2,1)S(1)} fusion(f32[768,2048]{1,0:T(8,128)} %reshape.1028, f32[768,2048]{1,0:T(8,128)} %copy.128), kind=kLoop, calls=%fused_computation.26 | loop fusion | flops 3145728 | bytes 15728640 | tf_op jit(solution)/shard_map/convert_element_type | solution.py:272
  353.9 3.5 collective-permute-start.22
  357.4 4.0 subtract_multiply_fusion
  367.7 4.0 collective-permute-start.33
  371.7 7.9 %collective-permute-start.32 = (f32[3,2,4224]{2,1,0:T(2,128)S(1)}, f32[3,2,4224]{2,1,0:T(2,128)S(1)}, u32[]{:S(2)}, u32[]{:S(2)}) collective-permute-start(f32[3,2,4224]{2,1,0:T(2,128)S(1)} %maximum_maximum_fusion), channel_id=1, source_target_pairs={{0,32},{16,48},{32,64},{48,80},{64,96},{80,112},{1,33},{17,49},{33... | collective-permute-start | bytes 304136 | tf_op jit(solution)/shard_map/ppermute | solution.py:20
  382.3 6.8 %pad_maximum_fusion.1 = f32[3,256,2048]{2,1,0:T(8,128)} fusion(f32[3,255,2048]{2,1,0:T(8,128)} %bitcast.300, f32[3,1,2048]{2,1,0:T(1,128)S(1)} %maximum_multiply_fusion), kind=kLoop, calls=%fused_computation.21 | loop fusion | flops 1572864 | bytes 12582912 | tf_op jit(solution)/shard_map/concatenate | solution.py:281
  389.1 9.2 %reshape.915 = f32[768,2,4,2,128]{4,3,2,1,0:T(2,128)} reshape(f32[3,256,2048]{2,1,0:T(8,128)} %pad_maximum_fusion.1) | data formatting | bytes 12582912 | tf_op jit(solution)/shard_map/reshape | solution.py:283
  398.3 8.5 %fusion.6 = (bf16[768,2,4,2,128]{4,0,1,2,3:T(8,128)(2,1)}, bf16[768,2,4,2,128]{4,0,1,2,3:T(8,128)(2,1)}) fusion(bf16[768,2,4,2,128]{4,0,1,2,3:T(8,128)(2,1)} %get-tuple-element.21, f32[768,2,4,2,128]{4,3,2,1,0:T(2,128)} %reshape.915, f32[2,4,2,128]{3,0,1,2:T(2,128)S(1)} %copy.133, f32[768]{0:T(1024)S(1)} %add_rsqrt_fusion, ...), kind=kLoop, calls=%fused_computation.18 | loop fusion | flops 15728640 | bytes 15751168 | tf_op jit(solution)/shard_map/convert_element_type | solution.py:285
  406.8 4.7 copy.132
  411.5 3.8 fusion.27
  415.3 4.7 copy.134
  420.0 8.9 %convolution_convert_fusion = bf16[768,2048]{1,0:T(8,128)(2,1)} fusion(bf16[2,2048,448]{1,2,0:T(8,128)(2,1)} %all-gather.5.cloned.1.call-done, bf16[768,2048]{0,1:T(8,128)(2,1)} %bitcast.308), kind=kOutput, calls=%fused_computation.37 | convolution fusion | flops 2821177344 | bytes 9961472 | tf_op jit(solution)/shard_map/dot_general | solution.py:291
  428.9 4.6 copy.135
  433.6 3.8 fusion.93
  455.1 7.7 %collective-permute-done.24 = bf16[768,2,128]{2,0,1:T(8,128)(2,1)S(1)} collective-permute-done((bf16[768,2,128]{2,0,1:T(8,128)(2,1)}, bf16[768,2,128]{2,0,1:T(8,128)(2,1)S(1)}, u32[]{:S(2)}, u32[]{:S(2)}) %collective-permute-start.24) | collective-permute-done | bytes 393248 | tf_op jit(solution)/shard_map/ppermute | solution.py:35
  462.8 7.3 %collective-permute-done.26 = bf16[768,2,128]{2,0,1:T(8,128)(2,1)S(1)} collective-permute-done((bf16[768,2,128]{2,0,1:T(8,128)(2,1)S(1)}, bf16[768,2,128]{2,0,1:T(8,128)(2,1)S(1)}, u32[]{:S(2)}, u32[]{:S(2)}) %collective-permute-start.26) | collective-permute-done | bytes 393248 | tf_op jit(solution)/shard_map/ppermute | solution.py:35
  484.2 3.9 collective-permute-start.28
  490.1 3.9 collective-permute-start.30
  494.1 6.9 %collective-permute-done.30 = bf16[3,256,128]{2,1,0:T(8,128)(2,1)S(1)} collective-permute-done((bf16[3,256,128]{2,1,0:T(8,128)(2,1)S(1)}, bf16[3,256,128]{2,1,0:T(8,128)(2,1)S(1)}, u32[]{:S(2)}, u32[]{:S(2)}) %collective-permute-start.30) | collective-permute-done | bytes 196640 | tf_op jit(solution)/shard_map/ppermute | solution.py:20
  (381 shorter events, 188.3 us)
Async XLA Ops:
  7.2 111.3 %copy-start = (bf16[2048,160]{0,1:T(8,128)(2,1)S(1)}, bf16[2048,160]{0,1:T(8,128)(2,1)}, u32[]{:S(2)}) copy-start(bf16[2048,160]{0,1:T(8,128)(2,1)} %param.26) | copy-start | bytes 1966084
  7.2 149.3 %all-gather.3.cloned.1.call-start = ((), (), s32[]{:S(2)}) async-start(), calls=%async_computation | async-start | bytes 3538944 | tf_op jit(solution)/shard_map/all_gather | solution.py:173
  20.6 8.3 %collective-permute-start = (bf16[776,128]{1,0:T(8,128)(2,1)S(1)}, bf16[776,128]{1,0:T(8,128)(2,1)S(1)}, u32[]{:S(2)}, u32[]{:S(2)}) collective-permute-start(bf16[776,128]{1,0:T(8,128)(2,1)S(1)} %broadcast_select_fusion), channel_id=1, source_target_pairs={{0,8},{1,9},{2,10},{3,11},{4,12},{5,13},{6,14},{7,15},{8,0},{9,1},... | collective-permute-start | bytes 595976 | tf_op jit(solution)/shard_map/ppermute | solution.py:25
  25.8 394.2 %all-gather.5.cloned.1.call-start = ((), (), s32[]{:S(2)}) async-start(), calls=%async_computation.1 | async-start | bytes 4128768 | tf_op jit(solution)/shard_map/all_gather | solution.py:175
  25.9 37.9 %copy-start.33 = (pred[4]{0:T(512)(128)(4,1)}, pred[4]{0:T(512)(128)(4,1)S(1)}, u32[]{:S(2)}) copy-start(pred[4]{0:T(512)(128)(4,1)S(1)} %compare_and_fusion.3) | copy-start | bytes 16
  26.3 28.5 %copy-start.35 = (s32[1024]{0:T(1024)}, s32[1024]{0:T(1024)S(1)}, u32[]{:S(2)}) copy-start(s32[1024]{0:T(1024)S(1)} %pad_clamp_fusion.2) | copy-start | bytes 12292
  29.0 13.3 %collective-permute-start.3 = (bf16[776,2,128]{2,0,1:T(8,128)(2,1)S(1)}, bf16[776,2,128]{2,0,1:T(8,128)(2,1)S(1)}, u32[]{:S(2)}, u32[]{:S(2)}) collective-permute-start(bf16[776,2,128]{2,0,1:T(8,128)(2,1)S(1)} %maximum_select_fusion.3), channel_id=1, source_target_pairs={{0,2},{1,3},{2,4},{3,5},{4,6},{5,7},{6,0},{7,1},{8,10},{9,11},{10,... | collective-permute-start | bytes 1191944 | tf_op jit(solution)/shard_map/ppermute | solution.py:35
  31.0 20.2 %collective-permute-start.2 = (bf16[776,2,128]{2,0,1:T(8,128)(2,1)S(1)}, bf16[776,2,128]{2,0,1:T(8,128)(2,1)S(1)}, u32[]{:S(2)}, u32[]{:S(2)}) collective-permute-start(bf16[776,2,128]{2,0,1:T(8,128)(2,1)S(1)} %maximum_select_fusion.3), channel_id=1, source_target_pairs={{0,4},{1,5},{2,6},{3,7},{4,0},{5,1},{6,2},{7,3},{8,12},{9,13},{10,... | collective-permute-start | bytes 1191944 | tf_op jit(solution)/shard_map/ppermute | solution.py:35
  34.6 16.6 %collective-permute-start.1 = (bf16[776,2,128]{2,0,1:T(8,128)(2,1)S(1)}, bf16[776,2,128]{2,0,1:T(8,128)(2,1)S(1)}, u32[]{:S(2)}, u32[]{:S(2)}) collective-permute-start(bf16[776,2,128]{2,0,1:T(8,128)(2,1)S(1)} %maximum_select_fusion.3), channel_id=1, source_target_pairs={{0,6},{1,7},{2,0},{3,1},{4,2},{5,3},{6,4},{7,5},{8,14},{9,15},{10,... | collective-permute-start | bytes 1191944 | tf_op jit(solution)/shard_map/ppermute | solution.py:35
  56.3 7.8 %collective-permute-start.4 = (bf16[776,2,4,128]{3,0,1,2:T(8,128)(2,1)}, bf16[776,2,4,128]{3,0,1,2:T(8,128)(2,1)}, u32[]{:S(2)}, u32[]{:S(2)}) collective-permute-start(bf16[776,2,4,128]{3,0,1,2:T(8,128)(2,1)} %bitcast_select_fusion.1), channel_id=1, source_target_pairs={{0,1},{1,0},{2,3},{3,2},{4,5},{5,4},{6,7},{7,6},{8,9},{9,8},{10,11... | collective-permute-start | bytes 4767752 | tf_op jit(solution)/shard_map/ppermute | solution.py:25
  170.6 23.6 %copy-start.36 = (f32[6,2,64]{2,1,0:T(2,128)S(1)}, f32[6,2,64]{2,1,0:T(2,128)}, u32[]{:S(2)}) copy-start(f32[6,2,64]{2,1,0:T(2,128)} %get-tuple-element.81) | copy-start | bytes 9220
  170.7 13.8 %collective-permute-start.11 = (f32[2,65,64]{1,2,0:T(8,128)S(1)}, f32[2,65,64]{1,2,0:T(8,128)S(1)}, u32[]{:S(2)}, u32[]{:S(2)}) collective-permute-start(f32[2,65,64]{1,2,0:T(8,128)S(1)} %pad_maximum_fusion.6), channel_id=1, source_target_pairs={{0,112},{1,113},{2,114},{3,115},{4,116},{5,117},{6,118},{7,119},{8... | collective-permute-start | bytes 99848 | tf_op jit(solution)/shard_map/ppermute | solution.py:20
  171.4 16.4 %collective-permute-start.10 = (f32[2,65,64]{1,2,0:T(8,128)S(1)}, f32[2,65,64]{1,2,0:T(8,128)S(1)}, u32[]{:S(2)}, u32[]{:S(2)}) collective-permute-start(f32[2,65,64]{1,2,0:T(8,128)S(1)} %pad_maximum_fusion.6), channel_id=1, source_target_pairs={{0,96},{16,112},{1,97},{17,113},{2,98},{18,114},{3,99},{19,115},{4... | collective-permute-start | bytes 99848 | tf_op jit(solution)/shard_map/ppermute | solution.py:20
  177.1 14.3 %collective-permute-start.9 = (f32[2,65,64]{1,2,0:T(8,128)S(1)}, f32[2,65,64]{1,2,0:T(8,128)S(1)}, u32[]{:S(2)}, u32[]{:S(2)}) collective-permute-start(f32[2,65,64]{1,2,0:T(8,128)S(1)} %pad_maximum_fusion.6), channel_id=1, source_target_pairs={{0,80},{16,96},{32,112},{1,81},{17,97},{33,113},{2,82},{18,98},{34... | collective-permute-start | bytes 99848 | tf_op jit(solution)/shard_map/ppermute | solution.py:20
  178.4 13.1 %collective-permute-start.8 = (f32[2,65,64]{1,2,0:T(8,128)S(1)}, f32[2,65,64]{1,2,0:T(8,128)S(1)}, u32[]{:S(2)}, u32[]{:S(2)}) collective-permute-start(f32[2,65,64]{1,2,0:T(8,128)S(1)} %pad_maximum_fusion.6), channel_id=1, source_target_pairs={{0,64},{16,80},{32,96},{48,112},{1,65},{17,81},{33,97},{49,113},{2... | collective-permute-start | bytes 99848 | tf_op jit(solution)/shard_map/ppermute | solution.py:20
  179.7 12.0 %collective-permute-start.7 = (f32[2,65,64]{1,2,0:T(8,128)S(1)}, f32[2,65,64]{1,2,0:T(8,128)S(1)}, u32[]{:S(2)}, u32[]{:S(2)}) collective-permute-start(f32[2,65,64]{1,2,0:T(8,128)S(1)} %pad_maximum_fusion.6), channel_id=1, source_target_pairs={{0,48},{16,64},{32,80},{48,96},{64,112},{1,49},{17,65},{33,81},{49... | collective-permute-start | bytes 99848 | tf_op jit(solution)/shard_map/ppermute | solution.py:20
  184.5 7.3 %collective-permute-start.6 = (f32[2,65,64]{1,2,0:T(8,128)S(1)}, f32[2,65,64]{1,2,0:T(8,128)S(1)}, u32[]{:S(2)}, u32[]{:S(2)}) collective-permute-start(f32[2,65,64]{1,2,0:T(8,128)S(1)} %pad_maximum_fusion.6), channel_id=1, source_target_pairs={{0,32},{16,48},{32,64},{48,80},{64,96},{80,112},{1,33},{17,49},{33... | collective-permute-start | bytes 99848 | tf_op jit(solution)/shard_map/ppermute | solution.py:20
  187.8 6.2 %collective-permute-start.5 = (f32[2,65,64]{1,2,0:T(8,128)S(1)}, f32[2,65,64]{1,2,0:T(8,128)S(1)}, u32[]{:S(2)}, u32[]{:S(2)}) collective-permute-start(f32[2,65,64]{1,2,0:T(8,128)S(1)} %pad_maximum_fusion.6), channel_id=1, source_target_pairs={{0,16},{16,32},{32,48},{48,64},{64,80},{80,96},{96,112},{1,17},{17... | collective-permute-start | bytes 99848 | tf_op jit(solution)/shard_map/ppermute | solution.py:20
  223.1 3.8 collective-permute-start.12
  230.2 42.5 %copy-start.50 = (s32[8]{0:T(128)S(1)}, s32[8]{0:T(128)}, u32[]{:S(2)}) copy-start(s32[8]{0:T(128)} %param.33) | copy-start | bytes 100
  230.3 12.9 %collective-permute-start.13 = (bf16[768,2,128]{2,0,1:T(8,128)(2,1)S(1)}, bf16[768,2,128]{2,0,1:T(8,128)(2,1)S(1)}, u32[]{:S(2)}, u32[]{:S(2)}) collective-permute-start(bf16[768,2,128]{2,0,1:T(8,128)(2,1)S(1)} %get-tuple-element.50), channel_id=1, source_target_pairs={{0,2},{1,3},{2,4},{3,5},{4,6},{5,7},{6,0},{7,1},{8,10},{9,11},{10,... | collective-permute-start | bytes 1179656 | tf_op jit(solution)/shard_map/ppermute | solution.py:35
  231.6 19.3 %collective-permute-start.15 = (bf16[768,2,128]{2,0,1:T(8,128)(2,1)S(1)}, bf16[768,2,128]{2,0,1:T(8,128)(2,1)S(1)}, u32[]{:S(2)}, u32[]{:S(2)}) collective-permute-start(bf16[768,2,128]{2,0,1:T(8,128)(2,1)S(1)} %get-tuple-element.51), channel_id=1, source_target_pairs={{0,6},{1,7},{2,0},{3,1},{4,2},{5,3},{6,4},{7,5},{8,14},{9,15},{10,... | collective-permute-start | bytes 1179656 | tf_op jit(solution)/shard_map/ppermute | solution.py:35
  233.6 18.5 %collective-permute-start.14 = (bf16[768,2,128]{2,0,1:T(8,128)(2,1)S(1)}, bf16[768,2,128]{2,0,1:T(8,128)(2,1)S(1)}, u32[]{:S(2)}, u32[]{:S(2)}) collective-permute-start(bf16[768,2,128]{2,0,1:T(8,128)(2,1)S(1)} %get-tuple-element.52), channel_id=1, source_target_pairs={{0,4},{1,5},{2,6},{3,7},{4,0},{5,1},{6,2},{7,3},{8,12},{9,13},{10,... | collective-permute-start | bytes 1179656 | tf_op jit(solution)/shard_map/ppermute | solution.py:35
  253.4 8.1 %collective-permute-start.16 = (bf16[768,128]{1,0:T(8,128)(2,1)S(1)}, bf16[768,128]{1,0:T(8,128)(2,1)S(1)}, u32[]{:S(2)}, u32[]{:S(2)}) collective-permute-start(bf16[768,128]{1,0:T(8,128)(2,1)S(1)} %select_bitcast_fusion.9), channel_id=1, source_target_pairs={{0,8},{1,9},{2,10},{3,11},{4,12},{5,13},{6,14},{7,15},{8,0},{9,1},... | collective-permute-start | bytes 589832 | tf_op jit(solution)/shard_map/ppermute | solution.py:25
  261.6 7.3 %collective-permute-start.17 = (bf16[768,128]{1,0:T(8,128)(2,1)S(1)}, bf16[768,128]{1,0:T(8,128)(2,1)S(1)}, u32[]{:S(2)}, u32[]{:S(2)}) collective-permute-start(bf16[768,128]{1,0:T(8,128)(2,1)S(1)} %fusion.35), channel_id=1, source_target_pairs={{0,8},{1,9},{2,10},{3,11},{4,12},{5,13},{6,14},{7,15},{8,0},{9,1},... | collective-permute-start | bytes 589832 | tf_op jit(solution)/shard_map/ppermute | solution.py:25
  268.9 18.8 %collective-permute-start.20 = (bf16[768,2,128]{2,0,1:T(8,128)(2,1)S(1)}, bf16[768,2,128]{2,0,1:T(8,128)(2,1)S(1)}, u32[]{:S(2)}, u32[]{:S(2)}) collective-permute-start(bf16[768,2,128]{2,0,1:T(8,128)(2,1)S(1)} %maximum_select_fusion.5), channel_id=1, source_target_pairs={{0,2},{1,3},{2,4},{3,5},{4,6},{5,7},{6,0},{7,1},{8,10},{9,11},{10,... | collective-permute-start | bytes 1179656 | tf_op jit(solution)/shard_map/ppermute | solution.py:35
  269.8 17.9 %collective-permute-start.19 = (bf16[768,2,128]{2,0,1:T(8,128)(2,1)S(1)}, bf16[768,2,128]{2,0,1:T(8,128)(2,1)S(1)}, u32[]{:S(2)}, u32[]{:S(2)}) collective-permute-start(bf16[768,2,128]{2,0,1:T(8,128)(2,1)S(1)} %maximum_select_fusion.5), channel_id=1, source_target_pairs={{0,4},{1,5},{2,6},{3,7},{4,0},{5,1},{6,2},{7,3},{8,12},{9,13},{10,... | collective-permute-start | bytes 1179656 | tf_op jit(solution)/shard_map/ppermute | solution.py:35
  272.1 16.2 %collective-permute-start.18 = (bf16[768,2,128]{2,0,1:T(8,128)(2,1)S(1)}, bf16[768,2,128]{2,0,1:T(8,128)(2,1)S(1)}, u32[]{:S(2)}, u32[]{:S(2)}) collective-permute-start(bf16[768,2,128]{2,0,1:T(8,128)(2,1)S(1)} %maximum_select_fusion.5), channel_id=1, source_target_pairs={{0,6},{1,7},{2,0},{3,1},{4,2},{5,3},{6,4},{7,5},{8,14},{9,15},{10,... | collective-permute-start | bytes 1179656 | tf_op jit(solution)/shard_map/ppermute | solution.py:35
  293.5 6.9 %collective-permute-start.21 = (bf16[768,2,4,128]{3,0,1,2:T(8,128)(2,1)}, bf16[768,2,4,128]{3,0,1,2:T(8,128)(2,1)}, u32[]{:S(2)}, u32[]{:S(2)}) collective-permute-start(bf16[768,2,4,128]{3,0,1,2:T(8,128)(2,1)} %bitcast_select_fusion.3), channel_id=1, source_target_pairs={{0,1},{1,0},{2,3},{3,2},{4,5},{5,4},{6,7},{7,6},{8,9},{9,8},{10,11... | collective-permute-start | bytes 4718600 | tf_op jit(solution)/shard_map/ppermute | solution.py:25
  353.9 25.7 %collective-permute-start.22 = (bf16[1,2048]{1,0:T(2,128)(2,1)S(1)}, bf16[1,2048]{1,0:T(2,128)(2,1)S(1)}, u32[]{:S(2)}, u32[]{:S(2)}) collective-permute-start(bf16[1,2048]{1,0:T(2,128)(2,1)S(1)} %slice.451), channel_id=1, source_target_pairs={{0,16},{16,32},{32,48},{48,64},{64,80},{80,96},{96,112},{1,17},{17... | collective-permute-start | bytes 12296 | tf_op jit(solution)/shard_map/ppermute | solution.py:20
  364.0 90.0 %collective-permute-start.35 = (f32[3,2,4224]{2,1,0:T(2,128)S(1)}, f32[3,2,4224]{2,1,0:T(2,128)S(1)}, u32[]{:S(2)}, u32[]{:S(2)}) collective-permute-start(f32[3,2,4224]{2,1,0:T(2,128)S(1)} %maximum_maximum_fusion), channel_id=1, source_target_pairs={{32,0},{48,16},{64,32},{80,48},{96,64},{112,80},{33,1},{49,17},{65... | collective-permute-start | bytes 304136 | tf_op jit(solution)/shard_map/ppermute | solution.py:20
  365.3 78.6 %collective-permute-start.34 = (f32[3,2,4224]{2,1,0:T(2,128)S(1)}, f32[3,2,4224]{2,1,0:T(2,128)S(1)}, u32[]{:S(2)}, u32[]{:S(2)}) collective-permute-start(f32[3,2,4224]{2,1,0:T(2,128)S(1)} %maximum_maximum_fusion), channel_id=1, source_target_pairs={{16,0},{32,16},{48,32},{64,48},{80,64},{96,80},{112,96},{17,1},{33... | collective-permute-start | bytes 304136 | tf_op jit(solution)/shard_map/ppermute | solution.py:20
  367.7 76.1 %collective-permute-start.33 = (f32[3,2,4224]{2,1,0:T(2,128)S(1)}, f32[3,2,4224]{2,1,0:T(2,128)S(1)}, u32[]{:S(2)}, u32[]{:S(2)}) collective-permute-start(f32[3,2,4224]{2,1,0:T(2,128)S(1)} %maximum_maximum_fusion), channel_id=1, source_target_pairs={{0,16},{16,32},{32,48},{48,64},{64,80},{80,96},{96,112},{1,17},{17... | collective-permute-start | bytes 304136 | tf_op jit(solution)/shard_map/ppermute | solution.py:20
  371.7 48.3 %collective-permute-start.32 = (f32[3,2,4224]{2,1,0:T(2,128)S(1)}, f32[3,2,4224]{2,1,0:T(2,128)S(1)}, u32[]{:S(2)}, u32[]{:S(2)}) collective-permute-start(f32[3,2,4224]{2,1,0:T(2,128)S(1)} %maximum_maximum_fusion), channel_id=1, source_target_pairs={{0,32},{16,48},{32,64},{48,80},{64,96},{80,112},{1,33},{17,49},{33... | collective-permute-start | bytes 304136 | tf_op jit(solution)/shard_map/ppermute | solution.py:20
  443.7 3.5 collective-permute-start.23
  449.0 27.3 %copy-start.38 = (pred[4]{0:T(512)(128)(4,1)S(1)}, pred[4]{0:T(512)(128)(4,1)}, u32[]{:S(2)}) copy-start(pred[4]{0:T(512)(128)(4,1)} %copy-done.37) | copy-start | bytes 16
  449.0 27.3 %copy-start.40 = (pred[4]{0:T(512)(128)(4,1)S(1)}, pred[4]{0:T(512)(128)(4,1)}, u32[]{:S(2)}) copy-start(pred[4]{0:T(512)(128)(4,1)} %copy-done.39) | copy-start | bytes 16
  449.9 12.9 %collective-permute-start.24 = (bf16[768,2,128]{2,0,1:T(8,128)(2,1)}, bf16[768,2,128]{2,0,1:T(8,128)(2,1)S(1)}, u32[]{:S(2)}, u32[]{:S(2)}) collective-permute-start(bf16[768,2,128]{2,0,1:T(8,128)(2,1)} %get-tuple-element.47), channel_id=1, source_target_pairs={{0,2},{1,3},{2,4},{3,5},{4,6},{5,7},{6,0},{7,1},{8,10},{9,11},{10,... | collective-permute-start | bytes 1179656 | tf_op jit(solution)/shard_map/ppermute | solution.py:35
  450.5 19.7 %collective-permute-start.26 = (bf16[768,2,128]{2,0,1:T(8,128)(2,1)S(1)}, bf16[768,2,128]{2,0,1:T(8,128)(2,1)S(1)}, u32[]{:S(2)}, u32[]{:S(2)}) collective-permute-start(bf16[768,2,128]{2,0,1:T(8,128)(2,1)S(1)} %get-tuple-element.48), channel_id=1, source_target_pairs={{0,6},{1,7},{2,0},{3,1},{4,2},{5,3},{6,4},{7,5},{8,14},{9,15},{10,... | collective-permute-start | bytes 1179656 | tf_op jit(solution)/shard_map/ppermute | solution.py:35
  453.4 18.6 %collective-permute-start.25 = (bf16[768,2,128]{2,0,1:T(8,128)(2,1)S(1)}, bf16[768,2,128]{2,0,1:T(8,128)(2,1)}, u32[]{:S(2)}, u32[]{:S(2)}) collective-permute-start(bf16[768,2,128]{2,0,1:T(8,128)(2,1)S(1)} %get-tuple-element.49), channel_id=1, source_target_pairs={{0,4},{1,5},{2,6},{3,7},{4,0},{5,1},{6,2},{7,3},{8,12},{9,13},{10,... | collective-permute-start | bytes 1179656 | tf_op jit(solution)/shard_map/ppermute | solution.py:35
  454.1 48.8 %copy-start.1 = (bf16[2048,160]{0,1:T(8,128)(2,1)S(1)}, bf16[2048,160]{0,1:T(8,128)(2,1)}, u32[]{:S(2)}) copy-start(bf16[2048,160]{0,1:T(8,128)(2,1)} %param.26) | copy-start | bytes 1966084
  455.1 46.8 %copy-start.46 = (pred[1024]{0:T(1024)(128)(4,1)S(1)}, pred[1024]{0:T(1024)(128)(4,1)}, u32[]{:S(2)}) copy-start(pred[1024]{0:T(1024)(128)(4,1)} %broadcast_in_dim.199) | copy-start | bytes 3076
  455.1 46.8 %copy-start.47 = (pred[1024]{0:T(1024)(128)(4,1)S(1)}, pred[1024]{0:T(1024)(128)(4,1)}, u32[]{:S(2)}) copy-start(pred[1024]{0:T(1024)(128)(4,1)} %broadcast_in_dim.196) | copy-start | bytes 3076
  473.4 7.7 %collective-permute-start.27 = (bf16[768,128]{1,0:T(8,128)(2,1)S(1)}, bf16[768,128]{1,0:T(8,128)(2,1)S(1)}, u32[]{:S(2)}, u32[]{:S(2)}) collective-permute-start(bf16[768,128]{1,0:T(8,128)(2,1)S(1)} %select_bitcast_fusion.8), channel_id=1, source_target_pairs={{0,8},{1,9},{2,10},{3,11},{4,12},{5,13},{6,14},{7,15},{8,0},{9,1},... | collective-permute-start | bytes 589832 | tf_op jit(solution)/shard_map/ppermute | solution.py:25
  482.2 11.8 %collective-permute-start.29 = (bf16[3,256,128]{2,1,0:T(8,128)(2,1)S(1)}, bf16[3,256,128]{2,1,0:T(8,128)(2,1)S(1)}, u32[]{:S(2)}, u32[]{:S(2)}) collective-permute-start(bf16[3,256,128]{2,1,0:T(8,128)(2,1)S(1)} %bitcast.320), channel_id=1, source_target_pairs={{0,16},{16,32},{32,48},{48,64},{64,80},{80,96},{96,112},{1,17},{17... | collective-permute-start | bytes 589832 | tf_op jit(solution)/shard_map/ppermute | solution.py:20
  484.2 9.8 %collective-permute-start.28 = (bf16[3,256,128]{2,1,0:T(8,128)(2,1)S(1)}, bf16[3,256,128]{2,1,0:T(8,128)(2,1)S(1)}, u32[]{:S(2)}, u32[]{:S(2)}) collective-permute-start(bf16[3,256,128]{2,1,0:T(8,128)(2,1)S(1)} %bitcast.321), channel_id=1, source_target_pairs={{0,32},{16,48},{32,64},{48,80},{64,96},{80,112},{1,33},{17,49},{33... | collective-permute-start | bytes 589832 | tf_op jit(solution)/shard_map/ppermute | solution.py:20
  488.8 12.3 %collective-permute-start.31 = (bf16[3,256,128]{2,1,0:T(8,128)(2,1)S(1)}, bf16[3,256,128]{2,1,0:T(8,128)(2,1)S(1)}, u32[]{:S(2)}, u32[]{:S(2)}) collective-permute-start(bf16[3,256,128]{2,1,0:T(8,128)(2,1)S(1)} %bitcast.322), channel_id=1, source_target_pairs={{32,0},{48,16},{64,32},{80,48},{96,64},{112,80},{33,1},{49,17},{65... | collective-permute-start | bytes 589832 | tf_op jit(solution)/shard_map/ppermute | solution.py:20
  490.1 11.0 %collective-permute-start.30 = (bf16[3,256,128]{2,1,0:T(8,128)(2,1)S(1)}, bf16[3,256,128]{2,1,0:T(8,128)(2,1)S(1)}, u32[]{:S(2)}, u32[]{:S(2)}) collective-permute-start(bf16[3,256,128]{2,1,0:T(8,128)(2,1)S(1)} %bitcast.323), channel_id=1, source_target_pairs={{16,0},{32,16},{48,32},{64,48},{80,64},{96,80},{112,96},{17,1},{33... | collective-permute-start | bytes 589832 | tf_op jit(solution)/shard_map/ppermute | solution.py:20
  (51 other events, 338.6 us)
Sparse Core Ops, SparseCore 0:
  25.9 42.8 all-gather.2
  300.0 57.9 all-gather.4

commit v7 on v4

--- a/solution.py
+++ b/solution.py
@@ -37,26 +37,22 @@
 
 def hier_reduce_scatter(partial, axis):
     h = lax.axis_index(axis)
-    rows, width = partial.shape
-    W = width // 16
     core = h % 2
     z = (h // 2) % 4
     yh = h // 8
-    blocks = partial.reshape(rows, 2, 4, 2, W)
-    mine = jnp.where(core == 0, blocks[:, :, :, 0], blocks[:, :, :, 1])
-    other = jnp.where(core == 0, blocks[:, :, :, 1], blocks[:, :, :, 0])
-    acc = mine.astype(jnp.float32) + _swap(other, axis, 1).astype(jnp.float32)
-    acc = acc.astype(jnp.bfloat16)
-    zsel = lambda a, k: jnp.take(a, k, axis=2)
-    total = zsel(acc, z).astype(jnp.float32)
+    _, rows, width = partial.shape
+    blocks = partial.reshape(2, 4, 2, rows, width)
+    mine = jnp.where(core == 0, blocks[:, :, 0], blocks[:, :, 1])
+    other = jnp.where(core == 0, blocks[:, :, 1], blocks[:, :, 0])
+    acc = (mine.astype(jnp.float32) + _swap(other, axis, 1).astype(jnp.float32)).astype(jnp.bfloat16)
+    total = jnp.take(acc, z, axis=1).astype(jnp.float32)
     for step in (1, 2, 3):
-        send = zsel(acc, (z + step) % 4)
+        send = jnp.take(acc, (z + step) % 4, axis=1)
         total = total + _ring(send, axis, step).astype(jnp.float32)
     total = total.astype(jnp.bfloat16)
-    keep = jnp.where(yh == 0, total[:, 0], total[:, 1])
-    give = jnp.where(yh == 0, total[:, 1], total[:, 0])
-    result = keep.astype(jnp.float32) + _swap(give, axis, 8).astype(jnp.float32)
-    return result
+    keep = jnp.where(yh == 0, total[0], total[1])
+    give = jnp.where(yh == 0, total[1], total[0])
+    return keep.astype(jnp.float32) + _swap(give, axis, 8).astype(jnp.float32)
 
 
 def hier_all_gather(piece, axis):
@@ -65,13 +61,13 @@
     z = (h // 2) % 4
     yh = h // 8
     got = _swap(piece, axis, 8)
-    pair = jnp.where(yh == 0, jnp.stack([piece, got], 1), jnp.stack([got, piece], 1))
+    pair = jnp.where(yh == 0, jnp.stack([piece, got]), jnp.stack([got, piece]))
     ring_parts = [pair] + [_ring(pair, axis, -step % 4) for step in (1, 2, 3)]
-    stacked = jnp.stack(ring_parts, 2)
-    by_z = jnp.take(stacked, (jnp.arange(4) - z) % 4, axis=2)
+    stacked = jnp.stack(ring_parts, 1)
+    by_z = jnp.take(stacked, (jnp.arange(4) - z) % 4, axis=1)
     partner = _swap(by_z, axis, 1)
-    both = jnp.where(core == 0, jnp.stack([by_z, partner], 3), jnp.stack([partner, by_z], 3))
-    return both.reshape(piece.shape[0], 16 * piece.shape[1])
+    both = jnp.where(core == 0, jnp.stack([by_z, partner], 2), jnp.stack([partner, by_z], 2))
+    return both.reshape((16,) + piece.shape)
 
 
 def layer_norm(value_rows):
@@ -264,11 +260,17 @@
     page_end = page_end + page_factor[:, :, :, None] * incoming[None]
     attended = block_out.transpose(0, 2, 1, 3).reshape(slot_rows, features_on_shard)
     normed = (group_norm(attended) * attender_scaling_coefs * gating).astype(jnp.bfloat16)
-    mixer_partial = lax.dot_general(
-        normed, output_weight_t, (((1,), (1,)), ((), ())), preferred_element_type=jnp.float32
+    head_count = lax.axis_size("head")
+    mixer_partial = jnp.einsum(
+        "rc,bfc->brf",
+        normed,
+        output_weight_t.reshape(head_count, -1, output_weight_t.shape[1]),
+        preferred_element_type=jnp.float32,
     ).astype(jnp.bfloat16)
     mixer_owned = hier_reduce_scatter(mixer_partial, "head").astype(jnp.bfloat16)
-    mixer_total = hier_all_gather(mixer_owned, "head").astype(jnp.float32)
+    mixer_total = (
+        hier_all_gather(mixer_owned, "head").transpose(1, 0, 2).reshape(slot_rows, full_width)
+    ).astype(jnp.float32)
     residual = (embedded.astype(jnp.float32) + mixer_total).astype(jnp.bfloat16)
     last_residual = residual[slot_rows - 1 : slot_rows]
     arriving = passed_along(last_residual, "group", 1)
@@ -288,8 +290,11 @@
     key_raw = jnp.dot(key_input, key_weight, preferred_element_type=jnp.float32)
     squared = jnp.square(jax.nn.relu(key_raw)).astype(jnp.bfloat16)
     channel = hier_reduce_scatter(
-        lax.dot_general(
-            squared, value_weight_t, (((1,), (1,)), ((), ())), preferred_element_type=jnp.float32
+        jnp.einsum(
+            "rk,bfk->brf",
+            squared,
+            value_weight_t.reshape(head_count, -1, value_weight_t.shape[1]),
+            preferred_element_type=jnp.float32,
         ).astype(jnp.bfloat16),
         "head",
     )

time: 425 us -> 395 us (0.929)
  local copies, waits for them, and re-layouts: 76.4 us -> 59.6 us
  matrix products: 63.1 us -> 58.6 us
    convert_element_type x4 -> x1, local copies, waits for them, and re-layouts: 22.8 us -> 0.55 us  [per_device(): mixer_total = hier_all_gather(mixer_owned, 'head').transpose(1, 0, 2).res...]
    unnamed x80 -> x98, local copies, waits for them, and re-layouts: 16 us -> 21.2 us
  transfers between devices with their start and end apart: 38 -> 38, of which waited for: 17 -> 14; matrix products, arithmetic and copies ran while one was open for 30% -> 27% of each run, Pallas kernels for 0% -> 0%
where the time goes in v7:
time: 395 us; the launch traced here: 389 us
  waiting for transfers between devices  118 us (30%)
  starting transfers between devices  76.6 us (19%)
  local copies, waits for them, and re-layouts  59.6 us (15%)
  matrix products  58.6 us (15%)
  other arithmetic  58.2 us (15%)
  between operations  17.6 us (4%)
    ppermute x20, starting transfers between devices, passed_along(): lax.ppermute(value, axis, [(source, source + steps) for source in range(i...  55.9 us
    all_gather x1, waiting for transfers between devices, per_device(): gathered_rows = lax.all_gather(own_rows, 'head', axis=1, tiled=True)  43.9 us
    ppermute x9, waiting for transfers between devices, _ring(): return lax.ppermute(value, axis, pairs)  38.5 us
    unnamed x98, local copies, waits for them, and re-layouts  21.2 us
    ppermute x6, waiting for transfers between devices, _swap(): return lax.ppermute(value, axis, [(s, s ^ flip) for s in range(count)])  18.2 us
    ppermute x20, waiting for transfers between devices, passed_along(): lax.ppermute(value, axis, [(source, source + steps) for source in range(i...  17.5 us
    dot_general x3, matrix products, mixed_inputs(): jnp.dot(column_part, blend_widening_maps[number], preferred_element_type=...  15.8 us
    ppermute x9, starting transfers between devices, _ring(): return lax.ppermute(value, axis, pairs)  12.4 us
  transfers between devices with their start and end apart: 38, of which 14 were waited for; matrix products, arithmetic and copies ran while one was open for 27% of the time, Pallas kernels for 0%

profile of v7, /device:TPU:2, one launch (start us, length us, event | category | flops | bytes accessed | tf_op | source)
XLA Modules:
  0.0 388.9 jit_solution(9341575268641893501)
XLA Ops:
  10.6 9.8 %gather_fusion.2 = bf16[776,128]{1,0:T(8,128)(2,1)S(1)} fusion(bf16[65536,128]{1,0:T(8,128)(2,1)} %param.20, s32[1024]{0:T(1024)S(1)} %pad_clamp_fusion.3), kind=kCustom, calls=%fused_computation.4 | custom fusion | bytes 400416 | tf_op jit(solution)/shard_map/jit(_take)/gather | solution.py:157
  31.8 43.9 %all-gather.4.cloned.1.call-done = bf16[776,2048]{1,0:T(8,128)(2,1)} async-done(((bf16[776,128]{1,0:T(8,128)(2,1)}), bf16[776,2048]{1,0:T(8,128)(2,1)}) %all-gather.4.cloned.1.call-update) | async-done | bytes 3178512 | tf_op jit(solution)/shard_map/all_gather | solution.py:158
  81.5 2.6 fusion.2
  92.2 6.2 %fusion.34 = bf16[768,64]{0,1:T(8,128)(2,1)S(1)} fusion(bf16[2048,64]{0,1:T(8,128)(2,1)S(1)} %copy-done.35, f32[768,2048]{1,0:T(8,128)} %copy-done.6, f32[2048]{0:T(1024)S(1)} %bitcast.347, f32[768]{0:T(1024)S(1)} %add_rsqrt_fusion.1, f32[768]{0:T(1024)S(1)} %broadcast_multiply_fusion.2, bf16[5,32,2048]{2,1,0:T(8,128)(2,1)} %param.27, ...), kind=kOutput, calls=%fused_computation.79 | convolution fusion | flops 313049088 | bytes 9994240 | tf_op jit(solution)/shard_map/dot_general | solution.py:100
  108.2 7.3 %add_convert_fusion.3 = bf16[768,2048]{1,0:T(8,128)(2,1)} fusion(f32[768,2048]{1,0:T(8,128)} %copy-done.6, f32[2048]{0:T(1024)S(1)} %bitcast.341, f32[768]{0:T(1024)S(1)} %add_rsqrt_fusion.1, f32[768]{0:T(1024)S(1)} %broadcast_multiply_fusion.2, bf16[5,32,2048]{2,1,0:T(8,128)(2,1)} %param.27, bf16[768,160]{0,1:T(8,128)(2,1)} %copy-done.18, ...), kind=kOutput, calls=%fused_computation.28 | convolution fusion | flops 111673344 | bytes 12777472 | tf_op jit(solution)/shard_map/dot_general | solution.py:89
  115.5 4.2 %add_convert_fusion.4 = bf16[768,2048]{1,0:T(8,128)(2,1)} fusion(f32[768,2048]{1,0:T(8,128)S(1)} %bitcast.305, f32[2048]{0:T(1024)S(1)} %bitcast.340, f32[768]{0:T(1024)S(1)} %add_rsqrt_fusion.1, f32[768]{0:T(1024)S(1)} %broadcast_multiply_fusion.2, bf16[5,32,2048]{2,1,0:T(8,128)(2,1)} %param.27, bf16[768,160]{0,1:T(8,128)(2,1)S(1)} %copy-done.19, ...), kind=kOutput, calls=%fused_computation.29 | convolution fusion | flops 111673344 | bytes 12779520 | tf_op jit(solution)/shard_map/dot_general | solution.py:89
  119.7 4.3 %add_convert_fusion.6 = bf16[768,2048]{1,0:T(8,128)(2,1)} fusion(f32[768,2048]{1,0:T(8,128)S(1)} %bitcast.305, f32[2048]{0:T(1024)S(1)} %bitcast.339, f32[768]{0:T(1024)S(1)} %add_rsqrt_fusion.1, f32[768]{0:T(1024)S(1)} %broadcast_multiply_fusion.2, bf16[5,32,2048]{2,1,0:T(8,128)(2,1)} %param.27, bf16[768,160]{0,1:T(8,128)(2,1)S(1)} %copy-done.19, ...), kind=kOutput, calls=%fused_computation.31 | convolution fusion | flops 111673344 | bytes 12779520 | tf_op jit(solution)/shard_map/dot_general | solution.py:89
  126.5 3.2 fusion.113
  129.7 3.1 convolution_bitcast_fusion.4
  139.0 4.6 %collective-permute-start.5 = (f32[2,65,64]{1,2,0:T(8,128)S(1)}, f32[2,65,64]{1,2,0:T(8,128)S(1)}, u32[]{:S(2)}, u32[]{:S(2)}) collective-permute-start(f32[2,65,64]{1,2,0:T(8,128)S(1)} %pad_maximum_fusion.5), channel_id=1, source_target_pairs={{0,96},{16,112},{1,97},{17,113},{2,98},{18,114},{3,99},{19,115},{4... | collective-permute-start | bytes 99848 | tf_op jit(solution)/shard_map/ppermute | solution.py:20
  151.1 3.1 collective-permute-start.1
  154.3 3.4 collective-permute-start
  163.3 5.9 %fusion.44 = bf16[768,128,1]{1,0,2:T(8,128)(2,1)S(1)} fusion(bf16[6,2048,128]{2,1,0:T(8,128)(2,1)} %all-gather.6.cloned.1.call-done, f32[768,2048]{1,0:T(8,128)} %copy-done.6, f32[2048]{0:T(1024)S(1)} %bitcast.346, f32[768]{0:T(1024)S(1)} %add_rsqrt_fusion.1, f32[768]{0:T(1024)S(1)} %broadcast_multiply_fusion.2, f32[768,128]{1,0:T(8,128)S(1)} %copy.102, ...), kind=kOutput, calls=%fused_computation.111 | convolution fusion | flops 515211264 | bytes 11534848 | tf_op jit(solution)/shard_map/dot_general | solution.py:191
  174.1 2.6 copy.126
  176.7 2.8 select_bitcast_fusion.1
  179.7 3.6 collective-permute-done.7
  185.7 3.2 collective-permute-start.10
  190.6 16.3 %collective-permute-done.8 = bf16[2,768,128]{2,1,0:T(8,128)(2,1)S(1)} collective-permute-done((bf16[2,768,128]{2,1,0:T(8,128)(2,1)S(1)}, bf16[2,768,128]{2,1,0:T(8,128)(2,1)S(1)}, u32[]{:S(2)}, u32[]{:S(2)}) %collective-permute-start.8) | collective-permute-done | bytes 393248 | tf_op jit(solution)/shard_map/ppermute | solution.py:35
  207.2 2.4 collective-permute-start.11
  209.6 5.4 %collective-permute-done.11 = bf16[768,128]{1,0:T(8,128)(2,1)S(1)} collective-permute-done((bf16[768,128]{1,0:T(8,128)(2,1)S(1)}, bf16[768,128]{1,0:T(8,128)(2,1)S(1)}, u32[]{:S(2)}, u32[]{:S(2)}) %collective-permute-start.11) | collective-permute-done | bytes 196640 | tf_op jit(solution)/shard_map/ppermute | solution.py:25
  215.1 2.7 collective-permute-start.12
  217.8 4.5 %collective-permute-done.12 = bf16[768,128]{1,0:T(8,128)(2,1)S(1)} collective-permute-done((bf16[768,128]{1,0:T(8,128)(2,1)S(1)}, bf16[768,128]{1,0:T(8,128)(2,1)S(1)}, u32[]{:S(2)}, u32[]{:S(2)}) %collective-permute-start.12) | collective-permute-done | bytes 196640 | tf_op jit(solution)/shard_map/ppermute | solution.py:25
  223.5 3.4 collective-permute-start.14
  227.9 6.7 %collective-permute-done.15 = bf16[2,768,128]{2,1,0:T(8,128)(2,1)S(1)} collective-permute-done((bf16[2,768,128]{2,1,0:T(8,128)(2,1)S(1)}, bf16[2,768,128]{2,1,0:T(8,128)(2,1)S(1)}, u32[]{:S(2)}, u32[]{:S(2)}) %collective-permute-start.15) | collective-permute-done | bytes 393248 | tf_op jit(solution)/shard_map/ppermute | solution.py:35
  234.5 7.3 %collective-permute-done.14 = bf16[2,768,128]{2,1,0:T(8,128)(2,1)S(1)} collective-permute-done((bf16[2,768,128]{2,1,0:T(8,128)(2,1)S(1)}, bf16[2,768,128]{2,1,0:T(8,128)(2,1)S(1)}, u32[]{:S(2)}, u32[]{:S(2)}) %collective-permute-start.14) | collective-permute-done | bytes 393248 | tf_op jit(solution)/shard_map/ppermute | solution.py:35
  249.5 2.8 collective-permute-start.27
  253.6 4.6 %collective-permute-start.29 = (f32[3,2,4096]{2,1,0:T(2,128)S(1)}, f32[3,2,4096]{2,1,0:T(2,128)S(1)}, u32[]{:S(2)}, u32[]{:S(2)}) collective-permute-start(f32[3,2,4096]{2,1,0:T(2,128)S(1)} %reshape.654), channel_id=1, source_target_pairs={{16,0},{32,16},{48,32},{64,48},{80,64},{96,80},{112,96},{17,1},{33... | collective-permute-start | bytes 294920 | tf_op jit(solution)/shard_map/ppermute | solution.py:20
  258.2 4.0 %collective-permute-start.28 = (f32[3,2,4096]{2,1,0:T(2,128)S(1)}, f32[3,2,4096]{2,1,0:T(2,128)S(1)}, u32[]{:S(2)}, u32[]{:S(2)}) collective-permute-start(f32[3,2,4096]{2,1,0:T(2,128)S(1)} %reshape.654), channel_id=1, source_target_pairs={{0,16},{16,32},{32,48},{48,64},{64,80},{80,96},{96,112},{1,17},{17... | collective-permute-start | bytes 294920 | tf_op jit(solution)/shard_map/ppermute | solution.py:20
  262.2 5.2 %collective-permute-done.28 = f32[3,2,4096]{2,1,0:T(2,128)S(1)} collective-permute-done((f32[3,2,4096]{2,1,0:T(2,128)S(1)}, f32[3,2,4096]{2,1,0:T(2,128)S(1)}, u32[]{:S(2)}, u32[]{:S(2)}) %collective-permute-start.28) | collective-permute-done | bytes 98336 | tf_op jit(solution)/shard_map/ppermute | solution.py:20
  267.7 2.7 fusion.9
  273.2 3.2 collective-permute-start.17
  278.1 2.6 copy-done.9
  283.5 3.7 pad_maximum_fusion.1
  287.2 3.6 bitcast_subtract_fusion
  292.9 9.6 %convolution_convert_fusion.1 = bf16[16,128,768]{2,1,0:T(8,128)(2,1)} fusion(bf16[16,128,448]{1,0,2:T(8,128)(2,1)S(1)} %bitcast.322, bf16[2,2048,448]{1,2,0:T(8,128)(2,1)} %all-gather.8.cloned.1.call-done, f32[768,2048]{1,0:T(8,128)} %bitcast_subtract_fusion, f32[2048]{0:T(1024)S(1)} %bitcast.345, bf16[768,2048]{1,0:T(8,128)(2,1)} %copy-done.7, ...), kind=kOutput, calls=%fused_computation.45 | convolution fusion | flops 2830614528 | bytes 16267264 | tf_op jit(solution)/shard_map/rk,bfk->brf/dot_general | solution.py:293
  302.5 3.8 fusion.107
  308.3 2.6 copy.128
  310.9 2.8 select_bitcast_fusion
  315.4 7.1 %collective-permute-start.31 = (f32[3,2,128]{2,1,0:T(2,128)S(1)}, f32[3,2,128]{2,1,0:T(2,128)S(1)}, u32[]{:S(2)}, u32[]{:S(2)}) collective-permute-start(f32[3,2,128]{2,1,0:T(2,128)S(1)} %pad_maximum_fusion.6), channel_id=1, source_target_pairs={{0,32},{16,48},{32,64},{48,80},{64,96},{80,112},{1,33},{17,49},{33... | collective-permute-start | bytes 9224 | tf_op jit(solution)/shard_map/ppermute | solution.py:20
  331.2 3.9 %collective-permute-start.32 = (f32[3,2,128]{2,1,0:T(2,128)S(1)}, f32[3,2,128]{2,1,0:T(2,128)S(1)}, u32[]{:S(2)}, u32[]{:S(2)}) collective-permute-start(f32[3,2,128]{2,1,0:T(2,128)S(1)} %pad_maximum_fusion.6), channel_id=1, source_target_pairs={{0,16},{16,32},{32,48},{48,64},{64,80},{80,96},{96,112},{1,17},{17... | collective-permute-start | bytes 9224 | tf_op jit(solution)/shard_map/ppermute | solution.py:20
  338.6 7.3 %collective-permute-done.21 = bf16[2,768,128]{2,1,0:T(8,128)(2,1)S(1)} collective-permute-done((bf16[2,768,128]{2,1,0:T(8,128)(2,1)S(1)}, bf16[2,768,128]{2,1,0:T(8,128)(2,1)S(1)}, u32[]{:S(2)}, u32[]{:S(2)}) %collective-permute-start.21) | collective-permute-done | bytes 393248 | tf_op jit(solution)/shard_map/ppermute | solution.py:35
  347.1 2.9 collective-permute-start.22
  350.5 4.8 %collective-permute-done.22 = bf16[768,128]{1,0:T(8,128)(2,1)S(1)} collective-permute-done((bf16[768,128]{1,0:T(8,128)(2,1)S(1)}, bf16[768,128]{1,0:T(8,128)(2,1)S(1)}, u32[]{:S(2)}, u32[]{:S(2)}) %collective-permute-start.22) | collective-permute-done | bytes 196640 | tf_op jit(solution)/shard_map/ppermute | solution.py:25
  355.3 5.3 %fusion.37 = bf16[768,128]{1,0:T(8,128)(2,1)S(1)} fusion(bf16[768,128]{1,0:T(8,128)(2,1)S(1)} %collective-permute-done.22, bf16[768,2048]{1,0:T(8,128)(2,1)} %copy-done.7, s32[]{:T(128)S(6)} %select_n.416, pred[]{:T(512)S(6)} %eq.58, bf16[2,768,128]{2,1,0:T(8,128)(2,1)S(1)} %add_convert_fusion.31, bf16[6,2048,128]{2,1,0:T(8,128)(2,1)} %all-gather.6.cloned.1.call-done, ...), kind=kOutput, calls=%fused_computation.95 | convolution fusion | flops 413171712 | bytes 10958853 | tf_op jit(solution)/shard_map/dot_general | solution.py:289
  360.6 2.9 collective-permute-start.24
  363.6 3.1 collective-permute-start.23
  368.6 2.9 collective-permute-start.25
  371.6 8.8 %collective-permute-done.25 = bf16[3,256,128]{2,1,0:T(8,128)(2,1)S(1)} collective-permute-done((bf16[3,256,128]{2,1,0:T(8,128)(2,1)S(1)}, bf16[3,256,128]{2,1,0:T(8,128)(2,1)S(1)}, u32[]{:S(2)}, u32[]{:S(2)}) %collective-permute-start.25) | collective-permute-done | bytes 196640 | tf_op jit(solution)/shard_map/ppermute | solution.py:20
  (310 shorter events, 108.7 us)
Async XLA Ops:
  7.2 82.4 %copy-start = (bf16[2048,160]{0,1:T(8,128)(2,1)S(1)}, bf16[2048,160]{0,1:T(8,128)(2,1)}, u32[]{:S(2)}) copy-start(bf16[2048,160]{0,1:T(8,128)(2,1)} %param.26) | copy-start | bytes 1966084
  7.2 18.5 %copy-start.17 = (f32[128,256]{1,0:T(8,128)S(1)}, f32[128,256]{1,0:T(8,128)}, u32[]{:S(2)}) copy-start(f32[128,256]{1,0:T(8,128)} %param.23) | copy-start | bytes 393220
  7.2 18.6 %copy-start.13 = (f32[5,256,128]{2,1,0:T(8,128)S(1)}, f32[5,256,128]{2,1,0:T(8,128)}, u32[]{:S(2)}) copy-start(f32[5,256,128]{2,1,0:T(8,128)} %param.21) | copy-start | bytes 1966084
  7.2 68.5 %all-gather.4.cloned.1.call-start = ((), (), s32[]{:S(2)}) async-start(), calls=%async_computation | async-start | bytes 3377152 | tf_op jit(solution)/shard_map/all_gather | solution.py:158
  8.3 22.8 %copy-start.21 = (f32[8,2048]{1,0:T(8,128)S(1)}, f32[8,2048]{1,0:T(8,128)}, u32[]{:S(2)}) copy-start(f32[8,2048]{1,0:T(8,128)} %param.25) | copy-start | bytes 196612
  21.3 102.7 %all-gather.6.cloned.1.call-start = ((), (), s32[]{:S(2)}) async-start(), calls=%async_computation.1 | async-start | bytes 3538944 | tf_op jit(solution)/shard_map/all_gather | solution.py:169
  81.2 209.6 %all-gather.8.cloned.1.call-start = ((), (), s32[]{:S(2)}) async-start(), calls=%async_computation.2 | async-start | bytes 4128768 | tf_op jit(solution)/shard_map/all_gather | solution.py:171
  101.3 14.2 %slice-start = ((s8[6291456]{0:T(1024)(128)(4,1)}), s8[2097152]{0:T(1024)(128)(4,1)S(1)}, s32[]{:S(2)}) async-start(s8[6291456]{0:T(1024)(128)(4,1)} %bitcast.304), calls=%async_computation.3 | async-start | bytes 4194304
  138.2 22.5 %copy-start.31 = (f32[6,2,64]{2,1,0:T(2,128)S(1)}, f32[6,2,64]{2,1,0:T(2,128)}, u32[]{:S(2)}) copy-start(f32[6,2,64]{2,1,0:T(2,128)} %copy-done.30) | copy-start | bytes 9220
  138.3 12.8 %collective-permute-start.6 = (f32[2,65,64]{1,2,0:T(8,128)S(1)}, f32[2,65,64]{1,2,0:T(8,128)S(1)}, u32[]{:S(2)}, u32[]{:S(2)}) collective-permute-start(f32[2,65,64]{1,2,0:T(8,128)S(1)} %pad_maximum_fusion.5), channel_id=1, source_target_pairs={{0,112},{1,113},{2,114},{3,115},{4,116},{5,117},{6,118},{7,119},{8... | collective-permute-start | bytes 99848 | tf_op jit(solution)/shard_map/ppermute | solution.py:20
  139.0 15.4 %collective-permute-start.5 = (f32[2,65,64]{1,2,0:T(8,128)S(1)}, f32[2,65,64]{1,2,0:T(8,128)S(1)}, u32[]{:S(2)}, u32[]{:S(2)}) collective-permute-start(f32[2,65,64]{1,2,0:T(8,128)S(1)} %pad_maximum_fusion.5), channel_id=1, source_target_pairs={{0,96},{16,112},{1,97},{17,113},{2,98},{18,114},{3,99},{19,115},{4... | collective-permute-start | bytes 99848 | tf_op jit(solution)/shard_map/ppermute | solution.py:20
  143.6 14.3 %collective-permute-start.4 = (f32[2,65,64]{1,2,0:T(8,128)S(1)}, f32[2,65,64]{1,2,0:T(8,128)S(1)}, u32[]{:S(2)}, u32[]{:S(2)}) collective-permute-start(f32[2,65,64]{1,2,0:T(8,128)S(1)} %pad_maximum_fusion.5), channel_id=1, source_target_pairs={{0,80},{16,96},{32,112},{1,81},{17,97},{33,113},{2,82},{18,98},{34... | collective-permute-start | bytes 99848 | tf_op jit(solution)/shard_map/ppermute | solution.py:20
  144.9 13.1 %collective-permute-start.3 = (f32[2,65,64]{1,2,0:T(8,128)S(1)}, f32[2,65,64]{1,2,0:T(8,128)S(1)}, u32[]{:S(2)}, u32[]{:S(2)}) collective-permute-start(f32[2,65,64]{1,2,0:T(8,128)S(1)} %pad_maximum_fusion.5), channel_id=1, source_target_pairs={{0,64},{16,80},{32,96},{48,112},{1,65},{17,81},{33,97},{49,113},{2... | collective-permute-start | bytes 99848 | tf_op jit(solution)/shard_map/ppermute | solution.py:20
  146.2 12.0 %collective-permute-start.2 = (f32[2,65,64]{1,2,0:T(8,128)S(1)}, f32[2,65,64]{1,2,0:T(8,128)S(1)}, u32[]{:S(2)}, u32[]{:S(2)}) collective-permute-start(f32[2,65,64]{1,2,0:T(8,128)S(1)} %pad_maximum_fusion.5), channel_id=1, source_target_pairs={{0,48},{16,64},{32,80},{48,96},{64,112},{1,49},{17,65},{33,81},{49... | collective-permute-start | bytes 99848 | tf_op jit(solution)/shard_map/ppermute | solution.py:20
  151.1 7.3 %collective-permute-start.1 = (f32[2,65,64]{1,2,0:T(8,128)S(1)}, f32[2,65,64]{1,2,0:T(8,128)S(1)}, u32[]{:S(2)}, u32[]{:S(2)}) collective-permute-start(f32[2,65,64]{1,2,0:T(8,128)S(1)} %pad_maximum_fusion.5), channel_id=1, source_target_pairs={{0,32},{16,48},{32,64},{48,80},{64,96},{80,112},{1,33},{17,49},{33... | collective-permute-start | bytes 99848 | tf_op jit(solution)/shard_map/ppermute | solution.py:20
  154.3 6.2 %collective-permute-start = (f32[2,65,64]{1,2,0:T(8,128)S(1)}, f32[2,65,64]{1,2,0:T(8,128)S(1)}, u32[]{:S(2)}, u32[]{:S(2)}) collective-permute-start(f32[2,65,64]{1,2,0:T(8,128)S(1)} %pad_maximum_fusion.5), channel_id=1, source_target_pairs={{0,16},{16,32},{32,48},{48,64},{64,80},{80,96},{96,112},{1,17},{17... | collective-permute-start | bytes 99848 | tf_op jit(solution)/shard_map/ppermute | solution.py:20
  179.5 3.8 collective-permute-start.7
  185.4 24.1 %copy-start.15 = (f32[256,448]{0,1:T(8,128)S(1)}, f32[256,448]{0,1:T(8,128)}, u32[]{:S(2)}) copy-start(f32[256,448]{0,1:T(8,128)} %param.22) | copy-start | bytes 1376260
  185.4 32.4 %copy-start.16 = (f32[448,256]{1,0:T(8,128)S(1)}, f32[448,256]{1,0:T(8,128)}, u32[]{:S(2)}) copy-start(f32[448,256]{1,0:T(8,128)} %param.24) | copy-start | bytes 1376260
  185.6 21.3 %collective-permute-start.8 = (bf16[2,768,128]{2,1,0:T(8,128)(2,1)S(1)}, bf16[2,768,128]{2,1,0:T(8,128)(2,1)S(1)}, u32[]{:S(2)}, u32[]{:S(2)}) collective-permute-start(bf16[2,768,128]{2,1,0:T(8,128)(2,1)S(1)} %get-tuple-element.51), channel_id=1, source_target_pairs={{0,2},{1,3},{2,4},{3,5},{4,6},{5,7},{6,0},{7,1},{8,10},{9,11},{10,... | collective-permute-start | bytes 1179656 | tf_op jit(solution)/shard_map/ppermute | solution.py:35
  185.7 21.3 %collective-permute-start.10 = (bf16[2,768,128]{2,1,0:T(8,128)(2,1)S(1)}, bf16[2,768,128]{2,1,0:T(8,128)(2,1)S(1)}, u32[]{:S(2)}, u32[]{:S(2)}) collective-permute-start(bf16[2,768,128]{2,1,0:T(8,128)(2,1)S(1)} %get-tuple-element.52), channel_id=1, source_target_pairs={{0,6},{1,7},{2,0},{3,1},{4,2},{5,3},{6,4},{7,5},{8,14},{9,15},{10,... | collective-permute-start | bytes 1179656 | tf_op jit(solution)/shard_map/ppermute | solution.py:35
  188.9 18.0 %collective-permute-start.9 = (bf16[2,768,128]{2,1,0:T(8,128)(2,1)S(1)}, bf16[2,768,128]{2,1,0:T(8,128)(2,1)S(1)}, u32[]{:S(2)}, u32[]{:S(2)}) collective-permute-start(bf16[2,768,128]{2,1,0:T(8,128)(2,1)S(1)} %get-tuple-element.53), channel_id=1, source_target_pairs={{0,4},{1,5},{2,6},{3,7},{4,0},{5,1},{6,2},{7,3},{8,12},{9,13},{10,... | collective-permute-start | bytes 1179656 | tf_op jit(solution)/shard_map/ppermute | solution.py:35
  207.2 7.8 %collective-permute-start.11 = (bf16[768,128]{1,0:T(8,128)(2,1)S(1)}, bf16[768,128]{1,0:T(8,128)(2,1)S(1)}, u32[]{:S(2)}, u32[]{:S(2)}) collective-permute-start(bf16[768,128]{1,0:T(8,128)(2,1)S(1)} %select_bitcast_fusion.9), channel_id=1, source_target_pairs={{0,8},{1,9},{2,10},{3,11},{4,12},{5,13},{6,14},{7,15},{8,0},{9,1},... | collective-permute-start | bytes 589832 | tf_op jit(solution)/shard_map/ppermute | solution.py:25
  215.1 7.3 %collective-permute-start.12 = (bf16[768,128]{1,0:T(8,128)(2,1)S(1)}, bf16[768,128]{1,0:T(8,128)(2,1)S(1)}, u32[]{:S(2)}, u32[]{:S(2)}) collective-permute-start(bf16[768,128]{1,0:T(8,128)(2,1)S(1)} %fusion.38), channel_id=1, source_target_pairs={{0,8},{1,9},{2,10},{3,11},{4,12},{5,13},{6,14},{7,15},{8,0},{9,1},... | collective-permute-start | bytes 589832 | tf_op jit(solution)/shard_map/ppermute | solution.py:25
  222.4 12.2 %collective-permute-start.15 = (bf16[2,768,128]{2,1,0:T(8,128)(2,1)S(1)}, bf16[2,768,128]{2,1,0:T(8,128)(2,1)S(1)}, u32[]{:S(2)}, u32[]{:S(2)}) collective-permute-start(bf16[2,768,128]{2,1,0:T(8,128)(2,1)S(1)} %maximum_select_fusion.2), channel_id=1, source_target_pairs={{0,2},{1,3},{2,4},{3,5},{4,6},{5,7},{6,0},{7,1},{8,10},{9,11},{10,... | collective-permute-start | bytes 1179656 | tf_op jit(solution)/shard_map/ppermute | solution.py:35
  223.5 18.3 %collective-permute-start.14 = (bf16[2,768,128]{2,1,0:T(8,128)(2,1)S(1)}, bf16[2,768,128]{2,1,0:T(8,128)(2,1)S(1)}, u32[]{:S(2)}, u32[]{:S(2)}) collective-permute-start(bf16[2,768,128]{2,1,0:T(8,128)(2,1)S(1)} %maximum_select_fusion.2), channel_id=1, source_target_pairs={{0,4},{1,5},{2,6},{3,7},{4,0},{5,1},{6,2},{7,3},{8,12},{9,13},{10,... | collective-permute-start | bytes 1179656 | tf_op jit(solution)/shard_map/ppermute | solution.py:35
  226.9 14.9 %collective-permute-start.13 = (bf16[2,768,128]{2,1,0:T(8,128)(2,1)S(1)}, bf16[2,768,128]{2,1,0:T(8,128)(2,1)S(1)}, u32[]{:S(2)}, u32[]{:S(2)}) collective-permute-start(bf16[2,768,128]{2,1,0:T(8,128)(2,1)S(1)} %maximum_select_fusion.2), channel_id=1, source_target_pairs={{0,6},{1,7},{2,0},{3,1},{4,2},{5,3},{6,4},{7,5},{8,14},{9,15},{10,... | collective-permute-start | bytes 1179656 | tf_op jit(solution)/shard_map/ppermute | solution.py:35
  246.8 20.9 %collective-permute-start.16 = (bf16[2,4,768,128]{3,2,0,1:T(8,128)(2,1)}, bf16[2,4,768,128]{3,2,0,1:T(8,128)(2,1)}, u32[]{:S(2)}, u32[]{:S(2)}) collective-permute-start(bf16[2,4,768,128]{3,2,0,1:T(8,128)(2,1)} %bitcast_select_fusion.1), channel_id=1, source_target_pairs={{0,1},{1,0},{2,3},{3,2},{4,5},{5,4},{6,7},{7,6},{8,9},{9,8},{10,11... | collective-permute-start | bytes 4718600 | tf_op jit(solution)/shard_map/ppermute | solution.py:25
  249.5 12.7 %collective-permute-start.27 = (f32[3,2,4096]{2,1,0:T(2,128)S(1)}, f32[3,2,4096]{2,1,0:T(2,128)S(1)}, u32[]{:S(2)}, u32[]{:S(2)}) collective-permute-start(f32[3,2,4096]{2,1,0:T(2,128)S(1)} %reshape.654), channel_id=1, source_target_pairs={{0,32},{16,48},{32,64},{48,80},{64,96},{80,112},{1,33},{17,49},{33... | collective-permute-start | bytes 294920 | tf_op jit(solution)/shard_map/ppermute | solution.py:20
  252.3 61.4 %collective-permute-start.30 = (f32[3,2,4096]{2,1,0:T(2,128)S(1)}, f32[3,2,4096]{2,1,0:T(2,128)S(1)}, u32[]{:S(2)}, u32[]{:S(2)}) collective-permute-start(f32[3,2,4096]{2,1,0:T(2,128)S(1)} %reshape.654), channel_id=1, source_target_pairs={{32,0},{48,16},{64,32},{80,48},{96,64},{112,80},{33,1},{49,17},{65... | collective-permute-start | bytes 294920 | tf_op jit(solution)/shard_map/ppermute | solution.py:20
  253.6 60.0 %collective-permute-start.29 = (f32[3,2,4096]{2,1,0:T(2,128)S(1)}, f32[3,2,4096]{2,1,0:T(2,128)S(1)}, u32[]{:S(2)}, u32[]{:S(2)}) collective-permute-start(f32[3,2,4096]{2,1,0:T(2,128)S(1)} %reshape.654), channel_id=1, source_target_pairs={{16,0},{32,16},{48,32},{64,48},{80,64},{96,80},{112,96},{17,1},{33... | collective-permute-start | bytes 294920 | tf_op jit(solution)/shard_map/ppermute | solution.py:20
  258.2 9.3 %collective-permute-start.28 = (f32[3,2,4096]{2,1,0:T(2,128)S(1)}, f32[3,2,4096]{2,1,0:T(2,128)S(1)}, u32[]{:S(2)}, u32[]{:S(2)}) collective-permute-start(f32[3,2,4096]{2,1,0:T(2,128)S(1)} %reshape.654), channel_id=1, source_target_pairs={{0,16},{16,32},{32,48},{48,64},{64,80},{80,96},{96,112},{1,17},{17... | collective-permute-start | bytes 294920 | tf_op jit(solution)/shard_map/ppermute | solution.py:20
  273.2 7.6 %collective-permute-start.17 = (bf16[1,2048]{1,0:T(2,128)(2,1)S(1)}, bf16[1,2048]{1,0:T(2,128)(2,1)S(1)}, u32[]{:S(2)}, u32[]{:S(2)}) collective-permute-start(bf16[1,2048]{1,0:T(2,128)(2,1)S(1)} %slice.439), channel_id=1, source_target_pairs={{0,16},{16,32},{32,48},{48,64},{64,80},{80,96},{96,112},{1,17},{17... | collective-permute-start | bytes 12296 | tf_op jit(solution)/shard_map/ppermute | solution.py:20
  313.7 8.9 %collective-permute-start.18 = (bf16[2,4,768,128]{3,2,0,1:T(8,128)(2,1)}, bf16[2,4,768,128]{3,2,0,1:T(8,128)(2,1)}, u32[]{:S(2)}, u32[]{:S(2)}) collective-permute-start(bf16[2,4,768,128]{3,2,0,1:T(8,128)(2,1)} %select_bitcast_fusion), channel_id=1, source_target_pairs={{0,1},{1,0},{2,3},{3,2},{4,5},{5,4},{6,7},{7,6},{8,9},{9,8},{10,11... | collective-permute-start | bytes 4718600 | tf_op jit(solution)/shard_map/ppermute | solution.py:25
  315.4 15.7 %collective-permute-start.31 = (f32[3,2,128]{2,1,0:T(2,128)S(1)}, f32[3,2,128]{2,1,0:T(2,128)S(1)}, u32[]{:S(2)}, u32[]{:S(2)}) collective-permute-start(f32[3,2,128]{2,1,0:T(2,128)S(1)} %pad_maximum_fusion.6), channel_id=1, source_target_pairs={{0,32},{16,48},{32,64},{48,80},{64,96},{80,112},{1,33},{17,49},{33... | collective-permute-start | bytes 9224 | tf_op jit(solution)/shard_map/ppermute | solution.py:20
  324.8 30.5 %copy-start.26 = (f32[1,2048]{1,0:T(1,128)S(1)}, f32[1,2048]{1,0:T(1,128)}, u32[]{:S(2)}) copy-start(f32[1,2048]{1,0:T(1,128)} %get-tuple-element.57) | copy-start | bytes 24580
  324.9 13.7 %collective-permute-start.19 = (bf16[2,768,128]{2,1,0:T(8,128)(2,1)S(1)}, bf16[2,768,128]{2,1,0:T(8,128)(2,1)S(1)}, u32[]{:S(2)}, u32[]{:S(2)}) collective-permute-start(bf16[2,768,128]{2,1,0:T(8,128)(2,1)S(1)} %get-tuple-element.48), channel_id=1, source_target_pairs={{0,2},{1,3},{2,4},{3,5},{4,6},{5,7},{6,0},{7,1},{8,10},{9,11},{10,... | collective-permute-start | bytes 1179656 | tf_op jit(solution)/shard_map/ppermute | solution.py:35
  326.2 19.7 %collective-permute-start.21 = (bf16[2,768,128]{2,1,0:T(8,128)(2,1)S(1)}, bf16[2,768,128]{2,1,0:T(8,128)(2,1)S(1)}, u32[]{:S(2)}, u32[]{:S(2)}) collective-permute-start(bf16[2,768,128]{2,1,0:T(8,128)(2,1)S(1)} %get-tuple-element.49), channel_id=1, source_target_pairs={{0,6},{1,7},{2,0},{3,1},{4,2},{5,3},{6,4},{7,5},{8,14},{9,15},{10,... | collective-permute-start | bytes 1179656 | tf_op jit(solution)/shard_map/ppermute | solution.py:35
  328.5 18.4 %collective-permute-start.20 = (bf16[2,768,128]{2,1,0:T(8,128)(2,1)S(1)}, bf16[2,768,128]{2,1,0:T(8,128)(2,1)S(1)}, u32[]{:S(2)}, u32[]{:S(2)}) collective-permute-start(bf16[2,768,128]{2,1,0:T(8,128)(2,1)S(1)} %get-tuple-element.50), channel_id=1, source_target_pairs={{0,4},{1,5},{2,6},{3,7},{4,0},{5,1},{6,2},{7,3},{8,12},{9,13},{10,... | collective-permute-start | bytes 1179656 | tf_op jit(solution)/shard_map/ppermute | solution.py:35
  329.9 20.1 %collective-permute-start.34 = (f32[3,2,128]{2,1,0:T(2,128)S(1)}, f32[3,2,128]{2,1,0:T(2,128)S(1)}, u32[]{:S(2)}, u32[]{:S(2)}) collective-permute-start(f32[3,2,128]{2,1,0:T(2,128)S(1)} %pad_maximum_fusion.6), channel_id=1, source_target_pairs={{32,0},{48,16},{64,32},{80,48},{96,64},{112,80},{33,1},{49,17},{65... | collective-permute-start | bytes 9224 | tf_op jit(solution)/shard_map/ppermute | solution.py:20
  331.2 5.5 %collective-permute-start.32 = (f32[3,2,128]{2,1,0:T(2,128)S(1)}, f32[3,2,128]{2,1,0:T(2,128)S(1)}, u32[]{:S(2)}, u32[]{:S(2)}) collective-permute-start(f32[3,2,128]{2,1,0:T(2,128)S(1)} %pad_maximum_fusion.6), channel_id=1, source_target_pairs={{0,16},{16,32},{32,48},{48,64},{64,80},{80,96},{96,112},{1,17},{17... | collective-permute-start | bytes 9224 | tf_op jit(solution)/shard_map/ppermute | solution.py:20
  336.7 13.3 %collective-permute-start.33 = (f32[3,2,128]{2,1,0:T(2,128)S(1)}, f32[3,2,128]{2,1,0:T(2,128)S(1)}, u32[]{:S(2)}, u32[]{:S(2)}) collective-permute-start(f32[3,2,128]{2,1,0:T(2,128)S(1)} %pad_maximum_fusion.6), channel_id=1, source_target_pairs={{16,0},{32,16},{48,32},{64,48},{80,64},{96,80},{112,96},{17,1},{33... | collective-permute-start | bytes 9224 | tf_op jit(solution)/shard_map/ppermute | solution.py:20
  347.1 8.2 %collective-permute-start.22 = (bf16[768,128]{1,0:T(8,128)(2,1)S(1)}, bf16[768,128]{1,0:T(8,128)(2,1)S(1)}, u32[]{:S(2)}, u32[]{:S(2)}) collective-permute-start(bf16[768,128]{1,0:T(8,128)(2,1)S(1)} %select_bitcast_fusion.8), channel_id=1, source_target_pairs={{0,8},{1,9},{2,10},{3,11},{4,12},{5,13},{6,14},{7,15},{8,0},{9,1},... | collective-permute-start | bytes 589832 | tf_op jit(solution)/shard_map/ppermute | solution.py:25
  355.3 26.8 %copy-start.1 = (bf16[2048,160]{0,1:T(8,128)(2,1)S(1)}, bf16[2048,160]{0,1:T(8,128)(2,1)}, u32[]{:S(2)}) copy-start(bf16[2048,160]{0,1:T(8,128)(2,1)} %param.26) | copy-start | bytes 1966084
  360.6 10.9 %collective-permute-start.24 = (bf16[3,256,128]{2,1,0:T(8,128)(2,1)S(1)}, bf16[3,256,128]{2,1,0:T(8,128)(2,1)S(1)}, u32[]{:S(2)}, u32[]{:S(2)}) collective-permute-start(bf16[3,256,128]{2,1,0:T(8,128)(2,1)S(1)} %bitcast.332), channel_id=1, source_target_pairs={{0,16},{16,32},{32,48},{48,64},{64,80},{80,96},{96,112},{1,17},{17... | collective-permute-start | bytes 589832 | tf_op jit(solution)/shard_map/ppermute | solution.py:20
  363.6 7.9 %collective-permute-start.23 = (bf16[3,256,128]{2,1,0:T(8,128)(2,1)S(1)}, bf16[3,256,128]{2,1,0:T(8,128)(2,1)S(1)}, u32[]{:S(2)}, u32[]{:S(2)}) collective-permute-start(bf16[3,256,128]{2,1,0:T(8,128)(2,1)S(1)} %bitcast.333), channel_id=1, source_target_pairs={{0,32},{16,48},{32,64},{48,80},{64,96},{80,112},{1,33},{17,49},{33... | collective-permute-start | bytes 589832 | tf_op jit(solution)/shard_map/ppermute | solution.py:20
  367.3 13.1 %collective-permute-start.26 = (bf16[3,256,128]{2,1,0:T(8,128)(2,1)S(1)}, bf16[3,256,128]{2,1,0:T(8,128)(2,1)S(1)}, u32[]{:S(2)}, u32[]{:S(2)}) collective-permute-start(bf16[3,256,128]{2,1,0:T(8,128)(2,1)S(1)} %bitcast.334), channel_id=1, source_target_pairs={{32,0},{48,16},{64,32},{80,48},{96,64},{112,80},{33,1},{49,17},{65... | collective-permute-start | bytes 589832 | tf_op jit(solution)/shard_map/ppermute | solution.py:20
  368.6 11.8 %collective-permute-start.25 = (bf16[3,256,128]{2,1,0:T(8,128)(2,1)S(1)}, bf16[3,256,128]{2,1,0:T(8,128)(2,1)S(1)}, u32[]{:S(2)}, u32[]{:S(2)}) collective-permute-start(bf16[3,256,128]{2,1,0:T(8,128)(2,1)S(1)} %bitcast.335), channel_id=1, source_target_pairs={{16,0},{32,16},{48,32},{64,48},{80,64},{96,80},{112,96},{17,1},{33... | collective-permute-start | bytes 589832 | tf_op jit(solution)/shard_map/ppermute | solution.py:20
  (29 other events, 142.0 us)
Sparse Core Ops, SparseCore 0:
  21.5 54.1 all-gather.3
  81.3 40.2 all-gather.5
  227.9 61.8 all-gather.7
